TPU v7x, 32 devices: a whole 2x2x4 slice. The times are simulated.
32 devices in a mesh: blk: 4 (over x, core), rep: 8 (over z, y).
Axes of the slice: x: 2, y: 2, z: 4, core: 2. Of those that a mesh axis runs over, the one named last changes fastest.
Arguments:
- features: bfloat16 [4096, 256], P(('blk', 'rep')), may hold values from -6 to 6
- weight_one: bfloat16 [256, 256], replicated, may hold values from -0.375 to 0.375
- weight_two: bfloat16 [256, 256], replicated, may hold values from -0.375 to 0.375
- tile_values: bfloat16 [4, 8, 24, 128, 128], P('blk', 'rep'), may hold values from -0.125 to 0.125
- tile_rows: int32 [4, 8, 24], P('blk', 'rep'), may hold values from 0 to 7, as said below
- tile_cols: int32 [4, 8, 24], P('blk', 'rep'), may hold values from 0 to 31, as said below
- tile_count: int32 [4, 8], P('blk', 'rep'), may hold values from 16 to 24, as said below
Outputs:
- aggregated: bfloat16 [4096, 256], P(('blk', 'rep'))
Inputs may be any that keep to these rules, and one draw needn't show every extreme that they name: `tile_rows`: block row within the holder's row group into which a tile adds; slots k >= tile_count are ignored. `tile_cols`: A tile held at rep index r has column block j * 8 + r for some j: its columns are nodes held by a device of rep index r. `tile_count`: one device holds exactly 24 live tiles.
All inputs are finite; a program needn't handle non-finite values.
Results may differ from a plain program's by a relative error of at most 0.035.
Values may be sent and summed in bfloat16 or wider, within the bound.
No kernel may reach another device: no remote copies, remote signals or barrier semaphores. Data moves between devices by JAX's collectives and lax.ppermute only.
A program may use at most 64 MiB of HBM per device.

v0:
```python
import jax
import jax.numpy as jnp
from jax import lax
from jax.sharding import PartitionSpec as P


def tile_products(panel_rows, tile_vals, local_block, block_size, feat_width):
    gathered = lax.all_gather(panel_rows, "blk", axis=0, tiled=True)
    source = gathered.reshape(-1, block_size, feat_width)[local_block]
    return jnp.einsum("kab,kbf->kaf", tile_vals, source, preferred_element_type=jnp.float32)


def body(features, weight_one, weight_two, tile_values, tile_rows, tile_cols, tile_count):
    tile_vals = tile_values[0, 0]
    tile_row = tile_rows[0, 0]
    tile_col = tile_cols[0, 0]
    live_count = tile_count[0, 0]
    feat_width = features.shape[1]
    block_size = tile_vals.shape[-1]
    rows_dev = features.shape[0]
    sub_blocks = rows_dev // block_size
    replicas = lax.axis_size("rep")
    group_blocks = sub_blocks * replicas
    tile_slots = tile_vals.shape[0]
    local_block = tile_col // (replicas * sub_blocks) * sub_blocks + tile_col % sub_blocks
    is_live = (lax.iota(jnp.int32, tile_slots) < live_count).astype(jnp.float32)
    hidden = features
    result = features
    for layer_id in range(2):
        weight = weight_one if layer_id == 0 else weight_two
        panel_rows = jnp.dot(hidden, weight, preferred_element_type=jnp.float32).astype(
            jnp.bfloat16
        )
        products = tile_products(panel_rows, tile_vals, local_block, block_size, feat_width)
        masked = products * is_live[:, None, None]
        partial_value = jax.ops.segment_sum(masked, tile_row, num_segments=group_blocks)
        partial_value = partial_value.astype(jnp.bfloat16).astype(jnp.float32)
        partial_value = partial_value.reshape(group_blocks * block_size, feat_width)
        group_sum = lax.psum(partial_value.astype(jnp.bfloat16), "rep").astype(jnp.float32)
        row_start = lax.axis_index("rep") * rows_dev
        summed = lax.dynamic_slice_in_dim(group_sum, row_start, rows_dev, 0)
        if layer_id == 0:
            hidden = jnp.maximum(summed, 0.0).astype(jnp.bfloat16)
        else:
            result = summed.astype(jnp.bfloat16)
    return result


def solution(mesh):
    in_specs = (
        P(("blk", "rep"), None),
        P(),
        P(),
        P("blk", "rep", None, None, None),
        P("blk", "rep", None),
        P("blk", "rep", None),
        P("blk", "rep"),
    )
    out_specs = P(("blk", "rep"), None)
    return jax.shard_map(body, mesh=mesh, in_specs=in_specs, out_specs=out_specs, check_vma=False)
```

profile of v0, /device:TPU:0, one launch (start us, length us, event | category | flops | bytes accessed | tf_op | source)
XLA Modules:
  0.0 204.6 jit_solution(6900066142206333216)
XLA Ops:
  6.5 0.0 copy-start
  6.5 0.0 all-reduce.3.cloned.1.call-start
  6.5 0.7 fusion.4
  7.3 1.1 convolution_convert_fusion.1
  8.4 7.2 %all_gather.6 = bf16[512,256]{1,0:T(8,128)(2,1)S(1)} all-gather(bf16[128,256]{1,0:T(8,128)(2,1)S(1)} %convolution_convert_fusion.1), channel_id=1, replica_groups=mesh['blk'=4,'rep'=8] {'blk'}, dimensions={0}, use_global_device_ids=true | all-gather | bytes 327680 | tf_op jit(solution)/shard_map/all_gather | solution.py:8
  16.3 0.6 gather_fusion
  16.9 0.0 copy-done
  16.9 2.4 %multiply_bitcast_fusion.1 = f32[24,128,256]{1,2,0:T(8,128)} fusion(bf16[24,128,256]{2,1,0:T(8,128)(2,1)S(1)} %gather_fusion, f32[24]{0:T(128)S(1)} %compare_convert_fusion, bf16[1,1,24,128,128]{4,3,2,1,0:T(8,128)(2,1)S(1)} %copy-done), kind=kOutput, calls=%fused_computation.5 | convolution fusion | flops 202113024 | bytes 5505120 | tf_op jit(solution)/shard_map/kab,kbf->kaf/dot_general | solution.py:10
  19.3 0.0 copy-start.2
  19.3 3.6 %copy.11 = f32[24,128,256]{2,1,0:T(8,128)} copy(f32[24,128,256]{1,2,0:T(8,128)} %multiply_bitcast_fusion.1) | data formatting | bytes 6291456 | tf_op jit(solution)/shard_map/mul | solution.py:35
  22.9 0.1 broadcast.95.clone
  23.0 0.0 copy-done.2
  23.0 0.0 copy-start.1
  23.0 6.1 %scatter_fusion = f32[8,128,256]{2,1,0:T(8,128)S(1)} fusion(f32[8,128,256]{2,1,0:T(8,128)S(1)} %broadcast.95.clone, s32[24]{0:T(128)S(1)} %bitcast.37, f32[24,128,256]{2,1,0:T(8,128)} %copy.11), kind=kCustom, calls=%fused_computation.2 | custom fusion | flops 786432 | bytes 9437280 | tf_op jit(solution)/shard_map/scatter-add | solution.py:36
  29.1 0.9 convert_element_type.43
  30.0 0.0 all-reduce.3.cloned.1.call-update
  30.0 0.0 all-reduce.5.cloned.1.call-start
  30.1 73.8 %all-reduce.3.cloned.1.call-done = bf16[1024,256]{1,0:T(8,128)(2,1)} async-done(((bf16[1024,256]{1,0:T(8,128)(2,1)}), bf16[1024,256]{1,0:T(8,128)(2,1)}) %all-reduce.3.cloned.1.call-update) | async-done | bytes 524304 | tf_op jit(solution)/shard_map/psum | solution.py:39
  103.9 0.0 copy-done.1
  103.9 1.0 convolution_convert_fusion
  104.9 5.8 %all_gather.7 = bf16[512,256]{1,0:T(8,128)(2,1)S(1)} all-gather(bf16[128,256]{1,0:T(8,128)(2,1)S(1)} %convolution_convert_fusion), channel_id=1, replica_groups=mesh['blk'=4,'rep'=8] {'blk'}, dimensions={0}, use_global_device_ids=true | all-gather | bytes 327680 | tf_op jit(solution)/shard_map/all_gather | solution.py:8
  110.7 0.6 gather_fusion.1
  111.3 2.4 %multiply_bitcast_fusion = f32[24,128,256]{1,2,0:T(8,128)} fusion(bf16[24,128,256]{2,1,0:T(8,128)(2,1)S(1)} %gather_fusion.1, f32[24]{0:T(128)S(1)} %compare_convert_fusion, bf16[1,1,24,128,128]{4,3,2,1,0:T(8,128)(2,1)S(1)} %copy-done), kind=kOutput, calls=%fused_computation.4 | convolution fusion | flops 202113024 | bytes 5505120 | tf_op jit(solution)/shard_map/kab,kbf->kaf/dot_general | solution.py:10
  113.7 3.6 %copy.13 = f32[24,128,256]{2,1,0:T(8,128)} copy(f32[24,128,256]{1,2,0:T(8,128)} %multiply_bitcast_fusion) | data formatting | bytes 6291456 | tf_op jit(solution)/shard_map/mul | solution.py:35
  117.3 0.1 broadcast.95
  117.4 6.1 %scatter_fusion.1 = f32[8,128,256]{2,1,0:T(8,128)S(1)} fusion(f32[8,128,256]{2,1,0:T(8,128)S(1)} %broadcast.95, s32[24]{0:T(128)S(1)} %bitcast.38, f32[24,128,256]{2,1,0:T(8,128)} %copy.13), kind=kCustom, calls=%fused_computation.3 | custom fusion | flops 786432 | bytes 9437280 | tf_op jit(solution)/shard_map/scatter-add | solution.py:36
  123.5 0.9 convert_element_type.48
  124.4 0.0 all-reduce.5.cloned.1.call-update
  124.4 71.9 %all-reduce.5.cloned.1.call-done = bf16[1024,256]{1,0:T(8,128)(2,1)} async-done(((bf16[1024,256]{1,0:T(8,128)(2,1)}), bf16[1024,256]{1,0:T(8,128)(2,1)}) %all-reduce.5.cloned.1.call-update) | async-done | bytes 524304 | tf_op jit(solution)/shard_map/psum | solution.py:39
  196.3 1.5 convert_convert_fusion
  (2 shorter events, 0.0 us)
Async XLA Ops:
  6.5 10.4 %copy-start = (bf16[1,1,24,128,128]{4,3,2,1,0:T(8,128)(2,1)S(1)}, bf16[1,1,24,128,128]{4,3,2,1,0:T(8,128)(2,1)}, u32[]{:S(2)}) copy-start(bf16[1,1,24,128,128]{4,3,2,1,0:T(8,128)(2,1)} %param.10) | copy-start | bytes 2359300
  6.5 97.4 %all-reduce.3.cloned.1.call-start = ((), (), s32[]{:S(2)}) async-start(), calls=%async_computation | async-start | bytes 1048576 | tf_op jit(solution)/shard_map/psum | solution.py:39
  19.3 3.7 %copy-start.2 = (s32[1,1,24]{2,1,0:T(1,128)S(1)}, s32[1,1,24]{2,1,0:T(1,128)}, u32[]{:S(2)}) copy-start(s32[1,1,24]{2,1,0:T(1,128)} %param.11) | copy-start | bytes 292
  23.0 80.9 %copy-start.1 = (bf16[256,256]{1,0:T(8,128)(2,1)S(1)}, bf16[256,256]{1,0:T(8,128)(2,1)}, u32[]{:S(2)}) copy-start(bf16[256,256]{1,0:T(8,128)(2,1)} %param.9) | copy-start | bytes 393220
  30.0 166.2 %all-reduce.5.cloned.1.call-start = ((), (), s32[]{:S(2)}) async-start(), calls=%async_computation.1 | async-start | bytes 1048576 | tf_op jit(solution)/shard_map/psum | solution.py:39
Sparse Core Ops, SparseCore 0:
  30.1 73.7 all-reduce.2
  124.5 71.6 all-reduce.4
where the time goes:
time: 205 us
  waiting for transfers between devices  146 us (71%)
  other arithmetic  16.1 us (8%)
  between operations  14.2 us (7%)
  blocking collectives  13 us (6%)
  local copies, waits for them, and re-layouts  8.65 us (4%)
  matrix products  6.9 us (3%)
    psum x2, waiting for transfers between devices, body(): lax.psum(partial_value.astype(jnp.bfloat16), 'rep').astype(jnp.float32)  146 us
    all_gather x2, blocking collectives, tile_products(): gathered = lax.all_gather(panel_rows, 'blk', axis=0, tiled=True)  13 us
    scatter-add x2, other arithmetic, body(): jax.ops.segment_sum(masked, tile_row, num_segments=group_blocks)  12.2 us
    mul x2, local copies, waits for them, and re-layouts, body(): masked = products * is_live[:, None, None]  7.18 us
    dot_general x2, matrix products, tile_products(): jnp.einsum('kab,kbf->kaf', tile_vals, source, preferred_element_type=jnp....  4.8 us
  transfers between devices with their start and end apart: 2, of which 2 were waited for; matrix products, arithmetic and copies ran while one was open for 0% of the time, Pallas kernels for 0%

commit v1 on v0

v1 whole, which is shorter than its diff:
```python
import functools

import jax
import jax.numpy as jnp
from jax import lax
from jax.experimental import pallas as pl
from jax.experimental.pallas import tpu as pltpu
from jax.sharding import PartitionSpec as P


def _agg_kernel(rows_ref, blks_ref, cnt_ref, panel_ref, tiles_ref, out_ref, acc_ref):
    acc_ref[...] = jnp.zeros_like(acc_ref)
    live = cnt_ref[0]
    n_rows = acc_ref.shape[0]
    n_src = panel_ref.shape[0]

    def step(k, carry):
        @pl.when(k < live)
        def _():
            row = jnp.clip(rows_ref[k], 0, n_rows - 1)
            src = jnp.clip(blks_ref[k], 0, n_src - 1)
            acc_ref[row] += jnp.dot(tiles_ref[k], panel_ref[src], preferred_element_type=jnp.float32)

        return carry

    lax.fori_loop(0, tiles_ref.shape[0], step, 0)
    out_ref[...] = acc_ref[...].astype(out_ref.dtype)


def aggregate(panel_blocks, tile_vals, tile_row, src_block, live_count, n_rows):
    slots, blk, _ = tile_vals.shape
    feat = panel_blocks.shape[-1]
    smem = pl.BlockSpec(memory_space=pltpu.SMEM)
    vmem = pl.BlockSpec(memory_space=pltpu.VMEM)
    flops = 2 * slots * blk * blk * feat
    nbytes = 2 * (panel_blocks.size + tile_vals.size + n_rows * blk * feat)
    return pl.pallas_call(
        _agg_kernel,
        out_shape=jax.ShapeDtypeStruct((n_rows, blk, feat), jnp.bfloat16),
        in_specs=[smem, smem, smem, vmem, vmem],
        out_specs=vmem,
        scratch_shapes=[pltpu.VMEM((n_rows, blk, feat), jnp.float32)],
        cost_estimate=pl.CostEstimate(flops=flops, bytes_accessed=nbytes, transcendentals=0),
    )(tile_row, src_block, live_count.reshape(1), panel_blocks, tile_vals)


def gather_blk(panel, mode):
    n = lax.axis_size("blk")
    if mode == "ag":
        return lax.all_gather(panel, "blk", axis=0, tiled=False)
    me = lax.axis_index("blk")
    pieces = [panel]
    for s in range(1, n):
        perm = [(src, (src + s) % n) for src in range(n)]
        pieces.append(lax.ppermute(panel, "blk", perm))
    stacked = jnp.stack(pieces)
    order = (me - jnp.arange(n)) % n
    inv = jnp.argsort(order)
    return stacked[inv]


def exchange_rep(partial, mode):
    n = lax.axis_size("rep")
    if mode == "rs":
        flat = partial.reshape(-1, partial.shape[-1])
        return lax.psum_scatter(flat, "rep", scatter_dimension=0, tiled=True).astype(jnp.float32)
    if mode == "a2a":
        got = lax.all_to_all(partial, "rep", 0, 0, tiled=True)
        return jnp.sum(got.astype(jnp.float32), axis=0)
    me = lax.axis_index("rep")
    total = lax.dynamic_index_in_dim(partial, me, 0, keepdims=False).astype(jnp.float32)
    for s in range(1, n):
        perm = [(src, (src + s) % n) for src in range(n)]
        piece = lax.dynamic_index_in_dim(partial, (me + s) % n, 0, keepdims=False)
        total = total + lax.ppermute(piece, "rep", perm).astype(jnp.float32)
    return total


def make_body(gmode, xmode):
    def body(features, weight_one, weight_two, tile_values, tile_rows, tile_cols, tile_count):
        tile_vals = tile_values[0, 0]
        tile_row = tile_rows[0, 0]
        tile_col = tile_cols[0, 0]
        live_count = tile_count[0, 0]
        replicas = lax.axis_size("rep")
        src_block = tile_col // replicas
        hidden = features
        for layer_id in range(2):
            weight = weight_one if layer_id == 0 else weight_two
            panel = jnp.dot(hidden, weight, preferred_element_type=jnp.float32).astype(jnp.bfloat16)
            blocks = gather_blk(panel, gmode)
            partial = aggregate(blocks, tile_vals, tile_row, src_block, live_count, replicas)
            summed = exchange_rep(partial, xmode)
            if layer_id == 0:
                hidden = jnp.maximum(summed, 0.0).astype(jnp.bfloat16)
            else:
                return summed.astype(jnp.bfloat16)

    return body


def solution(mesh, gmode="ag", xmode="pp"):
    in_specs = (
        P(("blk", "rep"), None),
        P(),
        P(),
        P("blk", "rep", None, None, None),
        P("blk", "rep", None),
        P("blk", "rep", None),
        P("blk", "rep"),
    )
    out_specs = P(("blk", "rep"), None)
    return jax.shard_map(make_body(gmode, xmode), mesh=mesh, in_specs=in_specs, out_specs=out_specs, check_vma=False)
```

time: 205 us -> 67.1 us (0.33)
  waiting for transfers between devices: 146 us -> 14.9 us
  starting transfers between devices: 0.04 us -> 21.3 us
  other arithmetic: 16.1 us -> 2.06 us
  between operations: 14.2 us -> 0.76 us
  Pallas kernels: 0 us -> 11.1 us
  local copies, waits for them, and re-layouts: 8.65 us -> 2.17 us
  matrix products: 6.9 us -> 1.2 us
    psum x2 -> x0, waiting for transfers between devices: 146 us -> none  [body(): lax.psum(partial_value.astype(jnp.bfloat16), 'rep').astype(jnp.float32)]
    ppermute x0 -> x14, starting transfers between devices: none -> 21.3 us  [exchange_rep(): total = total + lax.ppermute(piece, 'rep', perm).astype(jnp.float32)]
    ppermute x0 -> x14, waiting for transfers between devices: none -> 14.9 us  [exchange_rep(): total = total + lax.ppermute(piece, 'rep', perm).astype(jnp.float32)]
    scatter-add x2 -> x0, other arithmetic: 12.2 us -> none  [body(): jax.ops.segment_sum(masked, tile_row, num_segments=group_blocks)]
    pallas_call x0 -> x2, Pallas kernels: none -> 11.1 us  [aggregate(): pl.pallas_call(_agg_kernel, out_shape=jax.ShapeDtypeStruct((n_rows, blk,...]
    mul x2 -> x0, local copies, waits for them, and re-layouts: 7.18 us -> none  [body(): masked = products * is_live[:, None, None]]
    dot_general x2 -> x0, matrix products: 4.8 us -> none  [tile_products(): jnp.einsum('kab,kbf->kaf', tile_vals, source, preferred_element_type=jnp....]
    squeeze x0 -> x2, local copies, waits for them, and re-layouts: none -> 2.15 us  [exchange_rep(): piece = lax.dynamic_index_in_dim(partial, (me + s) % n, 0, keepdims=False)]
  transfers between devices with their start and end apart: 2 -> 14, of which waited for: 2 -> 5; matrix products, arithmetic and copies ran while one was open for 0% -> 0% of each run, Pallas kernels for 0% -> 0%
where the time goes in v1:
time: 67.1 us; the launch traced here: 67.4 us
  starting transfers between devices  21.3 us (32%)
  waiting for transfers between devices  14.9 us (22%)
  blocking collectives  13.9 us (21%)
  Pallas kernels  11.1 us (17%)
  local copies, waits for them, and re-layouts  2.17 us (3%)
  other arithmetic  2.06 us (3%)
  matrix products  1.2 us (2%)
  between operations  0.76 us (1%)
    ppermute x14, starting transfers between devices, exchange_rep(): total = total + lax.ppermute(piece, 'rep', perm).astype(jnp.float32)  21.3 us
    ppermute x14, waiting for transfers between devices, exchange_rep(): total = total + lax.ppermute(piece, 'rep', perm).astype(jnp.float32)  14.9 us
    all_gather x2, blocking collectives, gather_blk(): return lax.all_gather(panel, 'blk', axis=0, tiled=False)  13.9 us
    pallas_call x2, Pallas kernels, aggregate(): pl.pallas_call(_agg_kernel, out_shape=jax.ShapeDtypeStruct((n_rows, blk,...  11.1 us
    squeeze x2, local copies, waits for them, and re-layouts, exchange_rep(): piece = lax.dynamic_index_in_dim(partial, (me + s) % n, 0, keepdims=False)  2.15 us
    convert_element_type x1, other arithmetic, body(): return summed.astype(jnp.bfloat16)  1.54 us
  transfers between devices with their start and end apart: 14, of which 5 were waited for; matrix products, arithmetic and copies ran while one was open for 0% of the time, Pallas kernels for 0%

profile of v1, /device:TPU:0, one launch (start us, length us, event | category | flops | bytes accessed | tf_op | source)
XLA Modules:
  0.0 67.4 jit_solution(9231101432126344835)
XLA Ops:
  0.0 0.0 copy-start
  0.0 0.0 copy-start.2
  0.0 0.0 copy-start.3
  0.7 0.0 copy-done.3
  0.7 0.5 and_select_fusion.blks_ref
  1.2 0.0 copy-done
  1.2 0.0 copy-done.2
  1.2 0.2 convolution_convert_fusion.1
  1.4 7.6 %all-gather = bf16[512,256]{1,0:T(8,128)(2,1)} all-gather(bf16[128,256]{1,0:T(8,128)(2,1)S(1)} %convolution_convert_fusion.1), channel_id=2, replica_groups=mesh['blk'=4,'rep'=8] {'blk'}, dimensions={0}, use_global_device_ids=true | all-gather | bytes 327680 | tf_op jit(solution)/shard_map/all_gather | solution.py:50
  9.1 5.6 %shard_map.73 = bf16[8,128,256]{2,1,0:T(8,128)(2,1)} custom-call(s32[24]{0:T(128)} %bitcast.59, s32[24]{0:T(128)} %and_select_fusion.blks_ref, s32[1]{0:T(128)} %bitcast.53.cnt_ref, bf16[4,128,256]{2,1,0:T(8,128)(2,1)} %bitcast.57, bf16[24,128,128]{2,1,0:T(8,128)(2,1)} %bitcast.55), custom_call_target="tpu_custom_call" | custom-call | flops 201326592 | bytes 1572864 | tf_op jit(solution)/shard_map/pallas_call | solution.py:37
  14.6 0.0 copy-start.1
  14.6 1.1 %dynamic-slice_bitcast_fusion.13 = (bf16[128,256]{1,0:T(8,128)(2,1)S(1)}, bf16[128,256]{1,0:T(8,128)(2,1)S(1)}, bf16[128,256]{1,0:T(8,128)(2,1)S(1)}, bf16[128,2...) fusion(bf16[8,128,256]{2,1,0:T(8,128)(2,1)} %shard_map.73, ...), kind=kLoop, calls=%fused_computation.34 | loop fusion | bytes 917532 | tf_op jit(solution)/shard_map/jit(dynamic_index_in_dim)/squeeze | solution.py:74
  15.7 1.6 %collective-permute-start = (bf16[128,256]{1,0:T(8,128)(2,1)S(1)}, bf16[128,256]{1,0:T(8,128)(2,1)S(1)}, u32[]{:S(2)}, u32[]{:S(2)}) collective-permute-start(bf16[128,256]{1,0:T(8,128)(2,1)S(1)} %get-tuple-element.12), channel_id=1, source_target_pairs={{0,1},{1,2},{2,3},{3,4},{4,5},{5,6},{6,7},{7,0},{8,9},{9,10},{10,1... | collective-permute-start | bytes 196616 | tf_op jit(solution)/shard_map/ppermute | solution.py:75
  17.3 3.2 %collective-permute-start.6 = (bf16[128,256]{1,0:T(8,128)(2,1)S(1)}, bf16[128,256]{1,0:T(8,128)(2,1)S(1)}, u32[]{:S(2)}, u32[]{:S(2)}) collective-permute-start(bf16[128,256]{1,0:T(8,128)(2,1)S(1)} %get-tuple-element.13), channel_id=1, source_target_pairs={{0,7},{1,0},{2,1},{3,2},{4,3},{5,4},{6,5},{7,6},{8,15},{9,8},{10,9... | collective-permute-start | bytes 196616 | tf_op jit(solution)/shard_map/ppermute | solution.py:75
  20.5 1.4 %collective-permute-start.5 = (bf16[128,256]{1,0:T(8,128)(2,1)S(1)}, bf16[128,256]{1,0:T(8,128)(2,1)S(1)}, u32[]{:S(2)}, u32[]{:S(2)}) collective-permute-start(bf16[128,256]{1,0:T(8,128)(2,1)S(1)} %get-tuple-element.14), channel_id=1, source_target_pairs={{0,6},{1,7},{2,0},{3,1},{4,2},{5,3},{6,4},{7,5},{8,14},{9,15},{10,... | collective-permute-start | bytes 196616 | tf_op jit(solution)/shard_map/ppermute | solution.py:75
  21.9 0.0 collective-permute-start.4
  21.9 2.8 %collective-permute-start.3 = (bf16[128,256]{1,0:T(8,128)(2,1)S(1)}, bf16[128,256]{1,0:T(8,128)(2,1)S(1)}, u32[]{:S(2)}, u32[]{:S(2)}) collective-permute-start(bf16[128,256]{1,0:T(8,128)(2,1)S(1)} %get-tuple-element.16), channel_id=1, source_target_pairs={{0,4},{1,5},{2,6},{3,7},{4,0},{5,1},{6,2},{7,3},{8,12},{9,13},{10,... | collective-permute-start | bytes 196616 | tf_op jit(solution)/shard_map/ppermute | solution.py:75
  24.8 0.0 collective-permute-done
  24.8 0.1 collective-permute-start.2
  24.9 0.0 collective-permute-done.6
  24.9 2.2 %collective-permute-start.1 = (bf16[128,256]{1,0:T(8,128)(2,1)S(1)}, bf16[128,256]{1,0:T(8,128)(2,1)S(1)}, u32[]{:S(2)}, u32[]{:S(2)}) collective-permute-start(bf16[128,256]{1,0:T(8,128)(2,1)S(1)} %get-tuple-element.18), channel_id=1, source_target_pairs={{0,2},{1,3},{2,4},{3,5},{4,6},{5,7},{6,0},{7,1},{8,10},{9,11},{10,... | collective-permute-start | bytes 196616 | tf_op jit(solution)/shard_map/ppermute | solution.py:75
  27.0 0.0 collective-permute-done.5
  27.0 0.6 collective-permute-done.4
  27.6 5.7 %collective-permute-done.3 = bf16[128,256]{1,0:T(8,128)(2,1)S(1)} collective-permute-done((bf16[128,256]{1,0:T(8,128)(2,1)S(1)}, bf16[128,256]{1,0:T(8,128)(2,1)S(1)}, u32[]{:S(2)}, u32[]{:S(2)}) %collective-permute-start.3) | collective-permute-done | bytes 65568 | tf_op jit(solution)/shard_map/ppermute | solution.py:75
  33.3 0.8 %collective-permute-done.2 = bf16[128,256]{1,0:T(8,128)(2,1)S(1)} collective-permute-done((bf16[128,256]{1,0:T(8,128)(2,1)S(1)}, bf16[128,256]{1,0:T(8,128)(2,1)S(1)}, u32[]{:S(2)}, u32[]{:S(2)}) %collective-permute-start.2) | collective-permute-done | bytes 65568 | tf_op jit(solution)/shard_map/ppermute | solution.py:75
  34.1 0.0 collective-permute-done.1
  34.1 0.0 copy-done.1
  34.2 1.0 %convolution_convert_fusion = bf16[128,256]{1,0:T(8,128)(2,1)S(1)} fusion(bf16[256,256]{1,0:T(8,128)(2,1)S(1)} %copy-done.1, bf16[128,256]{1,0:T(8,128)(2,1)S(1)} %collective-permute-done.6, bf16[128,256]{1,0:T(8,128)(2,1)S(1)} %collective-permute-done.5, bf16[128,256]{1,0:T(8,128)(2,1)S(1)} %collective-permute-done.4, ...), kind=kOutput, calls=%fused_computation | convolution fusion | flops 17367040 | bytes 720900 | tf_op jit(solution)/shard_map/dot_general | solution.py:90
  35.2 6.2 %all-gather.1 = bf16[512,256]{1,0:T(8,128)(2,1)} all-gather(bf16[128,256]{1,0:T(8,128)(2,1)S(1)} %convolution_convert_fusion), channel_id=3, replica_groups=mesh['blk'=4,'rep'=8] {'blk'}, dimensions={0}, use_global_device_ids=true | all-gather | bytes 327680 | tf_op jit(solution)/shard_map/all_gather | solution.py:50
  41.4 5.6 %shard_map.74 = bf16[8,128,256]{2,1,0:T(8,128)(2,1)} custom-call(s32[24]{0:T(128)} %bitcast.60, s32[24]{0:T(128)} %and_select_fusion.blks_ref, s32[1]{0:T(128)} %bitcast.54.cnt_ref, bf16[4,128,256]{2,1,0:T(8,128)(2,1)} %bitcast.58, bf16[24,128,128]{2,1,0:T(8,128)(2,1)} %bitcast.56), custom_call_target="tpu_custom_call" | custom-call | flops 201326592 | bytes 1572864 | tf_op jit(solution)/shard_map/pallas_call | solution.py:37
  47.0 1.1 %dynamic-slice_bitcast_fusion.6 = (bf16[128,256]{1,0:T(8,128)(2,1)S(1)}, bf16[128,256]{1,0:T(8,128)(2,1)S(1)}, bf16[128,256]{1,0:T(8,128)(2,1)S(1)}, bf16[128,25...) fusion(bf16[8,128,256]{2,1,0:T(8,128)(2,1)} %shard_map.74, ...), kind=kLoop, calls=%fused_computation.26 | loop fusion | bytes 917532 | tf_op jit(solution)/shard_map/jit(dynamic_index_in_dim)/squeeze | solution.py:74
  48.1 0.1 collective-permute-start.7
  48.1 4.7 %collective-permute-start.13 = (bf16[128,256]{1,0:T(8,128)(2,1)S(1)}, bf16[128,256]{1,0:T(8,128)(2,1)S(1)}, u32[]{:S(2)}, u32[]{:S(2)}) collective-permute-start(bf16[128,256]{1,0:T(8,128)(2,1)S(1)} %get-tuple-element.6), channel_id=1, source_target_pairs={{0,7},{1,0},{2,1},{3,2},{4,3},{5,4},{6,5},{7,6},{8,15},{9,8},{10,9... | collective-permute-start | bytes 196616 | tf_op jit(solution)/shard_map/ppermute | solution.py:75
  52.8 0.0 collective-permute-start.12
  52.8 0.0 collective-permute-start.11
  52.8 2.9 %collective-permute-start.10 = (bf16[128,256]{1,0:T(8,128)(2,1)S(1)}, bf16[128,256]{1,0:T(8,128)(2,1)S(1)}, u32[]{:S(2)}, u32[]{:S(2)}) collective-permute-start(bf16[128,256]{1,0:T(8,128)(2,1)S(1)} %get-tuple-element.9), channel_id=1, source_target_pairs={{0,4},{1,5},{2,6},{3,7},{4,0},{5,1},{6,2},{7,3},{8,12},{9,13},{10,... | collective-permute-start | bytes 196616 | tf_op jit(solution)/shard_map/ppermute | solution.py:75
  55.8 0.0 collective-permute-done.7
  55.8 0.0 collective-permute-start.9
  55.8 0.0 collective-permute-done.13
  55.8 2.3 %collective-permute-start.8 = (bf16[128,256]{1,0:T(8,128)(2,1)S(1)}, bf16[128,256]{1,0:T(8,128)(2,1)S(1)}, u32[]{:S(2)}, u32[]{:S(2)}) collective-permute-start(bf16[128,256]{1,0:T(8,128)(2,1)S(1)} %get-tuple-element.11), channel_id=1, source_target_pairs={{0,2},{1,3},{2,4},{3,5},{4,6},{5,7},{6,0},{7,1},{8,10},{9,11},{10,... | collective-permute-start | bytes 196616 | tf_op jit(solution)/shard_map/ppermute | solution.py:75
  58.1 0.0 collective-permute-done.12
  58.1 0.0 collective-permute-done.11
  58.1 6.2 %collective-permute-done.10 = bf16[128,256]{1,0:T(8,128)(2,1)S(1)} collective-permute-done((bf16[128,256]{1,0:T(8,128)(2,1)S(1)}, bf16[128,256]{1,0:T(8,128)(2,1)S(1)}, u32[]{:S(2)}, u32[]{:S(2)}) %collective-permute-start.10) | collective-permute-done | bytes 65568 | tf_op jit(solution)/shard_map/ppermute | solution.py:75
  64.4 1.5 %collective-permute-done.9 = bf16[128,256]{1,0:T(8,128)(2,1)S(1)} collective-permute-done((bf16[128,256]{1,0:T(8,128)(2,1)S(1)}, bf16[128,256]{1,0:T(8,128)(2,1)S(1)}, u32[]{:S(2)}, u32[]{:S(2)}) %collective-permute-start.9) | collective-permute-done | bytes 65568 | tf_op jit(solution)/shard_map/ppermute | solution.py:75
  65.9 0.0 collective-permute-done.8
  65.9 1.5 %fusion.6 = bf16[128,256]{1,0:T(8,128)(2,1)} fusion(bf16[128,256]{1,0:T(8,128)(2,1)S(1)} %collective-permute-done.13, bf16[128,256]{1,0:T(8,128)(2,1)S(1)} %collective-permute-done.12, bf16[128,256]{1,0:T(8,128)(2,1)S(1)} %collective-permute-done.11, bf16[128,256]{1,0:T(8,128)(2,1)S(1)} %collective-permute-done.10, ...), kind=kLoop, calls=%fused_computation.9 | loop fusion | flops 524288 | bytes 589828 | tf_op jit(solution)/shard_map/convert_element_type | solution.py:97
Async XLA Ops:
  0.0 1.2 %copy-start = (bf16[256,256]{1,0:T(8,128)(2,1)S(1)}, bf16[256,256]{1,0:T(8,128)(2,1)}, u32[]{:S(2)}) copy-start(bf16[256,256]{1,0:T(8,128)(2,1)} %param.8) | copy-start | bytes 393220
  0.0 1.2 %copy-start.2 = (bf16[128,256]{1,0:T(8,128)(2,1)S(1)}, bf16[128,256]{1,0:T(8,128)(2,1)}, u32[]{:S(2)}) copy-start(bf16[128,256]{1,0:T(8,128)(2,1)} %param.7) | copy-start | bytes 196612
  0.0 0.7 %copy-start.3 = (s32[1,1,24]{2,1,0:T(1,128)S(1)}, s32[1,1,24]{2,1,0:T(1,128)}, u32[]{:S(2)}) copy-start(s32[1,1,24]{2,1,0:T(1,128)} %param.12) | copy-start | bytes 292
  14.6 19.5 %copy-start.1 = (bf16[256,256]{1,0:T(8,128)(2,1)S(1)}, bf16[256,256]{1,0:T(8,128)(2,1)}, u32[]{:S(2)}) copy-start(bf16[256,256]{1,0:T(8,128)(2,1)} %param.9) | copy-start | bytes 393220
  15.7 9.0 %collective-permute-start = (bf16[128,256]{1,0:T(8,128)(2,1)S(1)}, bf16[128,256]{1,0:T(8,128)(2,1)S(1)}, u32[]{:S(2)}, u32[]{:S(2)}) collective-permute-start(bf16[128,256]{1,0:T(8,128)(2,1)S(1)} %get-tuple-element.12), channel_id=1, source_target_pairs={{0,1},{1,2},{2,3},{3,4},{4,5},{5,6},{6,7},{7,0},{8,9},{9,10},{10,1... | collective-permute-start | bytes 196616 | tf_op jit(solution)/shard_map/ppermute | solution.py:75
  17.3 7.5 %collective-permute-start.6 = (bf16[128,256]{1,0:T(8,128)(2,1)S(1)}, bf16[128,256]{1,0:T(8,128)(2,1)S(1)}, u32[]{:S(2)}, u32[]{:S(2)}) collective-permute-start(bf16[128,256]{1,0:T(8,128)(2,1)S(1)} %get-tuple-element.13), channel_id=1, source_target_pairs={{0,7},{1,0},{2,1},{3,2},{4,3},{5,4},{6,5},{7,6},{8,15},{9,8},{10,9... | collective-permute-start | bytes 196616 | tf_op jit(solution)/shard_map/ppermute | solution.py:75
  20.5 6.6 %collective-permute-start.5 = (bf16[128,256]{1,0:T(8,128)(2,1)S(1)}, bf16[128,256]{1,0:T(8,128)(2,1)S(1)}, u32[]{:S(2)}, u32[]{:S(2)}) collective-permute-start(bf16[128,256]{1,0:T(8,128)(2,1)S(1)} %get-tuple-element.14), channel_id=1, source_target_pairs={{0,6},{1,7},{2,0},{3,1},{4,2},{5,3},{6,4},{7,5},{8,14},{9,15},{10,... | collective-permute-start | bytes 196616 | tf_op jit(solution)/shard_map/ppermute | solution.py:75
  21.9 5.7 %collective-permute-start.4 = (bf16[128,256]{1,0:T(8,128)(2,1)S(1)}, bf16[128,256]{1,0:T(8,128)(2,1)S(1)}, u32[]{:S(2)}, u32[]{:S(2)}) collective-permute-start(bf16[128,256]{1,0:T(8,128)(2,1)S(1)} %get-tuple-element.15), channel_id=1, source_target_pairs={{0,5},{1,6},{2,7},{3,0},{4,1},{5,2},{6,3},{7,4},{8,13},{9,14},{10,... | collective-permute-start | bytes 196616 | tf_op jit(solution)/shard_map/ppermute | solution.py:75
  21.9 11.4 %collective-permute-start.3 = (bf16[128,256]{1,0:T(8,128)(2,1)S(1)}, bf16[128,256]{1,0:T(8,128)(2,1)S(1)}, u32[]{:S(2)}, u32[]{:S(2)}) collective-permute-start(bf16[128,256]{1,0:T(8,128)(2,1)S(1)} %get-tuple-element.16), channel_id=1, source_target_pairs={{0,4},{1,5},{2,6},{3,7},{4,0},{5,1},{6,2},{7,3},{8,12},{9,13},{10,... | collective-permute-start | bytes 196616 | tf_op jit(solution)/shard_map/ppermute | solution.py:75
  24.8 9.4 %collective-permute-start.2 = (bf16[128,256]{1,0:T(8,128)(2,1)S(1)}, bf16[128,256]{1,0:T(8,128)(2,1)S(1)}, u32[]{:S(2)}, u32[]{:S(2)}) collective-permute-start(bf16[128,256]{1,0:T(8,128)(2,1)S(1)} %get-tuple-element.17), channel_id=1, source_target_pairs={{0,3},{1,4},{2,5},{3,6},{4,7},{5,0},{6,1},{7,2},{8,11},{9,12},{10,... | collective-permute-start | bytes 196616 | tf_op jit(solution)/shard_map/ppermute | solution.py:75
  24.9 9.3 %collective-permute-start.1 = (bf16[128,256]{1,0:T(8,128)(2,1)S(1)}, bf16[128,256]{1,0:T(8,128)(2,1)S(1)}, u32[]{:S(2)}, u32[]{:S(2)}) collective-permute-start(bf16[128,256]{1,0:T(8,128)(2,1)S(1)} %get-tuple-element.18), channel_id=1, source_target_pairs={{0,2},{1,3},{2,4},{3,5},{4,6},{5,7},{6,0},{7,1},{8,10},{9,11},{10,... | collective-permute-start | bytes 196616 | tf_op jit(solution)/shard_map/ppermute | solution.py:75
  48.1 7.7 %collective-permute-start.7 = (bf16[128,256]{1,0:T(8,128)(2,1)S(1)}, bf16[128,256]{1,0:T(8,128)(2,1)S(1)}, u32[]{:S(2)}, u32[]{:S(2)}) collective-permute-start(bf16[128,256]{1,0:T(8,128)(2,1)S(1)} %get-tuple-element.5), channel_id=1, source_target_pairs={{0,1},{1,2},{2,3},{3,4},{4,5},{5,6},{6,7},{7,0},{8,9},{9,10},{10,1... | collective-permute-start | bytes 196616 | tf_op jit(solution)/shard_map/ppermute | solution.py:75
  48.1 7.6 %collective-permute-start.13 = (bf16[128,256]{1,0:T(8,128)(2,1)S(1)}, bf16[128,256]{1,0:T(8,128)(2,1)S(1)}, u32[]{:S(2)}, u32[]{:S(2)}) collective-permute-start(bf16[128,256]{1,0:T(8,128)(2,1)S(1)} %get-tuple-element.6), channel_id=1, source_target_pairs={{0,7},{1,0},{2,1},{3,2},{4,3},{5,4},{6,5},{7,6},{8,15},{9,8},{10,9... | collective-permute-start | bytes 196616 | tf_op jit(solution)/shard_map/ppermute | solution.py:75
  52.8 5.3 %collective-permute-start.12 = (bf16[128,256]{1,0:T(8,128)(2,1)S(1)}, bf16[128,256]{1,0:T(8,128)(2,1)S(1)}, u32[]{:S(2)}, u32[]{:S(2)}) collective-permute-start(bf16[128,256]{1,0:T(8,128)(2,1)S(1)} %get-tuple-element.7), channel_id=1, source_target_pairs={{0,6},{1,7},{2,0},{3,1},{4,2},{5,3},{6,4},{7,5},{8,14},{9,15},{10,... | collective-permute-start | bytes 196616 | tf_op jit(solution)/shard_map/ppermute | solution.py:75
  52.8 5.3 %collective-permute-start.11 = (bf16[128,256]{1,0:T(8,128)(2,1)S(1)}, bf16[128,256]{1,0:T(8,128)(2,1)S(1)}, u32[]{:S(2)}, u32[]{:S(2)}) collective-permute-start(bf16[128,256]{1,0:T(8,128)(2,1)S(1)} %get-tuple-element.8), channel_id=1, source_target_pairs={{0,5},{1,6},{2,7},{3,0},{4,1},{5,2},{6,3},{7,4},{8,13},{9,14},{10,... | collective-permute-start | bytes 196616 | tf_op jit(solution)/shard_map/ppermute | solution.py:75
  52.8 11.5 %collective-permute-start.10 = (bf16[128,256]{1,0:T(8,128)(2,1)S(1)}, bf16[128,256]{1,0:T(8,128)(2,1)S(1)}, u32[]{:S(2)}, u32[]{:S(2)}) collective-permute-start(bf16[128,256]{1,0:T(8,128)(2,1)S(1)} %get-tuple-element.9), channel_id=1, source_target_pairs={{0,4},{1,5},{2,6},{3,7},{4,0},{5,1},{6,2},{7,3},{8,12},{9,13},{10,... | collective-permute-start | bytes 196616 | tf_op jit(solution)/shard_map/ppermute | solution.py:75
  55.8 10.1 %collective-permute-start.9 = (bf16[128,256]{1,0:T(8,128)(2,1)S(1)}, bf16[128,256]{1,0:T(8,128)(2,1)S(1)}, u32[]{:S(2)}, u32[]{:S(2)}) collective-permute-start(bf16[128,256]{1,0:T(8,128)(2,1)S(1)} %get-tuple-element.10), channel_id=1, source_target_pairs={{0,3},{1,4},{2,5},{3,6},{4,7},{5,0},{6,1},{7,2},{8,11},{9,12},{10,... | collective-permute-start | bytes 196616 | tf_op jit(solution)/shard_map/ppermute | solution.py:75
  55.8 10.1 %collective-permute-start.8 = (bf16[128,256]{1,0:T(8,128)(2,1)S(1)}, bf16[128,256]{1,0:T(8,128)(2,1)S(1)}, u32[]{:S(2)}, u32[]{:S(2)}) collective-permute-start(bf16[128,256]{1,0:T(8,128)(2,1)S(1)} %get-tuple-element.11), channel_id=1, source_target_pairs={{0,2},{1,3},{2,4},{3,5},{4,6},{5,7},{6,0},{7,1},{8,10},{9,11},{10,... | collective-permute-start | bytes 196616 | tf_op jit(solution)/shard_map/ppermute | solution.py:75

commit v2 on v1

v2 whole, which is shorter than its diff:
```python
import jax
import jax.numpy as jnp
from jax import lax
from jax.experimental import pallas as pl
from jax.experimental.pallas import tpu as pltpu
from jax.sharding import PartitionSpec as P


def _agg_kernel(rows_ref, blks_ref, panel_ref, tiles_ref, *rest):
    out_refs, acc_ref = rest[:-1], rest[-1]
    acc_ref[...] = jnp.zeros_like(acc_ref)
    for k in range(tiles_ref.shape[0]):
        acc_ref[rows_ref[k]] += jnp.dot(
            tiles_ref[k], panel_ref[blks_ref[k]], preferred_element_type=jnp.float32
        )
    for s, out_ref in enumerate(out_refs):
        out_ref[...] = acc_ref[s].astype(out_ref.dtype)


def aggregate(panel_blocks, tile_vals, send_row, src_block, n_rows):
    slots, blk, _ = tile_vals.shape
    feat = panel_blocks.shape[-1]
    smem = pl.BlockSpec(memory_space=pltpu.SMEM)
    vmem = pl.BlockSpec(memory_space=pltpu.VMEM)
    flops = 2 * slots * blk * blk * feat
    nbytes = 2 * (panel_blocks.size + tile_vals.size + n_rows * blk * feat)
    return pl.pallas_call(
        _agg_kernel,
        out_shape=[jax.ShapeDtypeStruct((blk, feat), jnp.bfloat16) for _ in range(n_rows)],
        in_specs=[smem, smem, vmem, vmem],
        out_specs=[vmem] * n_rows,
        scratch_shapes=[pltpu.VMEM((n_rows + 1, blk, feat), jnp.float32)],
        cost_estimate=pl.CostEstimate(flops=flops, bytes_accessed=nbytes, transcendentals=0),
    )(send_row, src_block, panel_blocks, tile_vals)


def exchange_rep(partial):
    n = lax.axis_size("rep")
    total = partial[0].astype(jnp.float32)
    for s in range(1, n):
        perm = [(src, (src + s) % n) for src in range(n)]
        total = total + lax.ppermute(partial[s], "rep", perm).astype(jnp.float32)
    return total


def make_body():
    def body(features, weight_one, weight_two, tile_values, tile_rows, tile_cols, tile_count):
        tile_vals = tile_values[0, 0]
        tile_row = tile_rows[0, 0]
        tile_col = tile_cols[0, 0]
        live_count = tile_count[0, 0]
        replicas = lax.axis_size("rep")
        n_src = lax.axis_size("blk")
        me = lax.axis_index("rep")
        slot_ids = lax.iota(jnp.int32, tile_row.shape[0])
        send_row = jnp.where(
            slot_ids < live_count, (jnp.clip(tile_row, 0, replicas - 1) - me) % replicas, replicas
        )
        src_block = jnp.clip(tile_col // replicas, 0, n_src - 1)
        hidden = features
        for layer_id in range(2):
            weight = weight_one if layer_id == 0 else weight_two
            panel = jnp.dot(hidden, weight, preferred_element_type=jnp.float32).astype(jnp.bfloat16)
            blocks = lax.all_gather(panel, "blk", axis=0, tiled=False)
            partial = aggregate(blocks, tile_vals, send_row, src_block, replicas)
            summed = exchange_rep(partial)
            if layer_id == 0:
                hidden = jnp.maximum(summed, 0.0).astype(jnp.bfloat16)
            else:
                return summed.astype(jnp.bfloat16)

    return body


def solution(mesh):
    in_specs = (
        P(("blk", "rep"), None),
        P(),
        P(),
        P("blk", "rep", None, None, None),
        P("blk", "rep", None),
        P("blk", "rep", None),
        P("blk", "rep"),
    )
    out_specs = P(("blk", "rep"), None)
    return jax.shard_map(make_body(), mesh=mesh, in_specs=in_specs, out_specs=out_specs, check_vma=False)
```

time: 67.1 us -> 57.5 us (0.86)
  waiting for transfers between devices: 14.9 us -> 8.18 us
  Pallas kernels: 11.1 us -> 5.23 us
  starting transfers between devices: 21.3 us -> 24.1 us
  local copies, waits for them, and re-layouts: 2.17 us -> 0.91 us
  matrix products: 1.2 us -> 2.04 us
    ppermute x14, waiting for transfers between devices: 14.9 us -> 8.18 us  [exchange_rep(): total = total + lax.ppermute(partial[s], 'rep', perm).astype(jnp.float32)]
    pallas_call x2, Pallas kernels: 11.1 us -> 5.23 us  [aggregate(): pl.pallas_call(_agg_kernel, out_shape=[jax.ShapeDtypeStruct((blk, feat),...]
    ppermute x14, starting transfers between devices: 21.3 us -> 24.1 us  [exchange_rep(): total = total + lax.ppermute(partial[s], 'rep', perm).astype(jnp.float32)]
    squeeze x2 -> x0, local copies, waits for them, and re-layouts: 2.15 us -> none  [exchange_rep(): piece = lax.dynamic_index_in_dim(partial, (me + s) % n, 0, keepdims=False)]
    unnamed x8, local copies, waits for them, and re-layouts: 0.02 us -> 0.91 us
    dot_general x2, matrix products: 1.2 us -> 2.04 us  [body(): jnp.dot(hidden, weight, preferred_element_type=jnp.float32)]
  transfers between devices with their start and end apart: 14 -> 14, of which waited for: 5 -> 7; matrix products, arithmetic and copies ran while one was open for 0% -> 0% of each run, Pallas kernels for 0% -> 0%
where the time goes in v2:
time: 57.5 us; the launch traced here: 57.2 us
  starting transfers between devices  24.1 us (42%)
  blocking collectives  13.9 us (24%)
  waiting for transfers between devices  8.18 us (14%)
  Pallas kernels  5.23 us (9%)
  other arithmetic  2.09 us (4%)
  matrix products  2.04 us (4%)
  local copies, waits for them, and re-layouts  0.91 us (2%)
  between operations  0.72 us (1%)
    ppermute x14, starting transfers between devices, exchange_rep(): total = total + lax.ppermute(partial[s], 'rep', perm).astype(jnp.float32)  24.1 us
    all_gather x2, blocking collectives, body(): blocks = lax.all_gather(panel, 'blk', axis=0, tiled=False)  13.9 us
    ppermute x14, waiting for transfers between devices, exchange_rep(): total = total + lax.ppermute(partial[s], 'rep', perm).astype(jnp.float32)  8.18 us
    pallas_call x2, Pallas kernels, aggregate(): pl.pallas_call(_agg_kernel, out_shape=[jax.ShapeDtypeStruct((blk, feat),...  5.23 us
    dot_general x2, matrix products, body(): jnp.dot(hidden, weight, preferred_element_type=jnp.float32)  2.04 us
    convert_element_type x1, other arithmetic, body(): return summed.astype(jnp.bfloat16)  1.54 us
  transfers between devices with their start and end apart: 14, of which 7 were waited for; matrix products, arithmetic and copies ran while one was open for 0% of the time, Pallas kernels for 0%

profile of v2, /device:TPU:0, one launch (start us, length us, event | category | flops | bytes accessed | tf_op | source)
XLA Modules:
  0.0 57.2 jit_solution(6329501293745627629)
XLA Ops:
  0.0 0.0 copy-start
  0.7 0.2 copy-done
  0.9 1.0 %convolution_convert_fusion.1 = bf16[128,256]{1,0:T(8,128)(2,1)S(1)} fusion(bf16[128,256]{1,0:T(8,128)(2,1)} %param.7, bf16[256,256]{1,0:T(8,128)(2,1)S(1)} %copy-done), kind=kOutput, calls=%fused_computation.1 | convolution fusion | flops 16809984 | bytes 262144 | tf_op jit(solution)/shard_map/dot_general | solution.py:63
  1.9 7.6 %all-gather = bf16[512,256]{1,0:T(8,128)(2,1)} all-gather(bf16[128,256]{1,0:T(8,128)(2,1)S(1)} %convolution_convert_fusion.1), channel_id=2, replica_groups=mesh['blk'=4,'rep'=8] {'blk'}, dimensions={0}, use_global_device_ids=true | all-gather | bytes 327680 | tf_op jit(solution)/shard_map/all_gather | solution.py:64
  9.6 0.0 copy-start.2
  9.6 0.0 copy-start.3
  9.6 0.7 %copy-done.2 = s32[1,1,24]{2,1,0:T(1,128)S(1)} copy-done((s32[1,1,24]{2,1,0:T(1,128)S(1)}, s32[1,1,24]{2,1,0:T(1,128)}, u32[]{:S(2)}) %copy-start.2) | copy-done | bytes 120
  10.2 0.0 copy-done.3
  10.2 0.5 compare_select_fusion.2
  10.8 0.0 copy-start.1
  10.8 2.6 %shard_map.73 = (bf16[128,256]{1,0:T(8,128)(2,1)}, bf16[128,256]{1,0:T(8,128)(2,1)}, bf16[128,256]{1,0:T(8,128)(2,1)}, bf16[128,256]{1,0:T(8,128)(2,1)}, bf16[12...) custom-call(s32[24]{0:T(128)} %get-tuple-element.37.rows_ref, ...), custom_call_target="tpu_custom_call" | custom-call | flops 201326592 | bytes 1572864 | tf_op jit(solution)/shard_map/pallas_call | solution.py:27
  13.4 1.6 %collective-permute-start = (bf16[128,256]{1,0:T(8,128)(2,1)}, bf16[128,256]{1,0:T(8,128)(2,1)S(1)}, u32[]{:S(2)}, u32[]{:S(2)}) collective-permute-start(bf16[128,256]{1,0:T(8,128)(2,1)} %get-tuple-element.22), channel_id=1, source_target_pairs={{0,1},{1,2},{2,3},{3,4},{4,5},{5,6},{6,7},{7,0},{8,9},{9,10},{10,1... | collective-permute-start | bytes 196616 | tf_op jit(solution)/shard_map/ppermute | solution.py:42
  15.0 1.6 %collective-permute-start.1 = (bf16[128,256]{1,0:T(8,128)(2,1)}, bf16[128,256]{1,0:T(8,128)(2,1)S(1)}, u32[]{:S(2)}, u32[]{:S(2)}) collective-permute-start(bf16[128,256]{1,0:T(8,128)(2,1)} %get-tuple-element.23), channel_id=1, source_target_pairs={{0,2},{1,3},{2,4},{3,5},{4,6},{5,7},{6,0},{7,1},{8,10},{9,11},{10,... | collective-permute-start | bytes 196616 | tf_op jit(solution)/shard_map/ppermute | solution.py:42
  16.6 2.5 %collective-permute-start.2 = (bf16[128,256]{1,0:T(8,128)(2,1)}, bf16[128,256]{1,0:T(8,128)(2,1)S(1)}, u32[]{:S(2)}, u32[]{:S(2)}) collective-permute-start(bf16[128,256]{1,0:T(8,128)(2,1)} %get-tuple-element.24), channel_id=1, source_target_pairs={{0,3},{1,4},{2,5},{3,6},{4,7},{5,0},{6,1},{7,2},{8,11},{9,12},{10,... | collective-permute-start | bytes 196616 | tf_op jit(solution)/shard_map/ppermute | solution.py:42
  19.1 1.2 %collective-permute-start.3 = (bf16[128,256]{1,0:T(8,128)(2,1)}, bf16[128,256]{1,0:T(8,128)(2,1)S(1)}, u32[]{:S(2)}, u32[]{:S(2)}) collective-permute-start(bf16[128,256]{1,0:T(8,128)(2,1)} %get-tuple-element.25), channel_id=1, source_target_pairs={{0,4},{1,5},{2,6},{3,7},{4,0},{5,1},{6,2},{7,3},{8,12},{9,13},{10,... | collective-permute-start | bytes 196616 | tf_op jit(solution)/shard_map/ppermute | solution.py:42
  20.3 2.6 %collective-permute-start.4 = (bf16[128,256]{1,0:T(8,128)(2,1)}, bf16[128,256]{1,0:T(8,128)(2,1)S(1)}, u32[]{:S(2)}, u32[]{:S(2)}) collective-permute-start(bf16[128,256]{1,0:T(8,128)(2,1)} %get-tuple-element.26), channel_id=1, source_target_pairs={{0,5},{1,6},{2,7},{3,0},{4,1},{5,2},{6,3},{7,4},{8,13},{9,14},{10,... | collective-permute-start | bytes 196616 | tf_op jit(solution)/shard_map/ppermute | solution.py:42
  23.0 0.0 collective-permute-done
  23.0 1.4 %collective-permute-start.5 = (bf16[128,256]{1,0:T(8,128)(2,1)}, bf16[128,256]{1,0:T(8,128)(2,1)S(1)}, u32[]{:S(2)}, u32[]{:S(2)}) collective-permute-start(bf16[128,256]{1,0:T(8,128)(2,1)} %get-tuple-element.27), channel_id=1, source_target_pairs={{0,6},{1,7},{2,0},{3,1},{4,2},{5,3},{6,4},{7,5},{8,14},{9,15},{10,... | collective-permute-start | bytes 196616 | tf_op jit(solution)/shard_map/ppermute | solution.py:42
  24.3 0.0 collective-permute-done.1
  24.3 1.4 %collective-permute-start.6 = (bf16[128,256]{1,0:T(8,128)(2,1)}, bf16[128,256]{1,0:T(8,128)(2,1)S(1)}, u32[]{:S(2)}, u32[]{:S(2)}) collective-permute-start(bf16[128,256]{1,0:T(8,128)(2,1)} %get-tuple-element.28), channel_id=1, source_target_pairs={{0,7},{1,0},{2,1},{3,2},{4,3},{5,4},{6,5},{7,6},{8,15},{9,8},{10,9... | collective-permute-start | bytes 196616 | tf_op jit(solution)/shard_map/ppermute | solution.py:42
  25.7 0.9 %collective-permute-done.2 = bf16[128,256]{1,0:T(8,128)(2,1)S(1)} collective-permute-done((bf16[128,256]{1,0:T(8,128)(2,1)}, bf16[128,256]{1,0:T(8,128)(2,1)S(1)}, u32[]{:S(2)}, u32[]{:S(2)}) %collective-permute-start.2) | collective-permute-done | bytes 65568 | tf_op jit(solution)/shard_map/ppermute | solution.py:42
  26.7 1.0 %collective-permute-done.3 = bf16[128,256]{1,0:T(8,128)(2,1)S(1)} collective-permute-done((bf16[128,256]{1,0:T(8,128)(2,1)}, bf16[128,256]{1,0:T(8,128)(2,1)S(1)}, u32[]{:S(2)}, u32[]{:S(2)}) %collective-permute-start.3) | collective-permute-done | bytes 65568 | tf_op jit(solution)/shard_map/ppermute | solution.py:42
  27.6 1.1 %collective-permute-done.4 = bf16[128,256]{1,0:T(8,128)(2,1)S(1)} collective-permute-done((bf16[128,256]{1,0:T(8,128)(2,1)}, bf16[128,256]{1,0:T(8,128)(2,1)S(1)}, u32[]{:S(2)}, u32[]{:S(2)}) %collective-permute-start.4) | collective-permute-done | bytes 65568 | tf_op jit(solution)/shard_map/ppermute | solution.py:42
  28.7 0.9 %collective-permute-done.5 = bf16[128,256]{1,0:T(8,128)(2,1)S(1)} collective-permute-done((bf16[128,256]{1,0:T(8,128)(2,1)}, bf16[128,256]{1,0:T(8,128)(2,1)S(1)}, u32[]{:S(2)}, u32[]{:S(2)}) %collective-permute-start.5) | collective-permute-done | bytes 65568 | tf_op jit(solution)/shard_map/ppermute | solution.py:42
  29.6 0.0 collective-permute-done.6
  29.6 0.0 copy-done.1
  29.6 1.0 %convolution_convert_fusion = bf16[128,256]{1,0:T(8,128)(2,1)S(1)} fusion(bf16[256,256]{1,0:T(8,128)(2,1)S(1)} %copy-done.1, bf16[128,256]{1,0:T(8,128)(2,1)S(1)} %collective-permute-done.6, bf16[128,256]{1,0:T(8,128)(2,1)S(1)} %collective-permute-done.5, bf16[128,256]{1,0:T(8,128)(2,1)S(1)} %collective-permute-done.4, ...), kind=kOutput, calls=%fused_computation | convolution fusion | flops 17367040 | bytes 720896 | tf_op jit(solution)/shard_map/dot_general | solution.py:63
  30.7 6.2 %all-gather.1 = bf16[512,256]{1,0:T(8,128)(2,1)} all-gather(bf16[128,256]{1,0:T(8,128)(2,1)S(1)} %convolution_convert_fusion), channel_id=3, replica_groups=mesh['blk'=4,'rep'=8] {'blk'}, dimensions={0}, use_global_device_ids=true | all-gather | bytes 327680 | tf_op jit(solution)/shard_map/all_gather | solution.py:64
  36.9 2.6 %shard_map.74 = (bf16[128,256]{1,0:T(8,128)(2,1)}, bf16[128,256]{1,0:T(8,128)(2,1)}, bf16[128,256]{1,0:T(8,128)(2,1)}, bf16[128,256]{1,0:T(8,128)(2,1)}, bf16[12...) custom-call(s32[24]{0:T(128)} %get-tuple-element.37.rows_ref, ...), custom_call_target="tpu_custom_call" | custom-call | flops 201326592 | bytes 1572864 | tf_op jit(solution)/shard_map/pallas_call | solution.py:27
  39.5 2.2 %collective-permute-start.7 = (bf16[128,256]{1,0:T(8,128)(2,1)}, bf16[128,256]{1,0:T(8,128)(2,1)S(1)}, u32[]{:S(2)}, u32[]{:S(2)}) collective-permute-start(bf16[128,256]{1,0:T(8,128)(2,1)} %get-tuple-element.30), channel_id=1, source_target_pairs={{0,1},{1,2},{2,3},{3,4},{4,5},{5,6},{6,7},{7,0},{8,9},{9,10},{10,1... | collective-permute-start | bytes 196616 | tf_op jit(solution)/shard_map/ppermute | solution.py:42
  41.7 2.0 %collective-permute-start.8 = (bf16[128,256]{1,0:T(8,128)(2,1)}, bf16[128,256]{1,0:T(8,128)(2,1)S(1)}, u32[]{:S(2)}, u32[]{:S(2)}) collective-permute-start(bf16[128,256]{1,0:T(8,128)(2,1)} %get-tuple-element.31), channel_id=1, source_target_pairs={{0,2},{1,3},{2,4},{3,5},{4,6},{5,7},{6,0},{7,1},{8,10},{9,11},{10,... | collective-permute-start | bytes 196616 | tf_op jit(solution)/shard_map/ppermute | solution.py:42
  43.7 0.8 %collective-permute-start.9 = (bf16[128,256]{1,0:T(8,128)(2,1)}, bf16[128,256]{1,0:T(8,128)(2,1)S(1)}, u32[]{:S(2)}, u32[]{:S(2)}) collective-permute-start(bf16[128,256]{1,0:T(8,128)(2,1)} %get-tuple-element.32), channel_id=1, source_target_pairs={{0,3},{1,4},{2,5},{3,6},{4,7},{5,0},{6,1},{7,2},{8,11},{9,12},{10,... | collective-permute-start | bytes 196616 | tf_op jit(solution)/shard_map/ppermute | solution.py:42
  44.4 1.7 %collective-permute-start.10 = (bf16[128,256]{1,0:T(8,128)(2,1)}, bf16[128,256]{1,0:T(8,128)(2,1)S(1)}, u32[]{:S(2)}, u32[]{:S(2)}) collective-permute-start(bf16[128,256]{1,0:T(8,128)(2,1)} %get-tuple-element.33), channel_id=1, source_target_pairs={{0,4},{1,5},{2,6},{3,7},{4,0},{5,1},{6,2},{7,3},{8,12},{9,13},{10,... | collective-permute-start | bytes 196616 | tf_op jit(solution)/shard_map/ppermute | solution.py:42
  46.2 2.4 %collective-permute-start.11 = (bf16[128,256]{1,0:T(8,128)(2,1)}, bf16[128,256]{1,0:T(8,128)(2,1)S(1)}, u32[]{:S(2)}, u32[]{:S(2)}) collective-permute-start(bf16[128,256]{1,0:T(8,128)(2,1)} %get-tuple-element.34), channel_id=1, source_target_pairs={{0,5},{1,6},{2,7},{3,0},{4,1},{5,2},{6,3},{7,4},{8,13},{9,14},{10,... | collective-permute-start | bytes 196616 | tf_op jit(solution)/shard_map/ppermute | solution.py:42
  48.6 0.0 collective-permute-done.7
  48.6 2.5 %collective-permute-start.12 = (bf16[128,256]{1,0:T(8,128)(2,1)}, bf16[128,256]{1,0:T(8,128)(2,1)S(1)}, u32[]{:S(2)}, u32[]{:S(2)}) collective-permute-start(bf16[128,256]{1,0:T(8,128)(2,1)} %get-tuple-element.35), channel_id=1, source_target_pairs={{0,6},{1,7},{2,0},{3,1},{4,2},{5,3},{6,4},{7,5},{8,14},{9,15},{10,... | collective-permute-start | bytes 196616 | tf_op jit(solution)/shard_map/ppermute | solution.py:42
  51.1 0.0 collective-permute-done.8
  51.1 0.2 collective-permute-start.13
  51.4 1.8 %collective-permute-done.9 = bf16[128,256]{1,0:T(8,128)(2,1)S(1)} collective-permute-done((bf16[128,256]{1,0:T(8,128)(2,1)}, bf16[128,256]{1,0:T(8,128)(2,1)S(1)}, u32[]{:S(2)}, u32[]{:S(2)}) %collective-permute-start.9) | collective-permute-done | bytes 65568 | tf_op jit(solution)/shard_map/ppermute | solution.py:42
  53.2 0.0 collective-permute-done.10
  53.2 0.0 collective-permute-done.11
  53.2 2.1 %collective-permute-done.12 = bf16[128,256]{1,0:T(8,128)(2,1)S(1)} collective-permute-done((bf16[128,256]{1,0:T(8,128)(2,1)}, bf16[128,256]{1,0:T(8,128)(2,1)S(1)}, u32[]{:S(2)}, u32[]{:S(2)}) %collective-permute-start.12) | collective-permute-done | bytes 65568 | tf_op jit(solution)/shard_map/ppermute | solution.py:42
  55.3 0.3 collective-permute-done.13
  55.6 1.5 %add_convert_fusion = bf16[128,256]{1,0:T(8,128)(2,1)} fusion(bf16[128,256]{1,0:T(8,128)(2,1)S(1)} %collective-permute-done.13, bf16[128,256]{1,0:T(8,128)(2,1)S(1)} %collective-permute-done.12, bf16[128,256]{1,0:T(8,128)(2,1)S(1)} %collective-permute-done.11, bf16[128,256]{1,0:T(8,128)(2,1)S(1)} %collective-permute-done.10, ...), kind=kLoop, calls=%fused_computation.2 | loop fusion | flops 524288 | bytes 589824 | tf_op jit(solution)/shard_map/convert_element_type | solution.py:70
Async XLA Ops:
  0.0 0.9 %copy-start = (bf16[256,256]{1,0:T(8,128)(2,1)S(1)}, bf16[256,256]{1,0:T(8,128)(2,1)}, u32[]{:S(2)}) copy-start(bf16[256,256]{1,0:T(8,128)(2,1)} %param.8) | copy-start | bytes 393220
  9.6 0.7 %copy-start.2 = (s32[1,1,24]{2,1,0:T(1,128)S(1)}, s32[1,1,24]{2,1,0:T(1,128)}, u32[]{:S(2)}) copy-start(s32[1,1,24]{2,1,0:T(1,128)} %param.11) | copy-start | bytes 292
  9.6 0.7 %copy-start.3 = (s32[1,1,24]{2,1,0:T(1,128)S(1)}, s32[1,1,24]{2,1,0:T(1,128)}, u32[]{:S(2)}) copy-start(s32[1,1,24]{2,1,0:T(1,128)} %param.12) | copy-start | bytes 292
  10.8 18.8 %copy-start.1 = (bf16[256,256]{1,0:T(8,128)(2,1)S(1)}, bf16[256,256]{1,0:T(8,128)(2,1)}, u32[]{:S(2)}) copy-start(bf16[256,256]{1,0:T(8,128)(2,1)} %param.9) | copy-start | bytes 393220
  13.4 9.5 %collective-permute-start = (bf16[128,256]{1,0:T(8,128)(2,1)}, bf16[128,256]{1,0:T(8,128)(2,1)S(1)}, u32[]{:S(2)}, u32[]{:S(2)}) collective-permute-start(bf16[128,256]{1,0:T(8,128)(2,1)} %get-tuple-element.22), channel_id=1, source_target_pairs={{0,1},{1,2},{2,3},{3,4},{4,5},{5,6},{6,7},{7,0},{8,9},{9,10},{10,1... | collective-permute-start | bytes 196616 | tf_op jit(solution)/shard_map/ppermute | solution.py:42
  15.0 9.3 %collective-permute-start.1 = (bf16[128,256]{1,0:T(8,128)(2,1)}, bf16[128,256]{1,0:T(8,128)(2,1)S(1)}, u32[]{:S(2)}, u32[]{:S(2)}) collective-permute-start(bf16[128,256]{1,0:T(8,128)(2,1)} %get-tuple-element.23), channel_id=1, source_target_pairs={{0,2},{1,3},{2,4},{3,5},{4,6},{5,7},{6,0},{7,1},{8,10},{9,11},{10,... | collective-permute-start | bytes 196616 | tf_op jit(solution)/shard_map/ppermute | solution.py:42
  16.6 10.1 %collective-permute-start.2 = (bf16[128,256]{1,0:T(8,128)(2,1)}, bf16[128,256]{1,0:T(8,128)(2,1)S(1)}, u32[]{:S(2)}, u32[]{:S(2)}) collective-permute-start(bf16[128,256]{1,0:T(8,128)(2,1)} %get-tuple-element.24), channel_id=1, source_target_pairs={{0,3},{1,4},{2,5},{3,6},{4,7},{5,0},{6,1},{7,2},{8,11},{9,12},{10,... | collective-permute-start | bytes 196616 | tf_op jit(solution)/shard_map/ppermute | solution.py:42
  19.1 8.5 %collective-permute-start.3 = (bf16[128,256]{1,0:T(8,128)(2,1)}, bf16[128,256]{1,0:T(8,128)(2,1)S(1)}, u32[]{:S(2)}, u32[]{:S(2)}) collective-permute-start(bf16[128,256]{1,0:T(8,128)(2,1)} %get-tuple-element.25), channel_id=1, source_target_pairs={{0,4},{1,5},{2,6},{3,7},{4,0},{5,1},{6,2},{7,3},{8,12},{9,13},{10,... | collective-permute-start | bytes 196616 | tf_op jit(solution)/shard_map/ppermute | solution.py:42
  20.3 8.4 %collective-permute-start.4 = (bf16[128,256]{1,0:T(8,128)(2,1)}, bf16[128,256]{1,0:T(8,128)(2,1)S(1)}, u32[]{:S(2)}, u32[]{:S(2)}) collective-permute-start(bf16[128,256]{1,0:T(8,128)(2,1)} %get-tuple-element.26), channel_id=1, source_target_pairs={{0,5},{1,6},{2,7},{3,0},{4,1},{5,2},{6,3},{7,4},{8,13},{9,14},{10,... | collective-permute-start | bytes 196616 | tf_op jit(solution)/shard_map/ppermute | solution.py:42
  23.0 6.7 %collective-permute-start.5 = (bf16[128,256]{1,0:T(8,128)(2,1)}, bf16[128,256]{1,0:T(8,128)(2,1)S(1)}, u32[]{:S(2)}, u32[]{:S(2)}) collective-permute-start(bf16[128,256]{1,0:T(8,128)(2,1)} %get-tuple-element.27), channel_id=1, source_target_pairs={{0,6},{1,7},{2,0},{3,1},{4,2},{5,3},{6,4},{7,5},{8,14},{9,15},{10,... | collective-permute-start | bytes 196616 | tf_op jit(solution)/shard_map/ppermute | solution.py:42
  24.3 5.3 %collective-permute-start.6 = (bf16[128,256]{1,0:T(8,128)(2,1)}, bf16[128,256]{1,0:T(8,128)(2,1)S(1)}, u32[]{:S(2)}, u32[]{:S(2)}) collective-permute-start(bf16[128,256]{1,0:T(8,128)(2,1)} %get-tuple-element.28), channel_id=1, source_target_pairs={{0,7},{1,0},{2,1},{3,2},{4,3},{5,4},{6,5},{7,6},{8,15},{9,8},{10,9... | collective-permute-start | bytes 196616 | tf_op jit(solution)/shard_map/ppermute | solution.py:42
  39.5 9.1 %collective-permute-start.7 = (bf16[128,256]{1,0:T(8,128)(2,1)}, bf16[128,256]{1,0:T(8,128)(2,1)S(1)}, u32[]{:S(2)}, u32[]{:S(2)}) collective-permute-start(bf16[128,256]{1,0:T(8,128)(2,1)} %get-tuple-element.30), channel_id=1, source_target_pairs={{0,1},{1,2},{2,3},{3,4},{4,5},{5,6},{6,7},{7,0},{8,9},{9,10},{10,1... | collective-permute-start | bytes 196616 | tf_op jit(solution)/shard_map/ppermute | solution.py:42
  41.7 9.5 %collective-permute-start.8 = (bf16[128,256]{1,0:T(8,128)(2,1)}, bf16[128,256]{1,0:T(8,128)(2,1)S(1)}, u32[]{:S(2)}, u32[]{:S(2)}) collective-permute-start(bf16[128,256]{1,0:T(8,128)(2,1)} %get-tuple-element.31), channel_id=1, source_target_pairs={{0,2},{1,3},{2,4},{3,5},{4,6},{5,7},{6,0},{7,1},{8,10},{9,11},{10,... | collective-permute-start | bytes 196616 | tf_op jit(solution)/shard_map/ppermute | solution.py:42
  43.7 9.5 %collective-permute-start.9 = (bf16[128,256]{1,0:T(8,128)(2,1)}, bf16[128,256]{1,0:T(8,128)(2,1)S(1)}, u32[]{:S(2)}, u32[]{:S(2)}) collective-permute-start(bf16[128,256]{1,0:T(8,128)(2,1)} %get-tuple-element.32), channel_id=1, source_target_pairs={{0,3},{1,4},{2,5},{3,6},{4,7},{5,0},{6,1},{7,2},{8,11},{9,12},{10,... | collective-permute-start | bytes 196616 | tf_op jit(solution)/shard_map/ppermute | solution.py:42
  44.4 8.8 %collective-permute-start.10 = (bf16[128,256]{1,0:T(8,128)(2,1)}, bf16[128,256]{1,0:T(8,128)(2,1)S(1)}, u32[]{:S(2)}, u32[]{:S(2)}) collective-permute-start(bf16[128,256]{1,0:T(8,128)(2,1)} %get-tuple-element.33), channel_id=1, source_target_pairs={{0,4},{1,5},{2,6},{3,7},{4,0},{5,1},{6,2},{7,3},{8,12},{9,13},{10,... | collective-permute-start | bytes 196616 | tf_op jit(solution)/shard_map/ppermute | solution.py:42
  46.2 7.0 %collective-permute-start.11 = (bf16[128,256]{1,0:T(8,128)(2,1)}, bf16[128,256]{1,0:T(8,128)(2,1)S(1)}, u32[]{:S(2)}, u32[]{:S(2)}) collective-permute-start(bf16[128,256]{1,0:T(8,128)(2,1)} %get-tuple-element.34), channel_id=1, source_target_pairs={{0,5},{1,6},{2,7},{3,0},{4,1},{5,2},{6,3},{7,4},{8,13},{9,14},{10,... | collective-permute-start | bytes 196616 | tf_op jit(solution)/shard_map/ppermute | solution.py:42
  48.6 6.7 %collective-permute-start.12 = (bf16[128,256]{1,0:T(8,128)(2,1)}, bf16[128,256]{1,0:T(8,128)(2,1)S(1)}, u32[]{:S(2)}, u32[]{:S(2)}) collective-permute-start(bf16[128,256]{1,0:T(8,128)(2,1)} %get-tuple-element.35), channel_id=1, source_target_pairs={{0,6},{1,7},{2,0},{3,1},{4,2},{5,3},{6,4},{7,5},{8,14},{9,15},{10,... | collective-permute-start | bytes 196616 | tf_op jit(solution)/shard_map/ppermute | solution.py:42
  51.1 4.5 %collective-permute-start.13 = (bf16[128,256]{1,0:T(8,128)(2,1)}, bf16[128,256]{1,0:T(8,128)(2,1)S(1)}, u32[]{:S(2)}, u32[]{:S(2)}) collective-permute-start(bf16[128,256]{1,0:T(8,128)(2,1)} %get-tuple-element.36), channel_id=1, source_target_pairs={{0,7},{1,0},{2,1},{3,2},{4,3},{5,4},{6,5},{7,6},{8,15},{9,8},{10,9... | collective-permute-start | bytes 196616 | tf_op jit(solution)/shard_map/ppermute | solution.py:42

commit v3 on v2

--- a/solution.py
+++ b/solution.py
@@ -36,10 +36,17 @@
 
 def exchange_rep(partial):
     n = lax.axis_size("rep")
-    total = partial[0].astype(jnp.float32)
-    for s in range(1, n):
-        perm = [(src, (src + s) % n) for src in range(n)]
-        total = total + lax.ppermute(partial[s], "rep", perm).astype(jnp.float32)
+    outer = n // 2
+    pair = [(src, src ^ 1) for src in range(n)]
+    total = None
+    for t in range(outer):
+        got = lax.ppermute(partial[t * 2 + 1], "rep", pair)
+        both = partial[t * 2].astype(jnp.float32) + got.astype(jnp.float32)
+        if t == 0:
+            total = both
+            continue
+        perm = [(src, ((src // 2 + t) % outer) * 2 + src % 2) for src in range(n)]
+        total = total + lax.ppermute(both.astype(jnp.bfloat16), "rep", perm).astype(jnp.float32)
     return total
 
 
@@ -53,9 +60,10 @@
         n_src = lax.axis_size("blk")
         me = lax.axis_index("rep")
         slot_ids = lax.iota(jnp.int32, tile_row.shape[0])
-        send_row = jnp.where(
-            slot_ids < live_count, (jnp.clip(tile_row, 0, replicas - 1) - me) % replicas, replicas
-        )
+        row = jnp.clip(tile_row, 0, replicas - 1)
+        outer = replicas // 2
+        send_pos = ((row // 2 - me // 2) % outer) * 2 + ((row % 2) ^ (me % 2))
+        send_row = jnp.where(slot_ids < live_count, send_pos, replicas)
         src_block = jnp.clip(tile_col // replicas, 0, n_src - 1)
         hidden = features
         for layer_id in range(2):

time: 57.5 us -> 53.4 us (0.929)
  starting transfers between devices: 24.1 us -> 20.7 us
  other arithmetic: 2.09 us -> 3.12 us
  waiting for transfers between devices: 8.18 us -> 7.25 us
  matrix products: 2.04 us -> 1.17 us
    ppermute x14, starting transfers between devices: 24.1 us -> 20.7 us  [the longest x6 12.6 us: exchange_rep(): lax.ppermute(both.astype(jnp.bfloat16), 'rep', perm).astype(jnp.float32)]
    convert_element_type x0 -> x6, other arithmetic: none -> 1.86 us  [exchange_rep(): both.astype(jnp.bfloat16)]
    ppermute x14, waiting for transfers between devices: 8.18 us -> 7.25 us  [the longest x6 4.58 us: exchange_rep(): lax.ppermute(both.astype(jnp.bfloat16), 'rep', perm).astype(jnp.float32)]
    convert_element_type x1, other arithmetic: 1.54 us -> 0.67 us  [body(): return summed.astype(jnp.bfloat16)]
    dot_general x2, matrix products: 2.04 us -> 1.17 us  [body(): jnp.dot(hidden, weight, preferred_element_type=jnp.float32)]
  transfers between devices with their start and end apart: 14 -> 14, of which waited for: 7 -> 8; matrix products, arithmetic and copies ran while one was open for 0% -> 4% of each run, Pallas kernels for 0% -> 0%
where the time goes in v3:
time: 53.4 us; the launch traced here: 53 us
  starting transfers between devices  20.7 us (39%)
  blocking collectives  13.9 us (26%)
  waiting for transfers between devices  7.25 us (14%)
  Pallas kernels  5.18 us (10%)
  other arithmetic  3.12 us (6%)
  matrix products  1.17 us (2%)
  local copies, waits for them, and re-layouts  0.93 us (2%)
  between operations  0.76 us (1%)
    all_gather x2, blocking collectives, body(): blocks = lax.all_gather(panel, 'blk', axis=0, tiled=False)  13.9 us
    ppermute x6, starting transfers between devices, exchange_rep(): lax.ppermute(both.astype(jnp.bfloat16), 'rep', perm).astype(jnp.float32)  12.6 us
    ppermute x8, starting transfers between devices, exchange_rep(): got = lax.ppermute(partial[t * 2 + 1], 'rep', pair)  8.11 us
    pallas_call x2, Pallas kernels, aggregate(): pl.pallas_call(_agg_kernel, out_shape=[jax.ShapeDtypeStruct((blk, feat),...  5.18 us
    ppermute x6, waiting for transfers between devices, exchange_rep(): lax.ppermute(both.astype(jnp.bfloat16), 'rep', perm).astype(jnp.float32)  4.58 us
    ppermute x8, waiting for transfers between devices, exchange_rep(): got = lax.ppermute(partial[t * 2 + 1], 'rep', pair)  2.68 us
    convert_element_type x6, other arithmetic, exchange_rep(): both.astype(jnp.bfloat16)  1.86 us
    dot_general x2, matrix products, body(): jnp.dot(hidden, weight, preferred_element_type=jnp.float32)  1.17 us
  transfers between devices with their start and end apart: 14, of which 8 were waited for; matrix products, arithmetic and copies ran while one was open for 4% of the time, Pallas kernels for 0%

profile of v3, /device:TPU:0, one launch (start us, length us, event | category | flops | bytes accessed | tf_op | source)
XLA Modules:
  0.0 53.0 jit_solution(4287773086917890531)
XLA Ops:
  0.0 0.0 copy-start
  0.7 0.2 copy-done
  0.9 1.0 %convolution_convert_fusion.1 = bf16[128,256]{1,0:T(8,128)(2,1)S(1)} fusion(bf16[128,256]{1,0:T(8,128)(2,1)} %param.7, bf16[256,256]{1,0:T(8,128)(2,1)S(1)} %copy-done), kind=kOutput, calls=%fused_computation.1 | convolution fusion | flops 16809984 | bytes 262144 | tf_op jit(solution)/shard_map/dot_general | solution.py:71
  1.9 7.6 %all-gather = bf16[512,256]{1,0:T(8,128)(2,1)} all-gather(bf16[128,256]{1,0:T(8,128)(2,1)S(1)} %convolution_convert_fusion.1), channel_id=2, replica_groups=mesh['blk'=4,'rep'=8] {'blk'}, dimensions={0}, use_global_device_ids=true | all-gather | bytes 327680 | tf_op jit(solution)/shard_map/all_gather | solution.py:72
  9.6 0.7 %copy-done.8 = s32[1,1,24]{2,1,0:T(1,128)S(1)} copy-done((s32[1,1,24]{2,1,0:T(1,128)S(1)}, s32[1,1,24]{2,1,0:T(1,128)}, u32[]{:S(2)}) %copy-start.8) | copy-done | bytes 120
  10.2 0.0 copy-done.9
  10.2 0.6 %compare_select_fusion.2 = (s32[24]{0:T(128)}, s32[24]{0:T(128)}) fusion(s32[1,1,24]{2,1,0:T(1,128)S(1)} %copy-done.8, s32[]{:T(128)S(6)} %select_n.37, s32[]{:T(128)S(6)} %select_n.34, s32[]{:T(128)} %bitcast.30, s32[1,1,24]{2,1,0:T(1,128)S(1)} %copy-done.9), kind=kLoop, calls=%fused_computation.17 | loop fusion | flops 1272 | bytes 396 | tf_op jit(solution)/shard_map/jit(_where)/select_n | solution.py:66
  10.8 2.6 %shard_map.73 = (bf16[128,256]{1,0:T(8,128)(2,1)}, bf16[128,256]{1,0:T(8,128)(2,1)}, bf16[128,256]{1,0:T(8,128)(2,1)}, bf16[128,256]{1,0:T(8,128)(2,1)}, bf16[12...) custom-call(s32[24]{0:T(128)} %get-tuple-element.37.rows_ref, ...), custom_call_target="tpu_custom_call" | custom-call | flops 201326592 | bytes 1572864 | tf_op jit(solution)/shard_map/pallas_call | solution.py:27
  13.4 1.6 %collective-permute-start.1 = (bf16[128,256]{1,0:T(8,128)(2,1)}, bf16[128,256]{1,0:T(8,128)(2,1)S(1)}, u32[]{:S(2)}, u32[]{:S(2)}) collective-permute-start(bf16[128,256]{1,0:T(8,128)(2,1)} %get-tuple-element.24), channel_id=1, source_target_pairs={{0,1},{1,0},{2,3},{3,2},{4,5},{5,4},{6,7},{7,6},{8,9},{9,8},{10,11... | collective-permute-start | bytes 196616 | tf_op jit(solution)/shard_map/ppermute | solution.py:43
  15.0 0.5 collective-permute-start
  15.4 1.6 %collective-permute-start.3 = (bf16[128,256]{1,0:T(8,128)(2,1)}, bf16[128,256]{1,0:T(8,128)(2,1)S(1)}, u32[]{:S(2)}, u32[]{:S(2)}) collective-permute-start(bf16[128,256]{1,0:T(8,128)(2,1)} %get-tuple-element.26), channel_id=1, source_target_pairs={{0,1},{1,0},{2,3},{3,2},{4,5},{5,4},{6,7},{7,6},{8,9},{9,8},{10,11... | collective-permute-start | bytes 196616 | tf_op jit(solution)/shard_map/ppermute | solution.py:43
  17.0 0.5 collective-permute-start.5
  17.5 0.7 %collective-permute-done.1 = bf16[128,256]{1,0:T(8,128)(2,1)S(1)} collective-permute-done((bf16[128,256]{1,0:T(8,128)(2,1)}, bf16[128,256]{1,0:T(8,128)(2,1)S(1)}, u32[]{:S(2)}, u32[]{:S(2)}) %collective-permute-start.1) | collective-permute-done | bytes 65568 | tf_op jit(solution)/shard_map/ppermute | solution.py:43
  18.1 0.9 %add_convert_fusion.6 = bf16[128,256]{1,0:T(8,128)(2,1)S(1)} fusion(bf16[128,256]{1,0:T(8,128)(2,1)S(1)} %collective-permute-done.1, bf16[128,256]{1,0:T(8,128)(2,1)} %get-tuple-element.23), kind=kLoop, calls=%fused_computation.9 | loop fusion | flops 131072 | bytes 196608 | tf_op jit(solution)/shard_map/convert_element_type | solution.py:49
  19.0 1.7 %collective-permute-start.2 = (bf16[128,256]{1,0:T(8,128)(2,1)S(1)}, bf16[128,256]{1,0:T(8,128)(2,1)S(1)}, u32[]{:S(2)}, u32[]{:S(2)}) collective-permute-start(bf16[128,256]{1,0:T(8,128)(2,1)S(1)} %add_convert_fusion.6), channel_id=1, source_target_pairs={{0,2},{1,3},{2,4},{3,5},{4,6},{5,7},{6,0},{7,1},{8,10},{9,11},{10,... | collective-permute-start | bytes 196616 | tf_op jit(solution)/shard_map/ppermute | solution.py:49
  20.7 0.7 %collective-permute-done.3 = bf16[128,256]{1,0:T(8,128)(2,1)S(1)} collective-permute-done((bf16[128,256]{1,0:T(8,128)(2,1)}, bf16[128,256]{1,0:T(8,128)(2,1)S(1)}, u32[]{:S(2)}, u32[]{:S(2)}) %collective-permute-start.3) | collective-permute-done | bytes 65568 | tf_op jit(solution)/shard_map/ppermute | solution.py:43
  21.5 0.0 copy-done.5
  21.5 0.0 copy-start.1
  21.5 2.7 %collective-permute-start.4 = (bf16[128,256]{1,0:T(8,128)(2,1)S(1)}, bf16[128,256]{1,0:T(8,128)(2,1)S(1)}, u32[]{:S(2)}, u32[]{:S(2)}) collective-permute-start(bf16[128,256]{1,0:T(8,128)(2,1)S(1)} %add_convert_fusion.5), channel_id=1, source_target_pairs={{0,4},{1,5},{2,6},{3,7},{4,0},{5,1},{6,2},{7,3},{8,12},{9,13},{10,... | collective-permute-start | bytes 196616 | tf_op jit(solution)/shard_map/ppermute | solution.py:49
  24.2 0.0 collective-permute-done.5
  24.2 0.0 copy-done.3
  24.2 1.8 %collective-permute-start.6 = (bf16[128,256]{1,0:T(8,128)(2,1)S(1)}, bf16[128,256]{1,0:T(8,128)(2,1)S(1)}, u32[]{:S(2)}, u32[]{:S(2)}) collective-permute-start(bf16[128,256]{1,0:T(8,128)(2,1)S(1)} %add_convert_fusion.4), channel_id=1, source_target_pairs={{0,6},{1,7},{2,0},{3,1},{4,2},{5,3},{6,4},{7,5},{8,14},{9,15},{10,... | collective-permute-start | bytes 196616 | tf_op jit(solution)/shard_map/ppermute | solution.py:49
  26.0 0.0 collective-permute-done
  26.0 0.0 collective-permute-done.2
  26.0 1.2 %collective-permute-done.4 = bf16[128,256]{1,0:T(8,128)(2,1)S(1)} collective-permute-done((bf16[128,256]{1,0:T(8,128)(2,1)S(1)}, bf16[128,256]{1,0:T(8,128)(2,1)S(1)}, u32[]{:S(2)}, u32[]{:S(2)}) %collective-permute-start.4) | collective-permute-done | bytes 65568 | tf_op jit(solution)/shard_map/ppermute | solution.py:49
  27.2 1.4 %collective-permute-done.6 = bf16[128,256]{1,0:T(8,128)(2,1)S(1)} collective-permute-done((bf16[128,256]{1,0:T(8,128)(2,1)S(1)}, bf16[128,256]{1,0:T(8,128)(2,1)S(1)}, u32[]{:S(2)}, u32[]{:S(2)}) %collective-permute-start.6) | collective-permute-done | bytes 65568 | tf_op jit(solution)/shard_map/ppermute | solution.py:49
  28.6 0.0 copy-done.1
  28.6 0.0 copy-done.7
  28.6 0.2 convolution_convert_fusion
  28.8 6.2 %all-gather.1 = bf16[512,256]{1,0:T(8,128)(2,1)} all-gather(bf16[128,256]{1,0:T(8,128)(2,1)S(1)} %convolution_convert_fusion), channel_id=3, replica_groups=mesh['blk'=4,'rep'=8] {'blk'}, dimensions={0}, use_global_device_ids=true | all-gather | bytes 327680 | tf_op jit(solution)/shard_map/all_gather | solution.py:72
  35.0 2.6 %shard_map.74 = (bf16[128,256]{1,0:T(8,128)(2,1)}, bf16[128,256]{1,0:T(8,128)(2,1)}, bf16[128,256]{1,0:T(8,128)(2,1)}, bf16[128,256]{1,0:T(8,128)(2,1)}, bf16[12...) custom-call(s32[24]{0:T(128)} %get-tuple-element.37.rows_ref, ...), custom_call_target="tpu_custom_call" | custom-call | flops 201326592 | bytes 1572864 | tf_op jit(solution)/shard_map/pallas_call | solution.py:27
  37.6 1.6 %collective-permute-start.8 = (bf16[128,256]{1,0:T(8,128)(2,1)}, bf16[128,256]{1,0:T(8,128)(2,1)S(1)}, u32[]{:S(2)}, u32[]{:S(2)}) collective-permute-start(bf16[128,256]{1,0:T(8,128)(2,1)} %get-tuple-element.32), channel_id=1, source_target_pairs={{0,1},{1,0},{2,3},{3,2},{4,5},{5,4},{6,7},{7,6},{8,9},{9,8},{10,11... | collective-permute-start | bytes 196616 | tf_op jit(solution)/shard_map/ppermute | solution.py:43
  39.2 0.5 collective-permute-start.7
  39.6 1.6 %collective-permute-start.10 = (bf16[128,256]{1,0:T(8,128)(2,1)}, bf16[128,256]{1,0:T(8,128)(2,1)S(1)}, u32[]{:S(2)}, u32[]{:S(2)}) collective-permute-start(bf16[128,256]{1,0:T(8,128)(2,1)} %get-tuple-element.34), channel_id=1, source_target_pairs={{0,1},{1,0},{2,3},{3,2},{4,5},{5,4},{6,7},{7,6},{8,9},{9,8},{10,11... | collective-permute-start | bytes 196616 | tf_op jit(solution)/shard_map/ppermute | solution.py:43
  41.2 0.5 collective-permute-start.12
  41.6 0.6 %collective-permute-done.8 = bf16[128,256]{1,0:T(8,128)(2,1)S(1)} collective-permute-done((bf16[128,256]{1,0:T(8,128)(2,1)}, bf16[128,256]{1,0:T(8,128)(2,1)S(1)}, u32[]{:S(2)}, u32[]{:S(2)}) %collective-permute-start.8) | collective-permute-done | bytes 65568 | tf_op jit(solution)/shard_map/ppermute | solution.py:43
  42.3 0.9 %add_convert_fusion.3 = bf16[128,256]{1,0:T(8,128)(2,1)S(1)} fusion(bf16[128,256]{1,0:T(8,128)(2,1)S(1)} %collective-permute-done.8, bf16[128,256]{1,0:T(8,128)(2,1)} %get-tuple-element.31), kind=kLoop, calls=%fused_computation.5 | loop fusion | flops 131072 | bytes 196608 | tf_op jit(solution)/shard_map/convert_element_type | solution.py:49
  43.2 1.9 %collective-permute-start.9 = (bf16[128,256]{1,0:T(8,128)(2,1)S(1)}, bf16[128,256]{1,0:T(8,128)(2,1)S(1)}, u32[]{:S(2)}, u32[]{:S(2)}) collective-permute-start(bf16[128,256]{1,0:T(8,128)(2,1)S(1)} %add_convert_fusion.3), channel_id=1, source_target_pairs={{0,2},{1,3},{2,4},{3,5},{4,6},{5,7},{6,0},{7,1},{8,10},{9,11},{10,... | collective-permute-start | bytes 196616 | tf_op jit(solution)/shard_map/ppermute | solution.py:49
  45.1 0.6 %collective-permute-done.10 = bf16[128,256]{1,0:T(8,128)(2,1)S(1)} collective-permute-done((bf16[128,256]{1,0:T(8,128)(2,1)}, bf16[128,256]{1,0:T(8,128)(2,1)S(1)}, u32[]{:S(2)}, u32[]{:S(2)}) %collective-permute-start.10) | collective-permute-done | bytes 65568 | tf_op jit(solution)/shard_map/ppermute | solution.py:43
  45.7 0.0 copy-done.4
  45.7 2.3 %collective-permute-start.11 = (bf16[128,256]{1,0:T(8,128)(2,1)S(1)}, bf16[128,256]{1,0:T(8,128)(2,1)S(1)}, u32[]{:S(2)}, u32[]{:S(2)}) collective-permute-start(bf16[128,256]{1,0:T(8,128)(2,1)S(1)} %add_convert_fusion.2), channel_id=1, source_target_pairs={{0,4},{1,5},{2,6},{3,7},{4,0},{5,1},{6,2},{7,3},{8,12},{9,13},{10,... | collective-permute-start | bytes 196616 | tf_op jit(solution)/shard_map/ppermute | solution.py:49
  48.0 0.0 collective-permute-done.12
  48.0 2.3 %collective-permute-start.13 = (bf16[128,256]{1,0:T(8,128)(2,1)S(1)}, bf16[128,256]{1,0:T(8,128)(2,1)S(1)}, u32[]{:S(2)}, u32[]{:S(2)}) collective-permute-start(bf16[128,256]{1,0:T(8,128)(2,1)S(1)} %add_convert_fusion.1), channel_id=1, source_target_pairs={{0,6},{1,7},{2,0},{3,1},{4,2},{5,3},{6,4},{7,5},{8,14},{9,15},{10,... | collective-permute-start | bytes 196616 | tf_op jit(solution)/shard_map/ppermute | solution.py:49
  50.3 0.0 collective-permute-done.7
  50.3 0.0 collective-permute-done.9
  50.3 0.9 %collective-permute-done.11 = bf16[128,256]{1,0:T(8,128)(2,1)S(1)} collective-permute-done((bf16[128,256]{1,0:T(8,128)(2,1)S(1)}, bf16[128,256]{1,0:T(8,128)(2,1)S(1)}, u32[]{:S(2)}, u32[]{:S(2)}) %collective-permute-start.11) | collective-permute-done | bytes 65568 | tf_op jit(solution)/shard_map/ppermute | solution.py:49
  51.2 1.2 %collective-permute-done.13 = bf16[128,256]{1,0:T(8,128)(2,1)S(1)} collective-permute-done((bf16[128,256]{1,0:T(8,128)(2,1)S(1)}, bf16[128,256]{1,0:T(8,128)(2,1)S(1)}, u32[]{:S(2)}, u32[]{:S(2)}) %collective-permute-start.13) | collective-permute-done | bytes 65568 | tf_op jit(solution)/shard_map/ppermute | solution.py:49
  52.4 0.7 %add_convert_fusion = bf16[128,256]{1,0:T(8,128)(2,1)} fusion(bf16[128,256]{1,0:T(8,128)(2,1)S(1)} %collective-permute-done.13, bf16[128,256]{1,0:T(8,128)(2,1)S(1)} %collective-permute-done.11, bf16[128,256]{1,0:T(8,128)(2,1)S(1)} %collective-permute-done.9, bf16[128,256]{1,0:T(8,128)(2,1)S(1)} %collective-permute-done.7, bf16[128,256]{1,0:T(8,128)(2,1)S(1)} %copy-done.6), kind=kLoop, calls=%fused_computation.2 | loop fusion | flops 327680 | bytes 393216 | tf_op jit(solution)/shard_map/convert_element_type | solution.py:78
  (14 shorter events, 0.1 us)
Async XLA Ops:
  0.0 0.9 %copy-start = (bf16[256,256]{1,0:T(8,128)(2,1)S(1)}, bf16[256,256]{1,0:T(8,128)(2,1)}, u32[]{:S(2)}) copy-start(bf16[256,256]{1,0:T(8,128)(2,1)} %param.8) | copy-start | bytes 393220
  9.6 0.7 %copy-start.8 = (s32[1,1,24]{2,1,0:T(1,128)S(1)}, s32[1,1,24]{2,1,0:T(1,128)}, u32[]{:S(2)}) copy-start(s32[1,1,24]{2,1,0:T(1,128)} %param.11) | copy-start | bytes 292
  9.6 0.7 %copy-start.9 = (s32[1,1,24]{2,1,0:T(1,128)S(1)}, s32[1,1,24]{2,1,0:T(1,128)}, u32[]{:S(2)}) copy-start(s32[1,1,24]{2,1,0:T(1,128)} %param.12) | copy-start | bytes 292
  13.4 4.7 %collective-permute-start.1 = (bf16[128,256]{1,0:T(8,128)(2,1)}, bf16[128,256]{1,0:T(8,128)(2,1)S(1)}, u32[]{:S(2)}, u32[]{:S(2)}) collective-permute-start(bf16[128,256]{1,0:T(8,128)(2,1)} %get-tuple-element.24), channel_id=1, source_target_pairs={{0,1},{1,0},{2,3},{3,2},{4,5},{5,4},{6,7},{7,6},{8,9},{9,8},{10,11... | collective-permute-start | bytes 196616 | tf_op jit(solution)/shard_map/ppermute | solution.py:43
  15.0 11.1 %collective-permute-start = (bf16[128,256]{1,0:T(8,128)(2,1)}, bf16[128,256]{1,0:T(8,128)(2,1)S(1)}, u32[]{:S(2)}, u32[]{:S(2)}) collective-permute-start(bf16[128,256]{1,0:T(8,128)(2,1)} %get-tuple-element.22), channel_id=1, source_target_pairs={{0,1},{1,0},{2,3},{3,2},{4,5},{5,4},{6,7},{7,6},{8,9},{9,8},{10,11... | collective-permute-start | bytes 196616 | tf_op jit(solution)/shard_map/ppermute | solution.py:43
  15.4 6.0 %collective-permute-start.3 = (bf16[128,256]{1,0:T(8,128)(2,1)}, bf16[128,256]{1,0:T(8,128)(2,1)S(1)}, u32[]{:S(2)}, u32[]{:S(2)}) collective-permute-start(bf16[128,256]{1,0:T(8,128)(2,1)} %get-tuple-element.26), channel_id=1, source_target_pairs={{0,1},{1,0},{2,3},{3,2},{4,5},{5,4},{6,7},{7,6},{8,9},{9,8},{10,11... | collective-permute-start | bytes 196616 | tf_op jit(solution)/shard_map/ppermute | solution.py:43
  17.0 7.2 %collective-permute-start.5 = (bf16[128,256]{1,0:T(8,128)(2,1)}, bf16[128,256]{1,0:T(8,128)(2,1)S(1)}, u32[]{:S(2)}, u32[]{:S(2)}) collective-permute-start(bf16[128,256]{1,0:T(8,128)(2,1)} %get-tuple-element.28), channel_id=1, source_target_pairs={{0,1},{1,0},{2,3},{3,2},{4,5},{5,4},{6,7},{7,6},{8,9},{9,8},{10,11... | collective-permute-start | bytes 196616 | tf_op jit(solution)/shard_map/ppermute | solution.py:43
  18.1 3.3 %copy-start.5 = (bf16[128,256]{1,0:T(8,128)(2,1)S(1)}, bf16[128,256]{1,0:T(8,128)(2,1)}, u32[]{:S(2)}) copy-start(bf16[128,256]{1,0:T(8,128)(2,1)} %get-tuple-element.25) | copy-start | bytes 196612
  19.0 7.0 %collective-permute-start.2 = (bf16[128,256]{1,0:T(8,128)(2,1)S(1)}, bf16[128,256]{1,0:T(8,128)(2,1)S(1)}, u32[]{:S(2)}, u32[]{:S(2)}) collective-permute-start(bf16[128,256]{1,0:T(8,128)(2,1)S(1)} %add_convert_fusion.6), channel_id=1, source_target_pairs={{0,2},{1,3},{2,4},{3,5},{4,6},{5,7},{6,0},{7,1},{8,10},{9,11},{10,... | collective-permute-start | bytes 196616 | tf_op jit(solution)/shard_map/ppermute | solution.py:49
  21.5 2.7 %copy-start.3 = (bf16[128,256]{1,0:T(8,128)(2,1)S(1)}, bf16[128,256]{1,0:T(8,128)(2,1)}, u32[]{:S(2)}) copy-start(bf16[128,256]{1,0:T(8,128)(2,1)} %get-tuple-element.27) | copy-start | bytes 196612
  21.5 7.1 %copy-start.1 = (bf16[256,256]{1,0:T(8,128)(2,1)S(1)}, bf16[256,256]{1,0:T(8,128)(2,1)}, u32[]{:S(2)}) copy-start(bf16[256,256]{1,0:T(8,128)(2,1)} %param.9) | copy-start | bytes 393220
  21.5 5.7 %collective-permute-start.4 = (bf16[128,256]{1,0:T(8,128)(2,1)S(1)}, bf16[128,256]{1,0:T(8,128)(2,1)S(1)}, u32[]{:S(2)}, u32[]{:S(2)}) collective-permute-start(bf16[128,256]{1,0:T(8,128)(2,1)S(1)} %add_convert_fusion.5), channel_id=1, source_target_pairs={{0,4},{1,5},{2,6},{3,7},{4,0},{5,1},{6,2},{7,3},{8,12},{9,13},{10,... | collective-permute-start | bytes 196616 | tf_op jit(solution)/shard_map/ppermute | solution.py:49
  24.2 4.3 %copy-start.7 = (bf16[128,256]{1,0:T(8,128)(2,1)S(1)}, bf16[128,256]{1,0:T(8,128)(2,1)}, u32[]{:S(2)}) copy-start(bf16[128,256]{1,0:T(8,128)(2,1)} %get-tuple-element.21) | copy-start | bytes 196612
  24.2 4.3 %collective-permute-start.6 = (bf16[128,256]{1,0:T(8,128)(2,1)S(1)}, bf16[128,256]{1,0:T(8,128)(2,1)S(1)}, u32[]{:S(2)}, u32[]{:S(2)}) collective-permute-start(bf16[128,256]{1,0:T(8,128)(2,1)S(1)} %add_convert_fusion.4), channel_id=1, source_target_pairs={{0,6},{1,7},{2,0},{3,1},{4,2},{5,3},{6,4},{7,5},{8,14},{9,15},{10,... | collective-permute-start | bytes 196616 | tf_op jit(solution)/shard_map/ppermute | solution.py:49
  37.6 4.7 %collective-permute-start.8 = (bf16[128,256]{1,0:T(8,128)(2,1)}, bf16[128,256]{1,0:T(8,128)(2,1)S(1)}, u32[]{:S(2)}, u32[]{:S(2)}) collective-permute-start(bf16[128,256]{1,0:T(8,128)(2,1)} %get-tuple-element.32), channel_id=1, source_target_pairs={{0,1},{1,0},{2,3},{3,2},{4,5},{5,4},{6,7},{7,6},{8,9},{9,8},{10,11... | collective-permute-start | bytes 196616 | tf_op jit(solution)/shard_map/ppermute | solution.py:43
  39.2 11.1 %collective-permute-start.7 = (bf16[128,256]{1,0:T(8,128)(2,1)}, bf16[128,256]{1,0:T(8,128)(2,1)S(1)}, u32[]{:S(2)}, u32[]{:S(2)}) collective-permute-start(bf16[128,256]{1,0:T(8,128)(2,1)} %get-tuple-element.30), channel_id=1, source_target_pairs={{0,1},{1,0},{2,3},{3,2},{4,5},{5,4},{6,7},{7,6},{8,9},{9,8},{10,11... | collective-permute-start | bytes 196616 | tf_op jit(solution)/shard_map/ppermute | solution.py:43
  39.6 6.0 %collective-permute-start.10 = (bf16[128,256]{1,0:T(8,128)(2,1)}, bf16[128,256]{1,0:T(8,128)(2,1)S(1)}, u32[]{:S(2)}, u32[]{:S(2)}) collective-permute-start(bf16[128,256]{1,0:T(8,128)(2,1)} %get-tuple-element.34), channel_id=1, source_target_pairs={{0,1},{1,0},{2,3},{3,2},{4,5},{5,4},{6,7},{7,6},{8,9},{9,8},{10,11... | collective-permute-start | bytes 196616 | tf_op jit(solution)/shard_map/ppermute | solution.py:43
  41.2 6.8 %collective-permute-start.12 = (bf16[128,256]{1,0:T(8,128)(2,1)}, bf16[128,256]{1,0:T(8,128)(2,1)S(1)}, u32[]{:S(2)}, u32[]{:S(2)}) collective-permute-start(bf16[128,256]{1,0:T(8,128)(2,1)} %get-tuple-element.36), channel_id=1, source_target_pairs={{0,1},{1,0},{2,3},{3,2},{4,5},{5,4},{6,7},{7,6},{8,9},{9,8},{10,11... | collective-permute-start | bytes 196616 | tf_op jit(solution)/shard_map/ppermute | solution.py:43
  42.3 3.4 %copy-start.4 = (bf16[128,256]{1,0:T(8,128)(2,1)S(1)}, bf16[128,256]{1,0:T(8,128)(2,1)}, u32[]{:S(2)}) copy-start(bf16[128,256]{1,0:T(8,128)(2,1)} %get-tuple-element.33) | copy-start | bytes 196612
  43.2 7.1 %collective-permute-start.9 = (bf16[128,256]{1,0:T(8,128)(2,1)S(1)}, bf16[128,256]{1,0:T(8,128)(2,1)S(1)}, u32[]{:S(2)}, u32[]{:S(2)}) collective-permute-start(bf16[128,256]{1,0:T(8,128)(2,1)S(1)} %add_convert_fusion.3), channel_id=1, source_target_pairs={{0,2},{1,3},{2,4},{3,5},{4,6},{5,7},{6,0},{7,1},{8,10},{9,11},{10,... | collective-permute-start | bytes 196616 | tf_op jit(solution)/shard_map/ppermute | solution.py:49
  45.7 2.3 %copy-start.2 = (bf16[128,256]{1,0:T(8,128)(2,1)S(1)}, bf16[128,256]{1,0:T(8,128)(2,1)}, u32[]{:S(2)}) copy-start(bf16[128,256]{1,0:T(8,128)(2,1)} %get-tuple-element.35) | copy-start | bytes 196612
  45.7 5.5 %collective-permute-start.11 = (bf16[128,256]{1,0:T(8,128)(2,1)S(1)}, bf16[128,256]{1,0:T(8,128)(2,1)S(1)}, u32[]{:S(2)}, u32[]{:S(2)}) collective-permute-start(bf16[128,256]{1,0:T(8,128)(2,1)S(1)} %add_convert_fusion.2), channel_id=1, source_target_pairs={{0,4},{1,5},{2,6},{3,7},{4,0},{5,1},{6,2},{7,3},{8,12},{9,13},{10,... | collective-permute-start | bytes 196616 | tf_op jit(solution)/shard_map/ppermute | solution.py:49
  48.0 4.4 %copy-start.6 = (bf16[128,256]{1,0:T(8,128)(2,1)S(1)}, bf16[128,256]{1,0:T(8,128)(2,1)}, u32[]{:S(2)}) copy-start(bf16[128,256]{1,0:T(8,128)(2,1)} %get-tuple-element.29) | copy-start | bytes 196612
  48.0 4.4 %collective-permute-start.13 = (bf16[128,256]{1,0:T(8,128)(2,1)S(1)}, bf16[128,256]{1,0:T(8,128)(2,1)S(1)}, u32[]{:S(2)}, u32[]{:S(2)}) collective-permute-start(bf16[128,256]{1,0:T(8,128)(2,1)S(1)} %add_convert_fusion.1), channel_id=1, source_target_pairs={{0,6},{1,7},{2,0},{3,1},{4,2},{5,3},{6,4},{7,5},{8,14},{9,15},{10,... | collective-permute-start | bytes 196616 | tf_op jit(solution)/shard_map/ppermute | solution.py:49

commit v4 on v3

--- a/solution.py
+++ b/solution.py
@@ -6,18 +6,26 @@
 from jax.sharding import PartitionSpec as P
 
 
-def _agg_kernel(rows_ref, blks_ref, panel_ref, tiles_ref, *rest):
+def _agg_kernel(rows_ref, cols_ref, cnt_ref, panel_ref, tiles_ref, *rest):
     out_refs, acc_ref = rest[:-1], rest[-1]
+    n_rows = len(out_refs)
+    outer = n_rows // 2
+    n_src = panel_ref.shape[0]
+    me = lax.axis_index("rep")
+    live = cnt_ref[0]
     acc_ref[...] = jnp.zeros_like(acc_ref)
     for k in range(tiles_ref.shape[0]):
-        acc_ref[rows_ref[k]] += jnp.dot(
-            tiles_ref[k], panel_ref[blks_ref[k]], preferred_element_type=jnp.float32
-        )
+        row = jnp.clip(rows_ref[k], 0, n_rows - 1)
+        step = (row // 2 - me // 2 + outer) % outer
+        pos = step * 2 + (row % 2 + me % 2) % 2
+        dest = jnp.where(k < live, pos, n_rows)
+        src = jnp.clip(cols_ref[k] // n_rows, 0, n_src - 1)
+        acc_ref[dest] += jnp.dot(tiles_ref[k], panel_ref[src], preferred_element_type=jnp.float32)
     for s, out_ref in enumerate(out_refs):
         out_ref[...] = acc_ref[s].astype(out_ref.dtype)
 
 
-def aggregate(panel_blocks, tile_vals, send_row, src_block, n_rows):
+def aggregate(panel_blocks, tile_vals, tile_row, tile_col, live_count, n_rows):
     slots, blk, _ = tile_vals.shape
     feat = panel_blocks.shape[-1]
     smem = pl.BlockSpec(memory_space=pltpu.SMEM)
@@ -27,11 +35,11 @@
     return pl.pallas_call(
         _agg_kernel,
         out_shape=[jax.ShapeDtypeStruct((blk, feat), jnp.bfloat16) for _ in range(n_rows)],
-        in_specs=[smem, smem, vmem, vmem],
+        in_specs=[smem, smem, smem, vmem, vmem],
         out_specs=[vmem] * n_rows,
         scratch_shapes=[pltpu.VMEM((n_rows + 1, blk, feat), jnp.float32)],
         cost_estimate=pl.CostEstimate(flops=flops, bytes_accessed=nbytes, transcendentals=0),
-    )(send_row, src_block, panel_blocks, tile_vals)
+    )(tile_row, tile_col, live_count.reshape(1), panel_blocks, tile_vals)
 
 
 def exchange_rep(partial):
@@ -57,20 +65,12 @@
         tile_col = tile_cols[0, 0]
         live_count = tile_count[0, 0]
         replicas = lax.axis_size("rep")
-        n_src = lax.axis_size("blk")
-        me = lax.axis_index("rep")
-        slot_ids = lax.iota(jnp.int32, tile_row.shape[0])
-        row = jnp.clip(tile_row, 0, replicas - 1)
-        outer = replicas // 2
-        send_pos = ((row // 2 - me // 2) % outer) * 2 + ((row % 2) ^ (me % 2))
-        send_row = jnp.where(slot_ids < live_count, send_pos, replicas)
-        src_block = jnp.clip(tile_col // replicas, 0, n_src - 1)
         hidden = features
         for layer_id in range(2):
             weight = weight_one if layer_id == 0 else weight_two
             panel = jnp.dot(hidden, weight, preferred_element_type=jnp.float32).astype(jnp.bfloat16)
             blocks = lax.all_gather(panel, "blk", axis=0, tiled=False)
-            partial = aggregate(blocks, tile_vals, send_row, src_block, replicas)
+            partial = aggregate(blocks, tile_vals, tile_row, tile_col, live_count, replicas)
             summed = exchange_rep(partial)
             if layer_id == 0:
                 hidden = jnp.maximum(summed, 0.0).astype(jnp.bfloat16)

time: 53.4 us -> 52.3 us (0.979)
  local copies, waits for them, and re-layouts: 0.93 us -> 0.26 us
  other arithmetic: 3.12 us -> 2.54 us
    unnamed x20 -> x16, local copies, waits for them, and re-layouts: 0.93 us -> 0.26 us
    select_n x1 -> x0, other arithmetic: 0.58 us -> none  [body(): send_row = jnp.where(slot_ids < live_count, send_pos, replicas)]
where the time goes in v4:
time: 52.3 us; the launch traced here: 51.9 us
  starting transfers between devices  20.7 us (40%)
  blocking collectives  13.9 us (27%)
  waiting for transfers between devices  7.28 us (14%)
  Pallas kernels  5.32 us (10%)
  other arithmetic  2.54 us (5%)
  matrix products  1.18 us (2%)
  between operations  0.76 us (1%)
    all_gather x2, blocking collectives, body(): blocks = lax.all_gather(panel, 'blk', axis=0, tiled=False)  13.9 us
    ppermute x6, starting transfers between devices, exchange_rep(): lax.ppermute(both.astype(jnp.bfloat16), 'rep', perm).astype(jnp.float32)  12.6 us
    ppermute x8, starting transfers between devices, exchange_rep(): got = lax.ppermute(partial[t * 2 + 1], 'rep', pair)  8.11 us
    pallas_call x2, Pallas kernels, aggregate(): pl.pallas_call(_agg_kernel, out_shape=[jax.ShapeDtypeStruct((blk, feat),...  5.32 us
    ppermute x6, waiting for transfers between devices, exchange_rep(): lax.ppermute(both.astype(jnp.bfloat16), 'rep', perm).astype(jnp.float32)  4.58 us
    ppermute x8, waiting for transfers between devices, exchange_rep(): got = lax.ppermute(partial[t * 2 + 1], 'rep', pair)  2.7 us
    convert_element_type x6, other arithmetic, exchange_rep(): both.astype(jnp.bfloat16)  1.86 us
    dot_general x2, matrix products, body(): jnp.dot(hidden, weight, preferred_element_type=jnp.float32)  1.18 us
  transfers between devices with their start and end apart: 14, of which 8 were waited for; matrix products, arithmetic and copies ran while one was open for 4% of the time, Pallas kernels for 0%

profile of v4, /device:TPU:0, one launch (start us, length us, event | category | flops | bytes accessed | tf_op | source)
XLA Modules:
  0.0 51.9 jit_solution(8011865712731276707)
XLA Ops:
  0.0 0.0 copy-start
  0.7 0.2 copy-done
  0.9 1.0 %convolution_convert_fusion.1 = bf16[128,256]{1,0:T(8,128)(2,1)S(1)} fusion(bf16[128,256]{1,0:T(8,128)(2,1)} %param.7, bf16[256,256]{1,0:T(8,128)(2,1)S(1)} %copy-done), kind=kOutput, calls=%fused_computation.1 | convolution fusion | flops 16809984 | bytes 262144 | tf_op jit(solution)/shard_map/dot_general | solution.py:71
  1.9 7.6 %all-gather = bf16[512,256]{1,0:T(8,128)(2,1)} all-gather(bf16[128,256]{1,0:T(8,128)(2,1)S(1)} %convolution_convert_fusion.1), channel_id=2, replica_groups=mesh['blk'=4,'rep'=8] {'blk'}, dimensions={0}, use_global_device_ids=true | all-gather | bytes 327680 | tf_op jit(solution)/shard_map/all_gather | solution.py:72
  9.6 2.7 %shard_map.73 = (bf16[128,256]{1,0:T(8,128)(2,1)}, bf16[128,256]{1,0:T(8,128)(2,1)}, bf16[128,256]{1,0:T(8,128)(2,1)}, bf16[128,256]{1,0:T(8,128)(2,1)}, bf16[12...) custom-call(s32[24]{0:T(128)} %bitcast.15, s32[24]{0:T(128)} %bitcast.17, ...), custom_call_target="tpu_custom_call" | custom-call | flops 201326592 | bytes 1572864 | tf_op jit(solution)/shard_map/pallas_call | solution.py:35
  12.2 1.6 %collective-permute-start.1 = (bf16[128,256]{1,0:T(8,128)(2,1)}, bf16[128,256]{1,0:T(8,128)(2,1)S(1)}, u32[]{:S(2)}, u32[]{:S(2)}) collective-permute-start(bf16[128,256]{1,0:T(8,128)(2,1)} %get-tuple-element.24), channel_id=1, source_target_pairs={{0,1},{1,0},{2,3},{3,2},{4,5},{5,4},{6,7},{7,6},{8,9},{9,8},{10,11... | collective-permute-start | bytes 196616 | tf_op jit(solution)/shard_map/ppermute | solution.py:51
  13.8 0.5 collective-permute-start
  14.3 1.6 %collective-permute-start.3 = (bf16[128,256]{1,0:T(8,128)(2,1)}, bf16[128,256]{1,0:T(8,128)(2,1)S(1)}, u32[]{:S(2)}, u32[]{:S(2)}) collective-permute-start(bf16[128,256]{1,0:T(8,128)(2,1)} %get-tuple-element.26), channel_id=1, source_target_pairs={{0,1},{1,0},{2,3},{3,2},{4,5},{5,4},{6,7},{7,6},{8,9},{9,8},{10,11... | collective-permute-start | bytes 196616 | tf_op jit(solution)/shard_map/ppermute | solution.py:51
  15.8 0.5 collective-permute-start.5
  16.3 0.7 %collective-permute-done.1 = bf16[128,256]{1,0:T(8,128)(2,1)S(1)} collective-permute-done((bf16[128,256]{1,0:T(8,128)(2,1)}, bf16[128,256]{1,0:T(8,128)(2,1)S(1)}, u32[]{:S(2)}, u32[]{:S(2)}) %collective-permute-start.1) | collective-permute-done | bytes 65568 | tf_op jit(solution)/shard_map/ppermute | solution.py:51
  17.0 0.0 copy-start.5
  17.0 0.9 %add_convert_fusion.6 = bf16[128,256]{1,0:T(8,128)(2,1)S(1)} fusion(bf16[128,256]{1,0:T(8,128)(2,1)S(1)} %collective-permute-done.1, bf16[128,256]{1,0:T(8,128)(2,1)} %get-tuple-element.23), kind=kLoop, calls=%fused_computation.9 | loop fusion | flops 131072 | bytes 196608 | tf_op jit(solution)/shard_map/convert_element_type | solution.py:57
  17.9 1.7 %collective-permute-start.2 = (bf16[128,256]{1,0:T(8,128)(2,1)S(1)}, bf16[128,256]{1,0:T(8,128)(2,1)S(1)}, u32[]{:S(2)}, u32[]{:S(2)}) collective-permute-start(bf16[128,256]{1,0:T(8,128)(2,1)S(1)} %add_convert_fusion.6), channel_id=1, source_target_pairs={{0,2},{1,3},{2,4},{3,5},{4,6},{5,7},{6,0},{7,1},{8,10},{9,11},{10,... | collective-permute-start | bytes 196616 | tf_op jit(solution)/shard_map/ppermute | solution.py:57
  19.6 0.7 %collective-permute-done.3 = bf16[128,256]{1,0:T(8,128)(2,1)S(1)} collective-permute-done((bf16[128,256]{1,0:T(8,128)(2,1)}, bf16[128,256]{1,0:T(8,128)(2,1)S(1)}, u32[]{:S(2)}, u32[]{:S(2)}) %collective-permute-start.3) | collective-permute-done | bytes 65568 | tf_op jit(solution)/shard_map/ppermute | solution.py:51
  20.3 0.0 copy-done.5
  20.3 0.0 copy-start.1
  20.3 2.7 %collective-permute-start.4 = (bf16[128,256]{1,0:T(8,128)(2,1)S(1)}, bf16[128,256]{1,0:T(8,128)(2,1)S(1)}, u32[]{:S(2)}, u32[]{:S(2)}) collective-permute-start(bf16[128,256]{1,0:T(8,128)(2,1)S(1)} %add_convert_fusion.5), channel_id=1, source_target_pairs={{0,4},{1,5},{2,6},{3,7},{4,0},{5,1},{6,2},{7,3},{8,12},{9,13},{10,... | collective-permute-start | bytes 196616 | tf_op jit(solution)/shard_map/ppermute | solution.py:57
  23.0 0.0 collective-permute-done.5
  23.0 0.0 copy-done.3
  23.1 1.8 %collective-permute-start.6 = (bf16[128,256]{1,0:T(8,128)(2,1)S(1)}, bf16[128,256]{1,0:T(8,128)(2,1)S(1)}, u32[]{:S(2)}, u32[]{:S(2)}) collective-permute-start(bf16[128,256]{1,0:T(8,128)(2,1)S(1)} %add_convert_fusion.4), channel_id=1, source_target_pairs={{0,6},{1,7},{2,0},{3,1},{4,2},{5,3},{6,4},{7,5},{8,14},{9,15},{10,... | collective-permute-start | bytes 196616 | tf_op jit(solution)/shard_map/ppermute | solution.py:57
  24.9 0.0 collective-permute-done
  24.9 0.0 collective-permute-done.2
  24.9 1.1 %collective-permute-done.4 = bf16[128,256]{1,0:T(8,128)(2,1)S(1)} collective-permute-done((bf16[128,256]{1,0:T(8,128)(2,1)S(1)}, bf16[128,256]{1,0:T(8,128)(2,1)S(1)}, u32[]{:S(2)}, u32[]{:S(2)}) %collective-permute-start.4) | collective-permute-done | bytes 65568 | tf_op jit(solution)/shard_map/ppermute | solution.py:57
  26.0 1.4 %collective-permute-done.6 = bf16[128,256]{1,0:T(8,128)(2,1)S(1)} collective-permute-done((bf16[128,256]{1,0:T(8,128)(2,1)S(1)}, bf16[128,256]{1,0:T(8,128)(2,1)S(1)}, u32[]{:S(2)}, u32[]{:S(2)}) %collective-permute-start.6) | collective-permute-done | bytes 65568 | tf_op jit(solution)/shard_map/ppermute | solution.py:57
  27.4 0.0 copy-done.1
  27.4 0.0 copy-done.7
  27.4 0.2 convolution_convert_fusion
  27.6 6.2 %all-gather.1 = bf16[512,256]{1,0:T(8,128)(2,1)} all-gather(bf16[128,256]{1,0:T(8,128)(2,1)S(1)} %convolution_convert_fusion), channel_id=3, replica_groups=mesh['blk'=4,'rep'=8] {'blk'}, dimensions={0}, use_global_device_ids=true | all-gather | bytes 327680 | tf_op jit(solution)/shard_map/all_gather | solution.py:72
  33.8 2.7 %shard_map.74 = (bf16[128,256]{1,0:T(8,128)(2,1)}, bf16[128,256]{1,0:T(8,128)(2,1)}, bf16[128,256]{1,0:T(8,128)(2,1)}, bf16[128,256]{1,0:T(8,128)(2,1)}, bf16[12...) custom-call(s32[24]{0:T(128)} %bitcast.16, s32[24]{0:T(128)} %bitcast.18, ...), custom_call_target="tpu_custom_call" | custom-call | flops 201326592 | bytes 1572864 | tf_op jit(solution)/shard_map/pallas_call | solution.py:35
  36.5 1.6 %collective-permute-start.8 = (bf16[128,256]{1,0:T(8,128)(2,1)}, bf16[128,256]{1,0:T(8,128)(2,1)S(1)}, u32[]{:S(2)}, u32[]{:S(2)}) collective-permute-start(bf16[128,256]{1,0:T(8,128)(2,1)} %get-tuple-element.32), channel_id=1, source_target_pairs={{0,1},{1,0},{2,3},{3,2},{4,5},{5,4},{6,7},{7,6},{8,9},{9,8},{10,11... | collective-permute-start | bytes 196616 | tf_op jit(solution)/shard_map/ppermute | solution.py:51
  38.0 0.5 collective-permute-start.7
  38.5 1.5 %collective-permute-start.10 = (bf16[128,256]{1,0:T(8,128)(2,1)}, bf16[128,256]{1,0:T(8,128)(2,1)S(1)}, u32[]{:S(2)}, u32[]{:S(2)}) collective-permute-start(bf16[128,256]{1,0:T(8,128)(2,1)} %get-tuple-element.34), channel_id=1, source_target_pairs={{0,1},{1,0},{2,3},{3,2},{4,5},{5,4},{6,7},{7,6},{8,9},{9,8},{10,11... | collective-permute-start | bytes 196616 | tf_op jit(solution)/shard_map/ppermute | solution.py:51
  40.0 0.5 collective-permute-start.12
  40.5 0.7 %collective-permute-done.8 = bf16[128,256]{1,0:T(8,128)(2,1)S(1)} collective-permute-done((bf16[128,256]{1,0:T(8,128)(2,1)}, bf16[128,256]{1,0:T(8,128)(2,1)S(1)}, u32[]{:S(2)}, u32[]{:S(2)}) %collective-permute-start.8) | collective-permute-done | bytes 65568 | tf_op jit(solution)/shard_map/ppermute | solution.py:51
  41.2 0.9 %add_convert_fusion.3 = bf16[128,256]{1,0:T(8,128)(2,1)S(1)} fusion(bf16[128,256]{1,0:T(8,128)(2,1)S(1)} %collective-permute-done.8, bf16[128,256]{1,0:T(8,128)(2,1)} %get-tuple-element.31), kind=kLoop, calls=%fused_computation.5 | loop fusion | flops 131072 | bytes 196608 | tf_op jit(solution)/shard_map/convert_element_type | solution.py:57
  42.1 1.8 %collective-permute-start.9 = (bf16[128,256]{1,0:T(8,128)(2,1)S(1)}, bf16[128,256]{1,0:T(8,128)(2,1)S(1)}, u32[]{:S(2)}, u32[]{:S(2)}) collective-permute-start(bf16[128,256]{1,0:T(8,128)(2,1)S(1)} %add_convert_fusion.3), channel_id=1, source_target_pairs={{0,2},{1,3},{2,4},{3,5},{4,6},{5,7},{6,0},{7,1},{8,10},{9,11},{10,... | collective-permute-start | bytes 196616 | tf_op jit(solution)/shard_map/ppermute | solution.py:57
  43.9 0.6 %collective-permute-done.10 = bf16[128,256]{1,0:T(8,128)(2,1)S(1)} collective-permute-done((bf16[128,256]{1,0:T(8,128)(2,1)}, bf16[128,256]{1,0:T(8,128)(2,1)S(1)}, u32[]{:S(2)}, u32[]{:S(2)}) %collective-permute-start.10) | collective-permute-done | bytes 65568 | tf_op jit(solution)/shard_map/ppermute | solution.py:51
  44.5 0.0 copy-done.4
  44.6 2.3 %collective-permute-start.11 = (bf16[128,256]{1,0:T(8,128)(2,1)S(1)}, bf16[128,256]{1,0:T(8,128)(2,1)S(1)}, u32[]{:S(2)}, u32[]{:S(2)}) collective-permute-start(bf16[128,256]{1,0:T(8,128)(2,1)S(1)} %add_convert_fusion.2), channel_id=1, source_target_pairs={{0,4},{1,5},{2,6},{3,7},{4,0},{5,1},{6,2},{7,3},{8,12},{9,13},{10,... | collective-permute-start | bytes 196616 | tf_op jit(solution)/shard_map/ppermute | solution.py:57
  46.9 0.0 collective-permute-done.12
  46.9 0.0 copy-done.2
  46.9 2.3 %collective-permute-start.13 = (bf16[128,256]{1,0:T(8,128)(2,1)S(1)}, bf16[128,256]{1,0:T(8,128)(2,1)S(1)}, u32[]{:S(2)}, u32[]{:S(2)}) collective-permute-start(bf16[128,256]{1,0:T(8,128)(2,1)S(1)} %add_convert_fusion.1), channel_id=1, source_target_pairs={{0,6},{1,7},{2,0},{3,1},{4,2},{5,3},{6,4},{7,5},{8,14},{9,15},{10,... | collective-permute-start | bytes 196616 | tf_op jit(solution)/shard_map/ppermute | solution.py:57
  49.2 0.0 collective-permute-done.7
  49.2 0.0 collective-permute-done.9
  49.2 0.9 %collective-permute-done.11 = bf16[128,256]{1,0:T(8,128)(2,1)S(1)} collective-permute-done((bf16[128,256]{1,0:T(8,128)(2,1)S(1)}, bf16[128,256]{1,0:T(8,128)(2,1)S(1)}, u32[]{:S(2)}, u32[]{:S(2)}) %collective-permute-start.11) | collective-permute-done | bytes 65568 | tf_op jit(solution)/shard_map/ppermute | solution.py:57
  50.1 1.1 %collective-permute-done.13 = bf16[128,256]{1,0:T(8,128)(2,1)S(1)} collective-permute-done((bf16[128,256]{1,0:T(8,128)(2,1)S(1)}, bf16[128,256]{1,0:T(8,128)(2,1)S(1)}, u32[]{:S(2)}, u32[]{:S(2)}) %collective-permute-start.13) | collective-permute-done | bytes 65568 | tf_op jit(solution)/shard_map/ppermute | solution.py:57
  51.2 0.0 copy-done.6
  51.2 0.7 %add_convert_fusion = bf16[128,256]{1,0:T(8,128)(2,1)} fusion(bf16[128,256]{1,0:T(8,128)(2,1)S(1)} %collective-permute-done.13, bf16[128,256]{1,0:T(8,128)(2,1)S(1)} %collective-permute-done.11, bf16[128,256]{1,0:T(8,128)(2,1)S(1)} %collective-permute-done.9, bf16[128,256]{1,0:T(8,128)(2,1)S(1)} %collective-permute-done.7, bf16[128,256]{1,0:T(8,128)(2,1)S(1)} %copy-done.6), kind=kLoop, calls=%fused_computation.2 | loop fusion | flops 327680 | bytes 393216 | tf_op jit(solution)/shard_map/convert_element_type | solution.py:78
  (9 shorter events, 0.1 us)
Async XLA Ops:
  0.0 0.9 %copy-start = (bf16[256,256]{1,0:T(8,128)(2,1)S(1)}, bf16[256,256]{1,0:T(8,128)(2,1)}, u32[]{:S(2)}) copy-start(bf16[256,256]{1,0:T(8,128)(2,1)} %param.8) | copy-start | bytes 393220
  12.2 4.7 %collective-permute-start.1 = (bf16[128,256]{1,0:T(8,128)(2,1)}, bf16[128,256]{1,0:T(8,128)(2,1)S(1)}, u32[]{:S(2)}, u32[]{:S(2)}) collective-permute-start(bf16[128,256]{1,0:T(8,128)(2,1)} %get-tuple-element.24), channel_id=1, source_target_pairs={{0,1},{1,0},{2,3},{3,2},{4,5},{5,4},{6,7},{7,6},{8,9},{9,8},{10,11... | collective-permute-start | bytes 196616 | tf_op jit(solution)/shard_map/ppermute | solution.py:51
  13.8 11.1 %collective-permute-start = (bf16[128,256]{1,0:T(8,128)(2,1)}, bf16[128,256]{1,0:T(8,128)(2,1)S(1)}, u32[]{:S(2)}, u32[]{:S(2)}) collective-permute-start(bf16[128,256]{1,0:T(8,128)(2,1)} %get-tuple-element.22), channel_id=1, source_target_pairs={{0,1},{1,0},{2,3},{3,2},{4,5},{5,4},{6,7},{7,6},{8,9},{9,8},{10,11... | collective-permute-start | bytes 196616 | tf_op jit(solution)/shard_map/ppermute | solution.py:51
  14.3 6.0 %collective-permute-start.3 = (bf16[128,256]{1,0:T(8,128)(2,1)}, bf16[128,256]{1,0:T(8,128)(2,1)S(1)}, u32[]{:S(2)}, u32[]{:S(2)}) collective-permute-start(bf16[128,256]{1,0:T(8,128)(2,1)} %get-tuple-element.26), channel_id=1, source_target_pairs={{0,1},{1,0},{2,3},{3,2},{4,5},{5,4},{6,7},{7,6},{8,9},{9,8},{10,11... | collective-permute-start | bytes 196616 | tf_op jit(solution)/shard_map/ppermute | solution.py:51
  15.8 7.2 %collective-permute-start.5 = (bf16[128,256]{1,0:T(8,128)(2,1)}, bf16[128,256]{1,0:T(8,128)(2,1)S(1)}, u32[]{:S(2)}, u32[]{:S(2)}) collective-permute-start(bf16[128,256]{1,0:T(8,128)(2,1)} %get-tuple-element.28), channel_id=1, source_target_pairs={{0,1},{1,0},{2,3},{3,2},{4,5},{5,4},{6,7},{7,6},{8,9},{9,8},{10,11... | collective-permute-start | bytes 196616 | tf_op jit(solution)/shard_map/ppermute | solution.py:51
  17.0 3.3 %copy-start.5 = (bf16[128,256]{1,0:T(8,128)(2,1)S(1)}, bf16[128,256]{1,0:T(8,128)(2,1)}, u32[]{:S(2)}) copy-start(bf16[128,256]{1,0:T(8,128)(2,1)} %get-tuple-element.25) | copy-start | bytes 196612
  17.9 7.0 %collective-permute-start.2 = (bf16[128,256]{1,0:T(8,128)(2,1)S(1)}, bf16[128,256]{1,0:T(8,128)(2,1)S(1)}, u32[]{:S(2)}, u32[]{:S(2)}) collective-permute-start(bf16[128,256]{1,0:T(8,128)(2,1)S(1)} %add_convert_fusion.6), channel_id=1, source_target_pairs={{0,2},{1,3},{2,4},{3,5},{4,6},{5,7},{6,0},{7,1},{8,10},{9,11},{10,... | collective-permute-start | bytes 196616 | tf_op jit(solution)/shard_map/ppermute | solution.py:57
  20.3 2.7 %copy-start.3 = (bf16[128,256]{1,0:T(8,128)(2,1)S(1)}, bf16[128,256]{1,0:T(8,128)(2,1)}, u32[]{:S(2)}) copy-start(bf16[128,256]{1,0:T(8,128)(2,1)} %get-tuple-element.27) | copy-start | bytes 196612
  20.3 7.1 %copy-start.1 = (bf16[256,256]{1,0:T(8,128)(2,1)S(1)}, bf16[256,256]{1,0:T(8,128)(2,1)}, u32[]{:S(2)}) copy-start(bf16[256,256]{1,0:T(8,128)(2,1)} %param.9) | copy-start | bytes 393220
  20.3 5.7 %collective-permute-start.4 = (bf16[128,256]{1,0:T(8,128)(2,1)S(1)}, bf16[128,256]{1,0:T(8,128)(2,1)S(1)}, u32[]{:S(2)}, u32[]{:S(2)}) collective-permute-start(bf16[128,256]{1,0:T(8,128)(2,1)S(1)} %add_convert_fusion.5), channel_id=1, source_target_pairs={{0,4},{1,5},{2,6},{3,7},{4,0},{5,1},{6,2},{7,3},{8,12},{9,13},{10,... | collective-permute-start | bytes 196616 | tf_op jit(solution)/shard_map/ppermute | solution.py:57
  23.0 4.3 %copy-start.7 = (bf16[128,256]{1,0:T(8,128)(2,1)S(1)}, bf16[128,256]{1,0:T(8,128)(2,1)}, u32[]{:S(2)}) copy-start(bf16[128,256]{1,0:T(8,128)(2,1)} %get-tuple-element.21) | copy-start | bytes 196612
  23.1 4.3 %collective-permute-start.6 = (bf16[128,256]{1,0:T(8,128)(2,1)S(1)}, bf16[128,256]{1,0:T(8,128)(2,1)S(1)}, u32[]{:S(2)}, u32[]{:S(2)}) collective-permute-start(bf16[128,256]{1,0:T(8,128)(2,1)S(1)} %add_convert_fusion.4), channel_id=1, source_target_pairs={{0,6},{1,7},{2,0},{3,1},{4,2},{5,3},{6,4},{7,5},{8,14},{9,15},{10,... | collective-permute-start | bytes 196616 | tf_op jit(solution)/shard_map/ppermute | solution.py:57
  36.5 4.8 %collective-permute-start.8 = (bf16[128,256]{1,0:T(8,128)(2,1)}, bf16[128,256]{1,0:T(8,128)(2,1)S(1)}, u32[]{:S(2)}, u32[]{:S(2)}) collective-permute-start(bf16[128,256]{1,0:T(8,128)(2,1)} %get-tuple-element.32), channel_id=1, source_target_pairs={{0,1},{1,0},{2,3},{3,2},{4,5},{5,4},{6,7},{7,6},{8,9},{9,8},{10,11... | collective-permute-start | bytes 196616 | tf_op jit(solution)/shard_map/ppermute | solution.py:51
  38.0 11.2 %collective-permute-start.7 = (bf16[128,256]{1,0:T(8,128)(2,1)}, bf16[128,256]{1,0:T(8,128)(2,1)S(1)}, u32[]{:S(2)}, u32[]{:S(2)}) collective-permute-start(bf16[128,256]{1,0:T(8,128)(2,1)} %get-tuple-element.30), channel_id=1, source_target_pairs={{0,1},{1,0},{2,3},{3,2},{4,5},{5,4},{6,7},{7,6},{8,9},{9,8},{10,11... | collective-permute-start | bytes 196616 | tf_op jit(solution)/shard_map/ppermute | solution.py:51
  38.5 6.0 %collective-permute-start.10 = (bf16[128,256]{1,0:T(8,128)(2,1)}, bf16[128,256]{1,0:T(8,128)(2,1)S(1)}, u32[]{:S(2)}, u32[]{:S(2)}) collective-permute-start(bf16[128,256]{1,0:T(8,128)(2,1)} %get-tuple-element.34), channel_id=1, source_target_pairs={{0,1},{1,0},{2,3},{3,2},{4,5},{5,4},{6,7},{7,6},{8,9},{9,8},{10,11... | collective-permute-start | bytes 196616 | tf_op jit(solution)/shard_map/ppermute | solution.py:51
  40.0 6.8 %collective-permute-start.12 = (bf16[128,256]{1,0:T(8,128)(2,1)}, bf16[128,256]{1,0:T(8,128)(2,1)S(1)}, u32[]{:S(2)}, u32[]{:S(2)}) collective-permute-start(bf16[128,256]{1,0:T(8,128)(2,1)} %get-tuple-element.36), channel_id=1, source_target_pairs={{0,1},{1,0},{2,3},{3,2},{4,5},{5,4},{6,7},{7,6},{8,9},{9,8},{10,11... | collective-permute-start | bytes 196616 | tf_op jit(solution)/shard_map/ppermute | solution.py:51
  41.2 3.3 %copy-start.4 = (bf16[128,256]{1,0:T(8,128)(2,1)S(1)}, bf16[128,256]{1,0:T(8,128)(2,1)}, u32[]{:S(2)}) copy-start(bf16[128,256]{1,0:T(8,128)(2,1)} %get-tuple-element.33) | copy-start | bytes 196612
  42.1 7.1 %collective-permute-start.9 = (bf16[128,256]{1,0:T(8,128)(2,1)S(1)}, bf16[128,256]{1,0:T(8,128)(2,1)S(1)}, u32[]{:S(2)}, u32[]{:S(2)}) collective-permute-start(bf16[128,256]{1,0:T(8,128)(2,1)S(1)} %add_convert_fusion.3), channel_id=1, source_target_pairs={{0,2},{1,3},{2,4},{3,5},{4,6},{5,7},{6,0},{7,1},{8,10},{9,11},{10,... | collective-permute-start | bytes 196616 | tf_op jit(solution)/shard_map/ppermute | solution.py:57
  44.6 2.3 %copy-start.2 = (bf16[128,256]{1,0:T(8,128)(2,1)S(1)}, bf16[128,256]{1,0:T(8,128)(2,1)}, u32[]{:S(2)}) copy-start(bf16[128,256]{1,0:T(8,128)(2,1)} %get-tuple-element.35) | copy-start | bytes 196612
  44.6 5.5 %collective-permute-start.11 = (bf16[128,256]{1,0:T(8,128)(2,1)S(1)}, bf16[128,256]{1,0:T(8,128)(2,1)S(1)}, u32[]{:S(2)}, u32[]{:S(2)}) collective-permute-start(bf16[128,256]{1,0:T(8,128)(2,1)S(1)} %add_convert_fusion.2), channel_id=1, source_target_pairs={{0,4},{1,5},{2,6},{3,7},{4,0},{5,1},{6,2},{7,3},{8,12},{9,13},{10,... | collective-permute-start | bytes 196616 | tf_op jit(solution)/shard_map/ppermute | solution.py:57
  46.9 4.4 %copy-start.6 = (bf16[128,256]{1,0:T(8,128)(2,1)S(1)}, bf16[128,256]{1,0:T(8,128)(2,1)}, u32[]{:S(2)}) copy-start(bf16[128,256]{1,0:T(8,128)(2,1)} %get-tuple-element.29) | copy-start | bytes 196612
  46.9 4.3 %collective-permute-start.13 = (bf16[128,256]{1,0:T(8,128)(2,1)S(1)}, bf16[128,256]{1,0:T(8,128)(2,1)S(1)}, u32[]{:S(2)}, u32[]{:S(2)}) collective-permute-start(bf16[128,256]{1,0:T(8,128)(2,1)S(1)} %add_convert_fusion.1), channel_id=1, source_target_pairs={{0,6},{1,7},{2,0},{3,1},{4,2},{5,3},{6,4},{7,5},{8,14},{9,15},{10,... | collective-permute-start | bytes 196616 | tf_op jit(solution)/shard_map/ppermute | solution.py:57

commit v5 on v4

--- a/solution.py
+++ b/solution.py
@@ -46,15 +46,17 @@
     n = lax.axis_size("rep")
     outer = n // 2
     pair = [(src, src ^ 1) for src in range(n)]
+    order = list(range(1, outer)) + [0]
+    got = {t: lax.ppermute(partial[t * 2 + 1], "rep", pair) for t in order}
     total = None
-    for t in range(outer):
-        got = lax.ppermute(partial[t * 2 + 1], "rep", pair)
-        both = partial[t * 2].astype(jnp.float32) + got.astype(jnp.float32)
+    for t in order:
+        both = partial[t * 2].astype(jnp.float32) + got[t].astype(jnp.float32)
         if t == 0:
-            total = both
-            continue
-        perm = [(src, ((src // 2 + t) % outer) * 2 + src % 2) for src in range(n)]
-        total = total + lax.ppermute(both.astype(jnp.bfloat16), "rep", perm).astype(jnp.float32)
+            piece = both
+        else:
+            perm = [(src, ((src // 2 + t) % outer) * 2 + src % 2) for src in range(n)]
+            piece = lax.ppermute(both.astype(jnp.bfloat16), "rep", perm).astype(jnp.float32)
+        total = piece if total is None else total + piece
     return total
 
 

time: 52.3 us -> 51.5 us (0.985)
  starting transfers between devices: 20.7 us -> 19.7 us
    ppermute x6, waiting for transfers between devices: 4.58 us -> 6.03 us  [exchange_rep(): lax.ppermute(both.astype(jnp.bfloat16), 'rep', perm).astype(jnp.float32)]
    ppermute x8, waiting for transfers between devices: 2.7 us -> 1.42 us  [exchange_rep(): got = {t: lax.ppermute(partial[t * 2 + 1], 'rep', pair) for t in order}]
    ppermute x6, starting transfers between devices: 12.6 us -> 11.6 us  [exchange_rep(): lax.ppermute(both.astype(jnp.bfloat16), 'rep', perm).astype(jnp.float32)]
  transfers between devices with their start and end apart: 14 -> 14, of which waited for: 8 -> 9; matrix products, arithmetic and copies ran while one was open for 4% -> 4% of each run, Pallas kernels for 0% -> 0%
where the time goes in v5:
time: 51.5 us; the launch traced here: 51.1 us
  starting transfers between devices  19.7 us (38%)
  blocking collectives  13.9 us (27%)
  waiting for transfers between devices  7.45 us (14%)
  Pallas kernels  5.33 us (10%)
  other arithmetic  2.54 us (5%)
  matrix products  1.17 us (2%)
  between operations  0.76 us (1%)
    all_gather x2, blocking collectives, body(): blocks = lax.all_gather(panel, 'blk', axis=0, tiled=False)  13.9 us
    ppermute x6, starting transfers between devices, exchange_rep(): lax.ppermute(both.astype(jnp.bfloat16), 'rep', perm).astype(jnp.float32)  11.6 us
    ppermute x8, starting transfers between devices, exchange_rep(): got = {t: lax.ppermute(partial[t * 2 + 1], 'rep', pair) for t in order}  8.11 us
    ppermute x6, waiting for transfers between devices, exchange_rep(): lax.ppermute(both.astype(jnp.bfloat16), 'rep', perm).astype(jnp.float32)  6.03 us
    pallas_call x2, Pallas kernels, aggregate(): pl.pallas_call(_agg_kernel, out_shape=[jax.ShapeDtypeStruct((blk, feat),...  5.33 us
    convert_element_type x6, other arithmetic, exchange_rep(): both.astype(jnp.bfloat16)  1.86 us
    ppermute x8, waiting for transfers between devices, exchange_rep(): got = {t: lax.ppermute(partial[t * 2 + 1], 'rep', pair) for t in order}  1.42 us
    dot_general x2, matrix products, body(): jnp.dot(hidden, weight, preferred_element_type=jnp.float32)  1.17 us
  transfers between devices with their start and end apart: 14, of which 9 were waited for; matrix products, arithmetic and copies ran while one was open for 4% of the time, Pallas kernels for 0%

profile of v5, /device:TPU:0, one launch (start us, length us, event | category | flops | bytes accessed | tf_op | source)
XLA Modules:
  0.0 51.1 jit_solution(12147885383265846317)
XLA Ops:
  0.0 0.0 copy-start
  0.7 0.2 copy-done
  0.9 1.0 %convolution_convert_fusion.1 = bf16[128,256]{1,0:T(8,128)(2,1)S(1)} fusion(bf16[128,256]{1,0:T(8,128)(2,1)} %param.7, bf16[256,256]{1,0:T(8,128)(2,1)S(1)} %copy-done), kind=kOutput, calls=%fused_computation.1 | convolution fusion | flops 16809984 | bytes 262144 | tf_op jit(solution)/shard_map/dot_general | solution.py:73
  1.9 7.6 %all-gather = bf16[512,256]{1,0:T(8,128)(2,1)} all-gather(bf16[128,256]{1,0:T(8,128)(2,1)S(1)} %convolution_convert_fusion.1), channel_id=2, replica_groups=mesh['blk'=4,'rep'=8] {'blk'}, dimensions={0}, use_global_device_ids=true | all-gather | bytes 327680 | tf_op jit(solution)/shard_map/all_gather | solution.py:74
  9.6 2.7 %shard_map.73 = (bf16[128,256]{1,0:T(8,128)(2,1)}, bf16[128,256]{1,0:T(8,128)(2,1)}, bf16[128,256]{1,0:T(8,128)(2,1)}, bf16[128,256]{1,0:T(8,128)(2,1)}, bf16[12...) custom-call(s32[24]{0:T(128)} %bitcast.15, s32[24]{0:T(128)} %bitcast.17, ...), custom_call_target="tpu_custom_call" | custom-call | flops 201326592 | bytes 1572864 | tf_op jit(solution)/shard_map/pallas_call | solution.py:35
  12.2 1.6 %collective-permute-start = (bf16[128,256]{1,0:T(8,128)(2,1)}, bf16[128,256]{1,0:T(8,128)(2,1)S(1)}, u32[]{:S(2)}, u32[]{:S(2)}) collective-permute-start(bf16[128,256]{1,0:T(8,128)(2,1)} %get-tuple-element.22), channel_id=1, source_target_pairs={{0,1},{1,0},{2,3},{3,2},{4,5},{5,4},{6,7},{7,6},{8,9},{9,8},{10,11... | collective-permute-start | bytes 196616 | tf_op jit(solution)/shard_map/ppermute | solution.py:50
  13.8 0.5 collective-permute-start.2
  14.3 1.6 %collective-permute-start.4 = (bf16[128,256]{1,0:T(8,128)(2,1)}, bf16[128,256]{1,0:T(8,128)(2,1)S(1)}, u32[]{:S(2)}, u32[]{:S(2)}) collective-permute-start(bf16[128,256]{1,0:T(8,128)(2,1)} %get-tuple-element.26), channel_id=1, source_target_pairs={{0,1},{1,0},{2,3},{3,2},{4,5},{5,4},{6,7},{7,6},{8,9},{9,8},{10,11... | collective-permute-start | bytes 196616 | tf_op jit(solution)/shard_map/ppermute | solution.py:50
  15.8 0.5 collective-permute-start.6
  16.3 0.7 %collective-permute-done = bf16[128,256]{1,0:T(8,128)(2,1)S(1)} collective-permute-done((bf16[128,256]{1,0:T(8,128)(2,1)}, bf16[128,256]{1,0:T(8,128)(2,1)S(1)}, u32[]{:S(2)}, u32[]{:S(2)}) %collective-permute-start) | collective-permute-done | bytes 65568 | tf_op jit(solution)/shard_map/ppermute | solution.py:50
  17.0 0.0 copy-start.5
  17.0 0.9 %add_convert_fusion.6 = bf16[128,256]{1,0:T(8,128)(2,1)S(1)} fusion(bf16[128,256]{1,0:T(8,128)(2,1)S(1)} %collective-permute-done, bf16[128,256]{1,0:T(8,128)(2,1)} %get-tuple-element.21), kind=kLoop, calls=%fused_computation.9 | loop fusion | flops 131072 | bytes 196608 | tf_op jit(solution)/shard_map/convert_element_type | solution.py:58
  17.9 1.7 %collective-permute-start.1 = (bf16[128,256]{1,0:T(8,128)(2,1)S(1)}, bf16[128,256]{1,0:T(8,128)(2,1)S(1)}, u32[]{:S(2)}, u32[]{:S(2)}) collective-permute-start(bf16[128,256]{1,0:T(8,128)(2,1)S(1)} %add_convert_fusion.6), channel_id=1, source_target_pairs={{0,2},{1,3},{2,4},{3,5},{4,6},{5,7},{6,0},{7,1},{8,10},{9,11},{10,... | collective-permute-start | bytes 196616 | tf_op jit(solution)/shard_map/ppermute | solution.py:58
  19.6 0.0 collective-permute-done.2
  19.6 0.0 copy-done.5
  19.6 0.0 copy-start.1
  19.6 2.7 %collective-permute-start.3 = (bf16[128,256]{1,0:T(8,128)(2,1)S(1)}, bf16[128,256]{1,0:T(8,128)(2,1)S(1)}, u32[]{:S(2)}, u32[]{:S(2)}) collective-permute-start(bf16[128,256]{1,0:T(8,128)(2,1)S(1)} %add_convert_fusion.5), channel_id=1, source_target_pairs={{0,4},{1,5},{2,6},{3,7},{4,0},{5,1},{6,2},{7,3},{8,12},{9,13},{10,... | collective-permute-start | bytes 196616 | tf_op jit(solution)/shard_map/ppermute | solution.py:58
  22.3 0.0 collective-permute-done.4
  22.3 0.0 copy-done.3
  22.3 1.7 %collective-permute-start.5 = (bf16[128,256]{1,0:T(8,128)(2,1)S(1)}, bf16[128,256]{1,0:T(8,128)(2,1)S(1)}, u32[]{:S(2)}, u32[]{:S(2)}) collective-permute-start(bf16[128,256]{1,0:T(8,128)(2,1)S(1)} %add_convert_fusion.4), channel_id=1, source_target_pairs={{0,6},{1,7},{2,0},{3,1},{4,2},{5,3},{6,4},{7,5},{8,14},{9,15},{10,... | collective-permute-start | bytes 196616 | tf_op jit(solution)/shard_map/ppermute | solution.py:58
  24.0 0.0 collective-permute-done.6
  24.0 0.7 %collective-permute-done.1 = bf16[128,256]{1,0:T(8,128)(2,1)S(1)} collective-permute-done((bf16[128,256]{1,0:T(8,128)(2,1)S(1)}, bf16[128,256]{1,0:T(8,128)(2,1)S(1)}, u32[]{:S(2)}, u32[]{:S(2)}) %collective-permute-start.1) | collective-permute-done | bytes 65568 | tf_op jit(solution)/shard_map/ppermute | solution.py:58
  24.7 2.1 %collective-permute-done.3 = bf16[128,256]{1,0:T(8,128)(2,1)S(1)} collective-permute-done((bf16[128,256]{1,0:T(8,128)(2,1)S(1)}, bf16[128,256]{1,0:T(8,128)(2,1)S(1)}, u32[]{:S(2)}, u32[]{:S(2)}) %collective-permute-start.3) | collective-permute-done | bytes 65568 | tf_op jit(solution)/shard_map/ppermute | solution.py:58
  26.9 0.1 collective-permute-done.5
  27.0 0.0 copy-done.1
  27.0 0.0 copy-done.7
  27.0 0.2 convolution_convert_fusion
  27.2 6.2 %all-gather.1 = bf16[512,256]{1,0:T(8,128)(2,1)} all-gather(bf16[128,256]{1,0:T(8,128)(2,1)S(1)} %convolution_convert_fusion), channel_id=3, replica_groups=mesh['blk'=4,'rep'=8] {'blk'}, dimensions={0}, use_global_device_ids=true | all-gather | bytes 327680 | tf_op jit(solution)/shard_map/all_gather | solution.py:74
  33.4 2.7 %shard_map.74 = (bf16[128,256]{1,0:T(8,128)(2,1)}, bf16[128,256]{1,0:T(8,128)(2,1)}, bf16[128,256]{1,0:T(8,128)(2,1)}, bf16[128,256]{1,0:T(8,128)(2,1)}, bf16[12...) custom-call(s32[24]{0:T(128)} %bitcast.16, s32[24]{0:T(128)} %bitcast.18, ...), custom_call_target="tpu_custom_call" | custom-call | flops 201326592 | bytes 1572864 | tf_op jit(solution)/shard_map/pallas_call | solution.py:35
  36.1 1.8 %collective-permute-start.7 = (bf16[128,256]{1,0:T(8,128)(2,1)}, bf16[128,256]{1,0:T(8,128)(2,1)S(1)}, u32[]{:S(2)}, u32[]{:S(2)}) collective-permute-start(bf16[128,256]{1,0:T(8,128)(2,1)} %get-tuple-element.30), channel_id=1, source_target_pairs={{0,1},{1,0},{2,3},{3,2},{4,5},{5,4},{6,7},{7,6},{8,9},{9,8},{10,11... | collective-permute-start | bytes 196616 | tf_op jit(solution)/shard_map/ppermute | solution.py:50
  37.9 0.2 collective-permute-start.9
  38.1 1.8 %collective-permute-start.11 = (bf16[128,256]{1,0:T(8,128)(2,1)}, bf16[128,256]{1,0:T(8,128)(2,1)S(1)}, u32[]{:S(2)}, u32[]{:S(2)}) collective-permute-start(bf16[128,256]{1,0:T(8,128)(2,1)} %get-tuple-element.34), channel_id=1, source_target_pairs={{0,1},{1,0},{2,3},{3,2},{4,5},{5,4},{6,7},{7,6},{8,9},{9,8},{10,11... | collective-permute-start | bytes 196616 | tf_op jit(solution)/shard_map/ppermute | solution.py:50
  39.9 0.2 collective-permute-start.13
  40.1 0.6 %collective-permute-done.7 = bf16[128,256]{1,0:T(8,128)(2,1)S(1)} collective-permute-done((bf16[128,256]{1,0:T(8,128)(2,1)}, bf16[128,256]{1,0:T(8,128)(2,1)S(1)}, u32[]{:S(2)}, u32[]{:S(2)}) %collective-permute-start.7) | collective-permute-done | bytes 65568 | tf_op jit(solution)/shard_map/ppermute | solution.py:50
  40.7 0.9 %add_convert_fusion.3 = bf16[128,256]{1,0:T(8,128)(2,1)S(1)} fusion(bf16[128,256]{1,0:T(8,128)(2,1)S(1)} %collective-permute-done.7, bf16[128,256]{1,0:T(8,128)(2,1)} %get-tuple-element.29), kind=kLoop, calls=%fused_computation.5 | loop fusion | flops 131072 | bytes 196608 | tf_op jit(solution)/shard_map/convert_element_type | solution.py:58
  41.6 1.3 %collective-permute-start.8 = (bf16[128,256]{1,0:T(8,128)(2,1)S(1)}, bf16[128,256]{1,0:T(8,128)(2,1)S(1)}, u32[]{:S(2)}, u32[]{:S(2)}) collective-permute-start(bf16[128,256]{1,0:T(8,128)(2,1)S(1)} %add_convert_fusion.3), channel_id=1, source_target_pairs={{0,2},{1,3},{2,4},{3,5},{4,6},{5,7},{6,0},{7,1},{8,10},{9,11},{10,... | collective-permute-start | bytes 196616 | tf_op jit(solution)/shard_map/ppermute | solution.py:58
  42.8 0.2 collective-permute-done.9
  43.0 0.0 copy-done.4
  43.0 2.5 %collective-permute-start.10 = (bf16[128,256]{1,0:T(8,128)(2,1)S(1)}, bf16[128,256]{1,0:T(8,128)(2,1)S(1)}, u32[]{:S(2)}, u32[]{:S(2)}) collective-permute-start(bf16[128,256]{1,0:T(8,128)(2,1)S(1)} %add_convert_fusion.2), channel_id=1, source_target_pairs={{0,4},{1,5},{2,6},{3,7},{4,0},{5,1},{6,2},{7,3},{8,12},{9,13},{10,... | collective-permute-start | bytes 196616 | tf_op jit(solution)/shard_map/ppermute | solution.py:58
  45.5 0.0 collective-permute-done.11
  45.5 0.0 copy-done.2
  45.6 1.8 %collective-permute-start.12 = (bf16[128,256]{1,0:T(8,128)(2,1)S(1)}, bf16[128,256]{1,0:T(8,128)(2,1)S(1)}, u32[]{:S(2)}, u32[]{:S(2)}) collective-permute-start(bf16[128,256]{1,0:T(8,128)(2,1)S(1)} %add_convert_fusion.1), channel_id=1, source_target_pairs={{0,6},{1,7},{2,0},{3,1},{4,2},{5,3},{6,4},{7,5},{8,14},{9,15},{10,... | collective-permute-start | bytes 196616 | tf_op jit(solution)/shard_map/ppermute | solution.py:58
  47.3 0.0 collective-permute-done.13
  47.3 1.0 %collective-permute-done.8 = bf16[128,256]{1,0:T(8,128)(2,1)S(1)} collective-permute-done((bf16[128,256]{1,0:T(8,128)(2,1)S(1)}, bf16[128,256]{1,0:T(8,128)(2,1)S(1)}, u32[]{:S(2)}, u32[]{:S(2)}) %collective-permute-start.8) | collective-permute-done | bytes 65568 | tf_op jit(solution)/shard_map/ppermute | solution.py:58
  48.3 1.7 %collective-permute-done.10 = bf16[128,256]{1,0:T(8,128)(2,1)S(1)} collective-permute-done((bf16[128,256]{1,0:T(8,128)(2,1)S(1)}, bf16[128,256]{1,0:T(8,128)(2,1)S(1)}, u32[]{:S(2)}, u32[]{:S(2)}) %collective-permute-start.10) | collective-permute-done | bytes 65568 | tf_op jit(solution)/shard_map/ppermute | solution.py:58
  50.0 0.4 collective-permute-done.12
  50.4 0.0 copy-done.6
  50.4 0.7 %add_convert_fusion = bf16[128,256]{1,0:T(8,128)(2,1)} fusion(bf16[128,256]{1,0:T(8,128)(2,1)S(1)} %collective-permute-done.13, bf16[128,256]{1,0:T(8,128)(2,1)S(1)} %copy-done.6, bf16[128,256]{1,0:T(8,128)(2,1)S(1)} %collective-permute-done.12, bf16[128,256]{1,0:T(8,128)(2,1)S(1)} %collective-permute-done.10, bf16[128,256]{1,0:T(8,128)(2,1)S(1)} %collective-permute-done.8), kind=kLoop, calls=%fused_computation.2 | loop fusion | flops 327680 | bytes 393216 | tf_op jit(solution)/shard_map/convert_element_type | solution.py:80
  (9 shorter events, 0.1 us)
Async XLA Ops:
  0.0 0.9 %copy-start = (bf16[256,256]{1,0:T(8,128)(2,1)S(1)}, bf16[256,256]{1,0:T(8,128)(2,1)}, u32[]{:S(2)}) copy-start(bf16[256,256]{1,0:T(8,128)(2,1)} %param.8) | copy-start | bytes 393220
  12.2 4.7 %collective-permute-start = (bf16[128,256]{1,0:T(8,128)(2,1)}, bf16[128,256]{1,0:T(8,128)(2,1)S(1)}, u32[]{:S(2)}, u32[]{:S(2)}) collective-permute-start(bf16[128,256]{1,0:T(8,128)(2,1)} %get-tuple-element.22), channel_id=1, source_target_pairs={{0,1},{1,0},{2,3},{3,2},{4,5},{5,4},{6,7},{7,6},{8,9},{9,8},{10,11... | collective-permute-start | bytes 196616 | tf_op jit(solution)/shard_map/ppermute | solution.py:50
  13.8 5.8 %collective-permute-start.2 = (bf16[128,256]{1,0:T(8,128)(2,1)}, bf16[128,256]{1,0:T(8,128)(2,1)S(1)}, u32[]{:S(2)}, u32[]{:S(2)}) collective-permute-start(bf16[128,256]{1,0:T(8,128)(2,1)} %get-tuple-element.24), channel_id=1, source_target_pairs={{0,1},{1,0},{2,3},{3,2},{4,5},{5,4},{6,7},{7,6},{8,9},{9,8},{10,11... | collective-permute-start | bytes 196616 | tf_op jit(solution)/shard_map/ppermute | solution.py:50
  14.3 8.0 %collective-permute-start.4 = (bf16[128,256]{1,0:T(8,128)(2,1)}, bf16[128,256]{1,0:T(8,128)(2,1)S(1)}, u32[]{:S(2)}, u32[]{:S(2)}) collective-permute-start(bf16[128,256]{1,0:T(8,128)(2,1)} %get-tuple-element.26), channel_id=1, source_target_pairs={{0,1},{1,0},{2,3},{3,2},{4,5},{5,4},{6,7},{7,6},{8,9},{9,8},{10,11... | collective-permute-start | bytes 196616 | tf_op jit(solution)/shard_map/ppermute | solution.py:50
  15.8 8.2 %collective-permute-start.6 = (bf16[128,256]{1,0:T(8,128)(2,1)}, bf16[128,256]{1,0:T(8,128)(2,1)S(1)}, u32[]{:S(2)}, u32[]{:S(2)}) collective-permute-start(bf16[128,256]{1,0:T(8,128)(2,1)} %get-tuple-element.28), channel_id=1, source_target_pairs={{0,1},{1,0},{2,3},{3,2},{4,5},{5,4},{6,7},{7,6},{8,9},{9,8},{10,11... | collective-permute-start | bytes 196616 | tf_op jit(solution)/shard_map/ppermute | solution.py:50
  17.0 2.6 %copy-start.5 = (bf16[128,256]{1,0:T(8,128)(2,1)S(1)}, bf16[128,256]{1,0:T(8,128)(2,1)}, u32[]{:S(2)}) copy-start(bf16[128,256]{1,0:T(8,128)(2,1)} %get-tuple-element.23) | copy-start | bytes 196612
  17.9 6.9 %collective-permute-start.1 = (bf16[128,256]{1,0:T(8,128)(2,1)S(1)}, bf16[128,256]{1,0:T(8,128)(2,1)S(1)}, u32[]{:S(2)}, u32[]{:S(2)}) collective-permute-start(bf16[128,256]{1,0:T(8,128)(2,1)S(1)} %add_convert_fusion.6), channel_id=1, source_target_pairs={{0,2},{1,3},{2,4},{3,5},{4,6},{5,7},{6,0},{7,1},{8,10},{9,11},{10,... | collective-permute-start | bytes 196616 | tf_op jit(solution)/shard_map/ppermute | solution.py:58
  19.6 2.7 %copy-start.3 = (bf16[128,256]{1,0:T(8,128)(2,1)S(1)}, bf16[128,256]{1,0:T(8,128)(2,1)}, u32[]{:S(2)}) copy-start(bf16[128,256]{1,0:T(8,128)(2,1)} %get-tuple-element.25) | copy-start | bytes 196612
  19.6 7.4 %copy-start.1 = (bf16[256,256]{1,0:T(8,128)(2,1)S(1)}, bf16[256,256]{1,0:T(8,128)(2,1)}, u32[]{:S(2)}) copy-start(bf16[256,256]{1,0:T(8,128)(2,1)} %param.9) | copy-start | bytes 393220
  19.6 7.2 %collective-permute-start.3 = (bf16[128,256]{1,0:T(8,128)(2,1)S(1)}, bf16[128,256]{1,0:T(8,128)(2,1)S(1)}, u32[]{:S(2)}, u32[]{:S(2)}) collective-permute-start(bf16[128,256]{1,0:T(8,128)(2,1)S(1)} %add_convert_fusion.5), channel_id=1, source_target_pairs={{0,4},{1,5},{2,6},{3,7},{4,0},{5,1},{6,2},{7,3},{8,12},{9,13},{10,... | collective-permute-start | bytes 196616 | tf_op jit(solution)/shard_map/ppermute | solution.py:58
  22.3 4.7 %copy-start.7 = (bf16[128,256]{1,0:T(8,128)(2,1)S(1)}, bf16[128,256]{1,0:T(8,128)(2,1)}, u32[]{:S(2)}) copy-start(bf16[128,256]{1,0:T(8,128)(2,1)} %get-tuple-element.27) | copy-start | bytes 196612
  22.3 4.7 %collective-permute-start.5 = (bf16[128,256]{1,0:T(8,128)(2,1)S(1)}, bf16[128,256]{1,0:T(8,128)(2,1)S(1)}, u32[]{:S(2)}, u32[]{:S(2)}) collective-permute-start(bf16[128,256]{1,0:T(8,128)(2,1)S(1)} %add_convert_fusion.4), channel_id=1, source_target_pairs={{0,6},{1,7},{2,0},{3,1},{4,2},{5,3},{6,4},{7,5},{8,14},{9,15},{10,... | collective-permute-start | bytes 196616 | tf_op jit(solution)/shard_map/ppermute | solution.py:58
  36.1 4.6 %collective-permute-start.7 = (bf16[128,256]{1,0:T(8,128)(2,1)}, bf16[128,256]{1,0:T(8,128)(2,1)S(1)}, u32[]{:S(2)}, u32[]{:S(2)}) collective-permute-start(bf16[128,256]{1,0:T(8,128)(2,1)} %get-tuple-element.30), channel_id=1, source_target_pairs={{0,1},{1,0},{2,3},{3,2},{4,5},{5,4},{6,7},{7,6},{8,9},{9,8},{10,11... | collective-permute-start | bytes 196616 | tf_op jit(solution)/shard_map/ppermute | solution.py:50
  37.9 5.2 %collective-permute-start.9 = (bf16[128,256]{1,0:T(8,128)(2,1)}, bf16[128,256]{1,0:T(8,128)(2,1)S(1)}, u32[]{:S(2)}, u32[]{:S(2)}) collective-permute-start(bf16[128,256]{1,0:T(8,128)(2,1)} %get-tuple-element.32), channel_id=1, source_target_pairs={{0,1},{1,0},{2,3},{3,2},{4,5},{5,4},{6,7},{7,6},{8,9},{9,8},{10,11... | collective-permute-start | bytes 196616 | tf_op jit(solution)/shard_map/ppermute | solution.py:50
  38.1 7.5 %collective-permute-start.11 = (bf16[128,256]{1,0:T(8,128)(2,1)}, bf16[128,256]{1,0:T(8,128)(2,1)S(1)}, u32[]{:S(2)}, u32[]{:S(2)}) collective-permute-start(bf16[128,256]{1,0:T(8,128)(2,1)} %get-tuple-element.34), channel_id=1, source_target_pairs={{0,1},{1,0},{2,3},{3,2},{4,5},{5,4},{6,7},{7,6},{8,9},{9,8},{10,11... | collective-permute-start | bytes 196616 | tf_op jit(solution)/shard_map/ppermute | solution.py:50
  39.9 7.4 %collective-permute-start.13 = (bf16[128,256]{1,0:T(8,128)(2,1)}, bf16[128,256]{1,0:T(8,128)(2,1)S(1)}, u32[]{:S(2)}, u32[]{:S(2)}) collective-permute-start(bf16[128,256]{1,0:T(8,128)(2,1)} %get-tuple-element.36), channel_id=1, source_target_pairs={{0,1},{1,0},{2,3},{3,2},{4,5},{5,4},{6,7},{7,6},{8,9},{9,8},{10,11... | collective-permute-start | bytes 196616 | tf_op jit(solution)/shard_map/ppermute | solution.py:50
  40.7 2.3 %copy-start.4 = (bf16[128,256]{1,0:T(8,128)(2,1)S(1)}, bf16[128,256]{1,0:T(8,128)(2,1)}, u32[]{:S(2)}) copy-start(bf16[128,256]{1,0:T(8,128)(2,1)} %get-tuple-element.31) | copy-start | bytes 196612
  41.6 6.7 %collective-permute-start.8 = (bf16[128,256]{1,0:T(8,128)(2,1)S(1)}, bf16[128,256]{1,0:T(8,128)(2,1)S(1)}, u32[]{:S(2)}, u32[]{:S(2)}) collective-permute-start(bf16[128,256]{1,0:T(8,128)(2,1)S(1)} %add_convert_fusion.3), channel_id=1, source_target_pairs={{0,2},{1,3},{2,4},{3,5},{4,6},{5,7},{6,0},{7,1},{8,10},{9,11},{10,... | collective-permute-start | bytes 196616 | tf_op jit(solution)/shard_map/ppermute | solution.py:58
  43.0 2.5 %copy-start.2 = (bf16[128,256]{1,0:T(8,128)(2,1)S(1)}, bf16[128,256]{1,0:T(8,128)(2,1)}, u32[]{:S(2)}) copy-start(bf16[128,256]{1,0:T(8,128)(2,1)} %get-tuple-element.33) | copy-start | bytes 196612
  43.0 7.0 %collective-permute-start.10 = (bf16[128,256]{1,0:T(8,128)(2,1)S(1)}, bf16[128,256]{1,0:T(8,128)(2,1)S(1)}, u32[]{:S(2)}, u32[]{:S(2)}) collective-permute-start(bf16[128,256]{1,0:T(8,128)(2,1)S(1)} %add_convert_fusion.2), channel_id=1, source_target_pairs={{0,4},{1,5},{2,6},{3,7},{4,0},{5,1},{6,2},{7,3},{8,12},{9,13},{10,... | collective-permute-start | bytes 196616 | tf_op jit(solution)/shard_map/ppermute | solution.py:58
  45.5 4.9 %copy-start.6 = (bf16[128,256]{1,0:T(8,128)(2,1)S(1)}, bf16[128,256]{1,0:T(8,128)(2,1)}, u32[]{:S(2)}) copy-start(bf16[128,256]{1,0:T(8,128)(2,1)} %get-tuple-element.35) | copy-start | bytes 196612
  45.6 4.9 %collective-permute-start.12 = (bf16[128,256]{1,0:T(8,128)(2,1)S(1)}, bf16[128,256]{1,0:T(8,128)(2,1)S(1)}, u32[]{:S(2)}, u32[]{:S(2)}) collective-permute-start(bf16[128,256]{1,0:T(8,128)(2,1)S(1)} %add_convert_fusion.1), channel_id=1, source_target_pairs={{0,6},{1,7},{2,0},{3,1},{4,2},{5,3},{6,4},{7,5},{8,14},{9,15},{10,... | collective-permute-start | bytes 196616 | tf_op jit(solution)/shard_map/ppermute | solution.py:58

commit v6 on v5

--- a/solution.py
+++ b/solution.py
@@ -34,7 +34,7 @@
     nbytes = 2 * (panel_blocks.size + tile_vals.size + n_rows * blk * feat)
     return pl.pallas_call(
         _agg_kernel,
-        out_shape=[jax.ShapeDtypeStruct((blk, feat), jnp.bfloat16) for _ in range(n_rows)],
+        out_shape=[pltpu.VMEM((blk, feat), jnp.bfloat16) for _ in range(n_rows)],
         in_specs=[smem, smem, smem, vmem, vmem],
         out_specs=[vmem] * n_rows,
         scratch_shapes=[pltpu.VMEM((n_rows + 1, blk, feat), jnp.float32)],

time: 51.5 us -> 48.7 us (0.946)
  starting transfers between devices: 19.7 us -> 21.6 us
  other arithmetic: 2.54 us -> 0.78 us
  waiting for transfers between devices: 7.45 us -> 6.06 us
  Pallas kernels: 5.33 us -> 3.95 us
    ppermute x6, starting transfers between devices: 11.6 us -> 13.4 us  [exchange_rep(): lax.ppermute(both.astype(jnp.bfloat16), 'rep', perm).astype(jnp.float32)]
    convert_element_type x6, other arithmetic: 1.86 us -> 0.11 us  [exchange_rep(): both.astype(jnp.bfloat16)]
    ppermute x6, waiting for transfers between devices: 6.03 us -> 4.47 us  [exchange_rep(): lax.ppermute(both.astype(jnp.bfloat16), 'rep', perm).astype(jnp.float32)]
    pallas_call x2, Pallas kernels: 5.33 us -> 3.95 us  [aggregate(): pl.pallas_call(_agg_kernel, out_shape=[pltpu.VMEM((blk, feat), jnp.bfloat...]
  transfers between devices with their start and end apart: 14 -> 14, of which waited for: 9 -> 8; matrix products, arithmetic and copies ran while one was open for 4% -> 0% of each run, Pallas kernels for 0% -> 0%
where the time goes in v6:
time: 48.7 us; the launch traced here: 48.5 us
  starting transfers between devices  21.6 us (44%)
  blocking collectives  13.9 us (29%)
  waiting for transfers between devices  6.06 us (12%)
  Pallas kernels  3.95 us (8%)
  matrix products  1.18 us (2%)
  other arithmetic  0.78 us (2%)
  between operations  0.77 us (2%)
    all_gather x2, blocking collectives, body(): blocks = lax.all_gather(panel, 'blk', axis=0, tiled=False)  13.9 us
    ppermute x6, starting transfers between devices, exchange_rep(): lax.ppermute(both.astype(jnp.bfloat16), 'rep', perm).astype(jnp.float32)  13.4 us
    ppermute x8, starting transfers between devices, exchange_rep(): got = {t: lax.ppermute(partial[t * 2 + 1], 'rep', pair) for t in order}  8.23 us
    ppermute x6, waiting for transfers between devices, exchange_rep(): lax.ppermute(both.astype(jnp.bfloat16), 'rep', perm).astype(jnp.float32)  4.47 us
    pallas_call x2, Pallas kernels, aggregate(): pl.pallas_call(_agg_kernel, out_shape=[pltpu.VMEM((blk, feat), jnp.bfloat...  3.95 us
    ppermute x8, waiting for transfers between devices, exchange_rep(): got = {t: lax.ppermute(partial[t * 2 + 1], 'rep', pair) for t in order}  1.59 us
    dot_general x2, matrix products, body(): jnp.dot(hidden, weight, preferred_element_type=jnp.float32)  1.18 us
  transfers between devices with their start and end apart: 14, of which 8 were waited for; matrix products, arithmetic and copies ran while one was open for 0% of the time, Pallas kernels for 0%

profile of v6, /device:TPU:0, one launch (start us, length us, event | category | flops | bytes accessed | tf_op | source)
XLA Modules:
  0.0 48.5 jit_solution(7840272790175294840)
XLA Ops:
  0.0 0.0 copy-start
  0.7 0.2 copy-done
  0.9 1.0 %convolution_convert_fusion.1 = bf16[128,256]{1,0:T(8,128)(2,1)S(1)} fusion(bf16[128,256]{1,0:T(8,128)(2,1)} %param.7, bf16[256,256]{1,0:T(8,128)(2,1)S(1)} %copy-done), kind=kOutput, calls=%fused_computation.1 | convolution fusion | flops 16809984 | bytes 262144 | tf_op jit(solution)/shard_map/dot_general | solution.py:73
  1.9 7.6 %all-gather = bf16[512,256]{1,0:T(8,128)(2,1)} all-gather(bf16[128,256]{1,0:T(8,128)(2,1)S(1)} %convolution_convert_fusion.1), channel_id=2, replica_groups=mesh['blk'=4,'rep'=8] {'blk'}, dimensions={0}, use_global_device_ids=true | all-gather | bytes 327680 | tf_op jit(solution)/shard_map/all_gather | solution.py:74
  9.6 2.0 %shard_map.73 = (bf16[128,256]{1,0:T(8,128)(2,1)S(1)}, bf16[128,256]{1,0:T(8,128)(2,1)S(1)}, bf16[128,256]{1,0:T(8,128)(2,1)S(1)}, bf16[128,256]{1,0:T(8,128)(2,...) custom-call(s32[24]{0:T(128)} %bitcast.15, ...), custom_call_target="tpu_custom_call" | custom-call | flops 201326592 | bytes 1572864 | tf_op jit(solution)/shard_map/pallas_call | solution.py:35
  11.5 1.6 %collective-permute-start = (bf16[128,256]{1,0:T(8,128)(2,1)S(1)}, bf16[128,256]{1,0:T(8,128)(2,1)S(1)}, u32[]{:S(2)}, u32[]{:S(2)}) collective-permute-start(bf16[128,256]{1,0:T(8,128)(2,1)S(1)} %get-tuple-element.22), channel_id=1, source_target_pairs={{0,1},{1,0},{2,3},{3,2},{4,5},{5,4},{6,7},{7,6},{8,9},{9,8},{10,11... | collective-permute-start | bytes 196616 | tf_op jit(solution)/shard_map/ppermute | solution.py:50
  13.2 0.5 collective-permute-start.2
  13.6 1.6 %collective-permute-start.4 = (bf16[128,256]{1,0:T(8,128)(2,1)S(1)}, bf16[128,256]{1,0:T(8,128)(2,1)S(1)}, u32[]{:S(2)}, u32[]{:S(2)}) collective-permute-start(bf16[128,256]{1,0:T(8,128)(2,1)S(1)} %get-tuple-element.26), channel_id=1, source_target_pairs={{0,1},{1,0},{2,3},{3,2},{4,5},{5,4},{6,7},{7,6},{8,9},{9,8},{10,11... | collective-permute-start | bytes 196616 | tf_op jit(solution)/shard_map/ppermute | solution.py:50
  15.2 0.5 collective-permute-start.6
  15.7 0.5 collective-permute-done
  16.2 1.7 %collective-permute-start.1 = (bf16[128,256]{1,0:T(8,128)(2,1)S(1)}, bf16[128,256]{1,0:T(8,128)(2,1)S(1)}, u32[]{:S(2)}, u32[]{:S(2)}) collective-permute-start(bf16[128,256]{1,0:T(8,128)(2,1)S(1)} %add_convert_fusion.6), channel_id=1, source_target_pairs={{0,2},{1,3},{2,4},{3,5},{4,6},{5,7},{6,0},{7,1},{8,10},{9,11},{10,... | collective-permute-start | bytes 196616 | tf_op jit(solution)/shard_map/ppermute | solution.py:58
  17.9 0.3 collective-permute-done.2
  18.1 0.0 copy-start.1
  18.2 2.7 %collective-permute-start.3 = (bf16[128,256]{1,0:T(8,128)(2,1)S(1)}, bf16[128,256]{1,0:T(8,128)(2,1)S(1)}, u32[]{:S(2)}, u32[]{:S(2)}) collective-permute-start(bf16[128,256]{1,0:T(8,128)(2,1)S(1)} %add_convert_fusion.5), channel_id=1, source_target_pairs={{0,4},{1,5},{2,6},{3,7},{4,0},{5,1},{6,2},{7,3},{8,12},{9,13},{10,... | collective-permute-start | bytes 196616 | tf_op jit(solution)/shard_map/ppermute | solution.py:58
  20.8 0.0 collective-permute-done.4
  20.8 2.3 %collective-permute-start.5 = (bf16[128,256]{1,0:T(8,128)(2,1)S(1)}, bf16[128,256]{1,0:T(8,128)(2,1)S(1)}, u32[]{:S(2)}, u32[]{:S(2)}) collective-permute-start(bf16[128,256]{1,0:T(8,128)(2,1)S(1)} %add_convert_fusion.4), channel_id=1, source_target_pairs={{0,6},{1,7},{2,0},{3,1},{4,2},{5,3},{6,4},{7,5},{8,14},{9,15},{10,... | collective-permute-start | bytes 196616 | tf_op jit(solution)/shard_map/ppermute | solution.py:58
  23.2 0.0 collective-permute-done.6
  23.2 0.0 collective-permute-done.1
  23.2 1.8 %collective-permute-done.3 = bf16[128,256]{1,0:T(8,128)(2,1)S(1)} collective-permute-done((bf16[128,256]{1,0:T(8,128)(2,1)S(1)}, bf16[128,256]{1,0:T(8,128)(2,1)S(1)}, u32[]{:S(2)}, u32[]{:S(2)}) %collective-permute-start.3) | collective-permute-done | bytes 65568 | tf_op jit(solution)/shard_map/ppermute | solution.py:58
  25.0 0.4 collective-permute-done.5
  25.4 0.0 copy-done.1
  25.4 0.2 convolution_convert_fusion
  25.6 6.2 %all-gather.1 = bf16[512,256]{1,0:T(8,128)(2,1)} all-gather(bf16[128,256]{1,0:T(8,128)(2,1)S(1)} %convolution_convert_fusion), channel_id=3, replica_groups=mesh['blk'=4,'rep'=8] {'blk'}, dimensions={0}, use_global_device_ids=true | all-gather | bytes 327680 | tf_op jit(solution)/shard_map/all_gather | solution.py:74
  31.9 2.0 %shard_map.74 = (bf16[128,256]{1,0:T(8,128)(2,1)S(1)}, bf16[128,256]{1,0:T(8,128)(2,1)S(1)}, bf16[128,256]{1,0:T(8,128)(2,1)S(1)}, bf16[128,256]{1,0:T(8,128)(2,...) custom-call(s32[24]{0:T(128)} %bitcast.16, ...), custom_call_target="tpu_custom_call" | custom-call | flops 201326592 | bytes 1572864 | tf_op jit(solution)/shard_map/pallas_call | solution.py:35
  33.8 1.6 %collective-permute-start.7 = (bf16[128,256]{1,0:T(8,128)(2,1)S(1)}, bf16[128,256]{1,0:T(8,128)(2,1)S(1)}, u32[]{:S(2)}, u32[]{:S(2)}) collective-permute-start(bf16[128,256]{1,0:T(8,128)(2,1)S(1)} %get-tuple-element.30), channel_id=1, source_target_pairs={{0,1},{1,0},{2,3},{3,2},{4,5},{5,4},{6,7},{7,6},{8,9},{9,8},{10,11... | collective-permute-start | bytes 196616 | tf_op jit(solution)/shard_map/ppermute | solution.py:50
  35.5 0.5 collective-permute-start.9
  35.9 1.6 %collective-permute-start.11 = (bf16[128,256]{1,0:T(8,128)(2,1)S(1)}, bf16[128,256]{1,0:T(8,128)(2,1)S(1)}, u32[]{:S(2)}, u32[]{:S(2)}) collective-permute-start(bf16[128,256]{1,0:T(8,128)(2,1)S(1)} %get-tuple-element.34), channel_id=1, source_target_pairs={{0,1},{1,0},{2,3},{3,2},{4,5},{5,4},{6,7},{7,6},{8,9},{9,8},{10,11... | collective-permute-start | bytes 196616 | tf_op jit(solution)/shard_map/ppermute | solution.py:50
  37.5 0.5 collective-permute-start.13
  38.0 0.5 collective-permute-done.7
  38.5 1.6 %collective-permute-start.8 = (bf16[128,256]{1,0:T(8,128)(2,1)S(1)}, bf16[128,256]{1,0:T(8,128)(2,1)S(1)}, u32[]{:S(2)}, u32[]{:S(2)}) collective-permute-start(bf16[128,256]{1,0:T(8,128)(2,1)S(1)} %add_convert_fusion.3), channel_id=1, source_target_pairs={{0,2},{1,3},{2,4},{3,5},{4,6},{5,7},{6,0},{7,1},{8,10},{9,11},{10,... | collective-permute-start | bytes 196616 | tf_op jit(solution)/shard_map/ppermute | solution.py:58
  40.0 0.4 collective-permute-done.9
  40.4 2.8 %collective-permute-start.10 = (bf16[128,256]{1,0:T(8,128)(2,1)S(1)}, bf16[128,256]{1,0:T(8,128)(2,1)S(1)}, u32[]{:S(2)}, u32[]{:S(2)}) collective-permute-start(bf16[128,256]{1,0:T(8,128)(2,1)S(1)} %add_convert_fusion.2), channel_id=1, source_target_pairs={{0,4},{1,5},{2,6},{3,7},{4,0},{5,1},{6,2},{7,3},{8,12},{9,13},{10,... | collective-permute-start | bytes 196616 | tf_op jit(solution)/shard_map/ppermute | solution.py:58
  43.2 0.0 collective-permute-done.11
  43.2 2.3 %collective-permute-start.12 = (bf16[128,256]{1,0:T(8,128)(2,1)S(1)}, bf16[128,256]{1,0:T(8,128)(2,1)S(1)}, u32[]{:S(2)}, u32[]{:S(2)}) collective-permute-start(bf16[128,256]{1,0:T(8,128)(2,1)S(1)} %add_convert_fusion.1), channel_id=1, source_target_pairs={{0,6},{1,7},{2,0},{3,1},{4,2},{5,3},{6,4},{7,5},{8,14},{9,15},{10,... | collective-permute-start | bytes 196616 | tf_op jit(solution)/shard_map/ppermute | solution.py:58
  45.6 0.0 collective-permute-done.13
  45.6 0.0 collective-permute-done.8
  45.6 1.8 %collective-permute-done.10 = bf16[128,256]{1,0:T(8,128)(2,1)S(1)} collective-permute-done((bf16[128,256]{1,0:T(8,128)(2,1)S(1)}, bf16[128,256]{1,0:T(8,128)(2,1)S(1)}, u32[]{:S(2)}, u32[]{:S(2)}) %collective-permute-start.10) | collective-permute-done | bytes 65568 | tf_op jit(solution)/shard_map/ppermute | solution.py:58
  47.3 0.4 collective-permute-done.12
  47.8 0.7 %add_convert_fusion = bf16[128,256]{1,0:T(8,128)(2,1)} fusion(bf16[128,256]{1,0:T(8,128)(2,1)S(1)} %collective-permute-done.13, bf16[128,256]{1,0:T(8,128)(2,1)S(1)} %get-tuple-element.35, bf16[128,256]{1,0:T(8,128)(2,1)S(1)} %collective-permute-done.12, bf16[128,256]{1,0:T(8,128)(2,1)S(1)} %collective-permute-done.10, ...), kind=kLoop, calls=%fused_computation.2 | loop fusion | flops 327680 | bytes 393216 | tf_op jit(solution)/shard_map/convert_element_type | solution.py:80
  (6 shorter events, 0.1 us)
Async XLA Ops:
  0.0 0.9 %copy-start = (bf16[256,256]{1,0:T(8,128)(2,1)S(1)}, bf16[256,256]{1,0:T(8,128)(2,1)}, u32[]{:S(2)}) copy-start(bf16[256,256]{1,0:T(8,128)(2,1)} %param.8) | copy-start | bytes 393220
  11.5 4.6 %collective-permute-start = (bf16[128,256]{1,0:T(8,128)(2,1)S(1)}, bf16[128,256]{1,0:T(8,128)(2,1)S(1)}, u32[]{:S(2)}, u32[]{:S(2)}) collective-permute-start(bf16[128,256]{1,0:T(8,128)(2,1)S(1)} %get-tuple-element.22), channel_id=1, source_target_pairs={{0,1},{1,0},{2,3},{3,2},{4,5},{5,4},{6,7},{7,6},{8,9},{9,8},{10,11... | collective-permute-start | bytes 196616 | tf_op jit(solution)/shard_map/ppermute | solution.py:50
  13.2 5.0 %collective-permute-start.2 = (bf16[128,256]{1,0:T(8,128)(2,1)S(1)}, bf16[128,256]{1,0:T(8,128)(2,1)S(1)}, u32[]{:S(2)}, u32[]{:S(2)}) collective-permute-start(bf16[128,256]{1,0:T(8,128)(2,1)S(1)} %get-tuple-element.24), channel_id=1, source_target_pairs={{0,1},{1,0},{2,3},{3,2},{4,5},{5,4},{6,7},{7,6},{8,9},{9,8},{10,11... | collective-permute-start | bytes 196616 | tf_op jit(solution)/shard_map/ppermute | solution.py:50
  13.6 7.2 %collective-permute-start.4 = (bf16[128,256]{1,0:T(8,128)(2,1)S(1)}, bf16[128,256]{1,0:T(8,128)(2,1)S(1)}, u32[]{:S(2)}, u32[]{:S(2)}) collective-permute-start(bf16[128,256]{1,0:T(8,128)(2,1)S(1)} %get-tuple-element.26), channel_id=1, source_target_pairs={{0,1},{1,0},{2,3},{3,2},{4,5},{5,4},{6,7},{7,6},{8,9},{9,8},{10,11... | collective-permute-start | bytes 196616 | tf_op jit(solution)/shard_map/ppermute | solution.py:50
  15.2 8.0 %collective-permute-start.6 = (bf16[128,256]{1,0:T(8,128)(2,1)S(1)}, bf16[128,256]{1,0:T(8,128)(2,1)S(1)}, u32[]{:S(2)}, u32[]{:S(2)}) collective-permute-start(bf16[128,256]{1,0:T(8,128)(2,1)S(1)} %get-tuple-element.28), channel_id=1, source_target_pairs={{0,1},{1,0},{2,3},{3,2},{4,5},{5,4},{6,7},{7,6},{8,9},{9,8},{10,11... | collective-permute-start | bytes 196616 | tf_op jit(solution)/shard_map/ppermute | solution.py:50
  16.2 7.0 %collective-permute-start.1 = (bf16[128,256]{1,0:T(8,128)(2,1)S(1)}, bf16[128,256]{1,0:T(8,128)(2,1)S(1)}, u32[]{:S(2)}, u32[]{:S(2)}) collective-permute-start(bf16[128,256]{1,0:T(8,128)(2,1)S(1)} %add_convert_fusion.6), channel_id=1, source_target_pairs={{0,2},{1,3},{2,4},{3,5},{4,6},{5,7},{6,0},{7,1},{8,10},{9,11},{10,... | collective-permute-start | bytes 196616 | tf_op jit(solution)/shard_map/ppermute | solution.py:58
  18.1 7.3 %copy-start.1 = (bf16[256,256]{1,0:T(8,128)(2,1)S(1)}, bf16[256,256]{1,0:T(8,128)(2,1)}, u32[]{:S(2)}) copy-start(bf16[256,256]{1,0:T(8,128)(2,1)} %param.9) | copy-start | bytes 393220
  18.2 6.9 %collective-permute-start.3 = (bf16[128,256]{1,0:T(8,128)(2,1)S(1)}, bf16[128,256]{1,0:T(8,128)(2,1)S(1)}, u32[]{:S(2)}, u32[]{:S(2)}) collective-permute-start(bf16[128,256]{1,0:T(8,128)(2,1)S(1)} %add_convert_fusion.5), channel_id=1, source_target_pairs={{0,4},{1,5},{2,6},{3,7},{4,0},{5,1},{6,2},{7,3},{8,12},{9,13},{10,... | collective-permute-start | bytes 196616 | tf_op jit(solution)/shard_map/ppermute | solution.py:58
  20.8 4.6 %collective-permute-start.5 = (bf16[128,256]{1,0:T(8,128)(2,1)S(1)}, bf16[128,256]{1,0:T(8,128)(2,1)S(1)}, u32[]{:S(2)}, u32[]{:S(2)}) collective-permute-start(bf16[128,256]{1,0:T(8,128)(2,1)S(1)} %add_convert_fusion.4), channel_id=1, source_target_pairs={{0,6},{1,7},{2,0},{3,1},{4,2},{5,3},{6,4},{7,5},{8,14},{9,15},{10,... | collective-permute-start | bytes 196616 | tf_op jit(solution)/shard_map/ppermute | solution.py:58
  33.8 4.6 %collective-permute-start.7 = (bf16[128,256]{1,0:T(8,128)(2,1)S(1)}, bf16[128,256]{1,0:T(8,128)(2,1)S(1)}, u32[]{:S(2)}, u32[]{:S(2)}) collective-permute-start(bf16[128,256]{1,0:T(8,128)(2,1)S(1)} %get-tuple-element.30), channel_id=1, source_target_pairs={{0,1},{1,0},{2,3},{3,2},{4,5},{5,4},{6,7},{7,6},{8,9},{9,8},{10,11... | collective-permute-start | bytes 196616 | tf_op jit(solution)/shard_map/ppermute | solution.py:50
  35.5 5.0 %collective-permute-start.9 = (bf16[128,256]{1,0:T(8,128)(2,1)S(1)}, bf16[128,256]{1,0:T(8,128)(2,1)S(1)}, u32[]{:S(2)}, u32[]{:S(2)}) collective-permute-start(bf16[128,256]{1,0:T(8,128)(2,1)S(1)} %get-tuple-element.32), channel_id=1, source_target_pairs={{0,1},{1,0},{2,3},{3,2},{4,5},{5,4},{6,7},{7,6},{8,9},{9,8},{10,11... | collective-permute-start | bytes 196616 | tf_op jit(solution)/shard_map/ppermute | solution.py:50
  35.9 7.3 %collective-permute-start.11 = (bf16[128,256]{1,0:T(8,128)(2,1)S(1)}, bf16[128,256]{1,0:T(8,128)(2,1)S(1)}, u32[]{:S(2)}, u32[]{:S(2)}) collective-permute-start(bf16[128,256]{1,0:T(8,128)(2,1)S(1)} %get-tuple-element.34), channel_id=1, source_target_pairs={{0,1},{1,0},{2,3},{3,2},{4,5},{5,4},{6,7},{7,6},{8,9},{9,8},{10,11... | collective-permute-start | bytes 196616 | tf_op jit(solution)/shard_map/ppermute | solution.py:50
  37.5 8.1 %collective-permute-start.13 = (bf16[128,256]{1,0:T(8,128)(2,1)S(1)}, bf16[128,256]{1,0:T(8,128)(2,1)S(1)}, u32[]{:S(2)}, u32[]{:S(2)}) collective-permute-start(bf16[128,256]{1,0:T(8,128)(2,1)S(1)} %get-tuple-element.36), channel_id=1, source_target_pairs={{0,1},{1,0},{2,3},{3,2},{4,5},{5,4},{6,7},{7,6},{8,9},{9,8},{10,11... | collective-permute-start | bytes 196616 | tf_op jit(solution)/shard_map/ppermute | solution.py:50
  38.5 7.1 %collective-permute-start.8 = (bf16[128,256]{1,0:T(8,128)(2,1)S(1)}, bf16[128,256]{1,0:T(8,128)(2,1)S(1)}, u32[]{:S(2)}, u32[]{:S(2)}) collective-permute-start(bf16[128,256]{1,0:T(8,128)(2,1)S(1)} %add_convert_fusion.3), channel_id=1, source_target_pairs={{0,2},{1,3},{2,4},{3,5},{4,6},{5,7},{6,0},{7,1},{8,10},{9,11},{10,... | collective-permute-start | bytes 196616 | tf_op jit(solution)/shard_map/ppermute | solution.py:58
  40.4 6.9 %collective-permute-start.10 = (bf16[128,256]{1,0:T(8,128)(2,1)S(1)}, bf16[128,256]{1,0:T(8,128)(2,1)S(1)}, u32[]{:S(2)}, u32[]{:S(2)}) collective-permute-start(bf16[128,256]{1,0:T(8,128)(2,1)S(1)} %add_convert_fusion.2), channel_id=1, source_target_pairs={{0,4},{1,5},{2,6},{3,7},{4,0},{5,1},{6,2},{7,3},{8,12},{9,13},{10,... | collective-permute-start | bytes 196616 | tf_op jit(solution)/shard_map/ppermute | solution.py:58
  43.2 4.6 %collective-permute-start.12 = (bf16[128,256]{1,0:T(8,128)(2,1)S(1)}, bf16[128,256]{1,0:T(8,128)(2,1)S(1)}, u32[]{:S(2)}, u32[]{:S(2)}) collective-permute-start(bf16[128,256]{1,0:T(8,128)(2,1)S(1)} %add_convert_fusion.1), channel_id=1, source_target_pairs={{0,6},{1,7},{2,0},{3,1},{4,2},{5,3},{6,4},{7,5},{8,14},{9,15},{10,... | collective-permute-start | bytes 196616 | tf_op jit(solution)/shard_map/ppermute | solution.py:58

commit v7 on v6

--- a/solution.py
+++ b/solution.py
@@ -39,7 +39,19 @@
         out_specs=[vmem] * n_rows,
         scratch_shapes=[pltpu.VMEM((n_rows + 1, blk, feat), jnp.float32)],
         cost_estimate=pl.CostEstimate(flops=flops, bytes_accessed=nbytes, transcendentals=0),
-    )(tile_row, tile_col, live_count.reshape(1), panel_blocks, tile_vals)
+    )(tile_row, tile_col, live_count.reshape(1), *on_chip(panel_blocks, tile_vals, n_rows))
+
+
+def on_chip(panel_blocks, tile_vals, n_rows):
+    blk, feat = panel_blocks.shape[1:]
+    footprint = 2 * (panel_blocks.size + tile_vals.size) + (2 + 4) * n_rows * blk * feat
+    if footprint > 4 * 2**20:
+        return panel_blocks, tile_vals
+    vmem = pltpu.MemorySpace.VMEM
+    return (
+        pltpu.with_memory_space_constraint(panel_blocks, vmem),
+        pltpu.with_memory_space_constraint(tile_vals, vmem),
+    )
 
 
 def exchange_rep(partial):

time: 48.7 us -> 47.9 us (0.984)
  local copies, waits for them, and re-layouts: 0.24 us -> 1.37 us
  Pallas kernels: 3.95 us -> 2.93 us
  blocking collectives: 13.9 us -> 13 us
    unnamed x4 -> x8, local copies, waits for them, and re-layouts: 0.24 us -> 1.37 us
    pallas_call x2, Pallas kernels: 3.95 us -> 2.93 us  [aggregate(): pl.pallas_call(_agg_kernel, out_shape=[pltpu.VMEM((blk, feat), jnp.bfloat...]
    all_gather x2, blocking collectives: 13.9 us -> 13 us  [body(): blocks = lax.all_gather(panel, 'blk', axis=0, tiled=False)]
where the time goes in v7:
time: 47.9 us; the launch traced here: 47.7 us
  starting transfers between devices  21.6 us (45%)
  blocking collectives  13 us (27%)
  waiting for transfers between devices  6.04 us (13%)
  Pallas kernels  2.93 us (6%)
  local copies, waits for them, and re-layouts  1.37 us (3%)
  matrix products  1.17 us (2%)
  other arithmetic  0.78 us (2%)
  between operations  0.77 us (2%)
    ppermute x6, starting transfers between devices, exchange_rep(): lax.ppermute(both.astype(jnp.bfloat16), 'rep', perm).astype(jnp.float32)  13.4 us
    all_gather x2, blocking collectives, body(): blocks = lax.all_gather(panel, 'blk', axis=0, tiled=False)  13 us
    ppermute x8, starting transfers between devices, exchange_rep(): got = {t: lax.ppermute(partial[t * 2 + 1], 'rep', pair) for t in order}  8.23 us
    ppermute x6, waiting for transfers between devices, exchange_rep(): lax.ppermute(both.astype(jnp.bfloat16), 'rep', perm).astype(jnp.float32)  4.46 us
    pallas_call x2, Pallas kernels, aggregate(): pl.pallas_call(_agg_kernel, out_shape=[pltpu.VMEM((blk, feat), jnp.bfloat...  2.93 us
    ppermute x8, waiting for transfers between devices, exchange_rep(): got = {t: lax.ppermute(partial[t * 2 + 1], 'rep', pair) for t in order}  1.58 us
    unnamed x8, local copies, waits for them, and re-layouts  1.37 us
    dot_general x2, matrix products, body(): jnp.dot(hidden, weight, preferred_element_type=jnp.float32)  1.17 us
  transfers between devices with their start and end apart: 14, of which 8 were waited for; matrix products, arithmetic and copies ran while one was open for 0% of the time, Pallas kernels for 0%

profile of v7, /device:TPU:0, one launch (start us, length us, event | category | flops | bytes accessed | tf_op | source)
XLA Modules:
  0.0 47.7 jit_solution(10457964405121054642)
XLA Ops:
  0.0 0.0 copy-start
  0.7 0.2 copy-done
  0.9 1.0 %convolution_convert_fusion.1 = bf16[128,256]{1,0:T(8,128)(2,1)S(1)} fusion(bf16[128,256]{1,0:T(8,128)(2,1)} %param.7, bf16[256,256]{1,0:T(8,128)(2,1)S(1)} %copy-done), kind=kOutput, calls=%fused_computation.1 | convolution fusion | flops 16809984 | bytes 262144 | tf_op jit(solution)/shard_map/dot_general | solution.py:85
  1.9 7.2 %all-gather = bf16[512,256]{1,0:T(8,128)(2,1)S(1)} all-gather(bf16[128,256]{1,0:T(8,128)(2,1)S(1)} %convolution_convert_fusion.1), channel_id=2, replica_groups=mesh['blk'=4,'rep'=8] {'blk'}, dimensions={0}, use_global_device_ids=true | all-gather | bytes 327680 | tf_op jit(solution)/shard_map/all_gather | solution.py:86
  9.1 0.0 copy-start.1
  9.1 1.1 %copy-done.1 = bf16[1,1,24,128,128]{4,3,2,1,0:T(8,128)(2,1)S(1)} copy-done((bf16[1,1,24,128,128]{4,3,2,1,0:T(8,128)(2,1)S(1)}, bf16[1,1,24,128,128]{4,3,2,1,0:T(8,128)(2,1)}, u32[]{:S(2)}) %copy-start.1) | copy-done | bytes 786456
  10.3 0.0 copy-start.3
  10.3 1.5 %shard_map.73 = (bf16[128,256]{1,0:T(8,128)(2,1)S(1)}, bf16[128,256]{1,0:T(8,128)(2,1)S(1)}, bf16[128,256]{1,0:T(8,128)(2,1)S(1)}, bf16[128,256]{1,0:T(8,128)(2,...) custom-call(s32[24]{0:T(128)} %bitcast.15, ...), custom_call_target="tpu_custom_call" | custom-call | flops 201326592 | bytes 1572864 | tf_op jit(solution)/shard_map/pallas_call | solution.py:35
  11.8 0.0 copy-start.2
  11.8 1.6 %collective-permute-start = (bf16[128,256]{1,0:T(8,128)(2,1)S(1)}, bf16[128,256]{1,0:T(8,128)(2,1)S(1)}, u32[]{:S(2)}, u32[]{:S(2)}) collective-permute-start(bf16[128,256]{1,0:T(8,128)(2,1)S(1)} %get-tuple-element.22), channel_id=1, source_target_pairs={{0,1},{1,0},{2,3},{3,2},{4,5},{5,4},{6,7},{7,6},{8,9},{9,8},{10,11... | collective-permute-start | bytes 196616 | tf_op jit(solution)/shard_map/ppermute | solution.py:62
  13.4 0.5 collective-permute-start.2
  13.9 1.6 %collective-permute-start.4 = (bf16[128,256]{1,0:T(8,128)(2,1)S(1)}, bf16[128,256]{1,0:T(8,128)(2,1)S(1)}, u32[]{:S(2)}, u32[]{:S(2)}) collective-permute-start(bf16[128,256]{1,0:T(8,128)(2,1)S(1)} %get-tuple-element.26), channel_id=1, source_target_pairs={{0,1},{1,0},{2,3},{3,2},{4,5},{5,4},{6,7},{7,6},{8,9},{9,8},{10,11... | collective-permute-start | bytes 196616 | tf_op jit(solution)/shard_map/ppermute | solution.py:62
  15.5 0.5 collective-permute-start.6
  15.9 0.5 collective-permute-done
  16.4 1.7 %collective-permute-start.1 = (bf16[128,256]{1,0:T(8,128)(2,1)S(1)}, bf16[128,256]{1,0:T(8,128)(2,1)S(1)}, u32[]{:S(2)}, u32[]{:S(2)}) collective-permute-start(bf16[128,256]{1,0:T(8,128)(2,1)S(1)} %add_convert_fusion.6), channel_id=1, source_target_pairs={{0,2},{1,3},{2,4},{3,5},{4,6},{5,7},{6,0},{7,1},{8,10},{9,11},{10,... | collective-permute-start | bytes 196616 | tf_op jit(solution)/shard_map/ppermute | solution.py:70
  18.1 0.2 collective-permute-done.2
  18.4 2.7 %collective-permute-start.3 = (bf16[128,256]{1,0:T(8,128)(2,1)S(1)}, bf16[128,256]{1,0:T(8,128)(2,1)S(1)}, u32[]{:S(2)}, u32[]{:S(2)}) collective-permute-start(bf16[128,256]{1,0:T(8,128)(2,1)S(1)} %add_convert_fusion.5), channel_id=1, source_target_pairs={{0,4},{1,5},{2,6},{3,7},{4,0},{5,1},{6,2},{7,3},{8,12},{9,13},{10,... | collective-permute-start | bytes 196616 | tf_op jit(solution)/shard_map/ppermute | solution.py:70
  21.1 0.0 collective-permute-done.4
  21.1 2.4 %collective-permute-start.5 = (bf16[128,256]{1,0:T(8,128)(2,1)S(1)}, bf16[128,256]{1,0:T(8,128)(2,1)S(1)}, u32[]{:S(2)}, u32[]{:S(2)}) collective-permute-start(bf16[128,256]{1,0:T(8,128)(2,1)S(1)} %add_convert_fusion.4), channel_id=1, source_target_pairs={{0,6},{1,7},{2,0},{3,1},{4,2},{5,3},{6,4},{7,5},{8,14},{9,15},{10,... | collective-permute-start | bytes 196616 | tf_op jit(solution)/shard_map/ppermute | solution.py:70
  23.4 0.0 collective-permute-done.6
  23.4 0.0 collective-permute-done.1
  23.4 1.8 %collective-permute-done.3 = bf16[128,256]{1,0:T(8,128)(2,1)S(1)} collective-permute-done((bf16[128,256]{1,0:T(8,128)(2,1)S(1)}, bf16[128,256]{1,0:T(8,128)(2,1)S(1)}, u32[]{:S(2)}, u32[]{:S(2)}) %collective-permute-start.3) | collective-permute-done | bytes 65568 | tf_op jit(solution)/shard_map/ppermute | solution.py:70
  25.3 0.4 collective-permute-done.5
  25.7 0.0 copy-done.3
  25.7 0.2 convolution_convert_fusion
  25.9 5.8 %all-gather.1 = bf16[512,256]{1,0:T(8,128)(2,1)S(1)} all-gather(bf16[128,256]{1,0:T(8,128)(2,1)S(1)} %convolution_convert_fusion), channel_id=3, replica_groups=mesh['blk'=4,'rep'=8] {'blk'}, dimensions={0}, use_global_device_ids=true | all-gather | bytes 327680 | tf_op jit(solution)/shard_map/all_gather | solution.py:86
  31.7 0.0 copy-done.2
  31.7 1.4 %shard_map.74 = (bf16[128,256]{1,0:T(8,128)(2,1)S(1)}, bf16[128,256]{1,0:T(8,128)(2,1)S(1)}, bf16[128,256]{1,0:T(8,128)(2,1)S(1)}, bf16[128,256]{1,0:T(8,128)(2,...) custom-call(s32[24]{0:T(128)} %bitcast.16, ...), custom_call_target="tpu_custom_call" | custom-call | flops 201326592 | bytes 1572864 | tf_op jit(solution)/shard_map/pallas_call | solution.py:35
  33.1 1.6 %collective-permute-start.7 = (bf16[128,256]{1,0:T(8,128)(2,1)S(1)}, bf16[128,256]{1,0:T(8,128)(2,1)S(1)}, u32[]{:S(2)}, u32[]{:S(2)}) collective-permute-start(bf16[128,256]{1,0:T(8,128)(2,1)S(1)} %get-tuple-element.30), channel_id=1, source_target_pairs={{0,1},{1,0},{2,3},{3,2},{4,5},{5,4},{6,7},{7,6},{8,9},{9,8},{10,11... | collective-permute-start | bytes 196616 | tf_op jit(solution)/shard_map/ppermute | solution.py:62
  34.7 0.5 %collective-permute-start.9 = (bf16[128,256]{1,0:T(8,128)(2,1)S(1)}, bf16[128,256]{1,0:T(8,128)(2,1)S(1)}, u32[]{:S(2)}, u32[]{:S(2)}) collective-permute-start(bf16[128,256]{1,0:T(8,128)(2,1)S(1)} %get-tuple-element.32), channel_id=1, source_target_pairs={{0,1},{1,0},{2,3},{3,2},{4,5},{5,4},{6,7},{7,6},{8,9},{9,8},{10,11... | collective-permute-start | bytes 196616 | tf_op jit(solution)/shard_map/ppermute | solution.py:62
  35.2 1.5 %collective-permute-start.11 = (bf16[128,256]{1,0:T(8,128)(2,1)S(1)}, bf16[128,256]{1,0:T(8,128)(2,1)S(1)}, u32[]{:S(2)}, u32[]{:S(2)}) collective-permute-start(bf16[128,256]{1,0:T(8,128)(2,1)S(1)} %get-tuple-element.34), channel_id=1, source_target_pairs={{0,1},{1,0},{2,3},{3,2},{4,5},{5,4},{6,7},{7,6},{8,9},{9,8},{10,11... | collective-permute-start | bytes 196616 | tf_op jit(solution)/shard_map/ppermute | solution.py:62
  36.7 0.5 %collective-permute-start.13 = (bf16[128,256]{1,0:T(8,128)(2,1)S(1)}, bf16[128,256]{1,0:T(8,128)(2,1)S(1)}, u32[]{:S(2)}, u32[]{:S(2)}) collective-permute-start(bf16[128,256]{1,0:T(8,128)(2,1)S(1)} %get-tuple-element.36), channel_id=1, source_target_pairs={{0,1},{1,0},{2,3},{3,2},{4,5},{5,4},{6,7},{7,6},{8,9},{9,8},{10,11... | collective-permute-start | bytes 196616 | tf_op jit(solution)/shard_map/ppermute | solution.py:62
  37.2 0.5 %collective-permute-done.7 = bf16[128,256]{1,0:T(8,128)(2,1)S(1)} collective-permute-done((bf16[128,256]{1,0:T(8,128)(2,1)S(1)}, bf16[128,256]{1,0:T(8,128)(2,1)S(1)}, u32[]{:S(2)}, u32[]{:S(2)}) %collective-permute-start.7) | collective-permute-done | bytes 65568 | tf_op jit(solution)/shard_map/ppermute | solution.py:62
  37.7 1.6 %collective-permute-start.8 = (bf16[128,256]{1,0:T(8,128)(2,1)S(1)}, bf16[128,256]{1,0:T(8,128)(2,1)S(1)}, u32[]{:S(2)}, u32[]{:S(2)}) collective-permute-start(bf16[128,256]{1,0:T(8,128)(2,1)S(1)} %add_convert_fusion.3), channel_id=1, source_target_pairs={{0,2},{1,3},{2,4},{3,5},{4,6},{5,7},{6,0},{7,1},{8,10},{9,11},{10,... | collective-permute-start | bytes 196616 | tf_op jit(solution)/shard_map/ppermute | solution.py:70
  39.3 0.4 collective-permute-done.9
  39.6 2.8 %collective-permute-start.10 = (bf16[128,256]{1,0:T(8,128)(2,1)S(1)}, bf16[128,256]{1,0:T(8,128)(2,1)S(1)}, u32[]{:S(2)}, u32[]{:S(2)}) collective-permute-start(bf16[128,256]{1,0:T(8,128)(2,1)S(1)} %add_convert_fusion.2), channel_id=1, source_target_pairs={{0,4},{1,5},{2,6},{3,7},{4,0},{5,1},{6,2},{7,3},{8,12},{9,13},{10,... | collective-permute-start | bytes 196616 | tf_op jit(solution)/shard_map/ppermute | solution.py:70
  42.4 0.0 collective-permute-done.11
  42.4 2.3 %collective-permute-start.12 = (bf16[128,256]{1,0:T(8,128)(2,1)S(1)}, bf16[128,256]{1,0:T(8,128)(2,1)S(1)}, u32[]{:S(2)}, u32[]{:S(2)}) collective-permute-start(bf16[128,256]{1,0:T(8,128)(2,1)S(1)} %add_convert_fusion.1), channel_id=1, source_target_pairs={{0,6},{1,7},{2,0},{3,1},{4,2},{5,3},{6,4},{7,5},{8,14},{9,15},{10,... | collective-permute-start | bytes 196616 | tf_op jit(solution)/shard_map/ppermute | solution.py:70
  44.8 0.0 collective-permute-done.13
  44.8 0.0 collective-permute-done.8
  44.8 1.8 %collective-permute-done.10 = bf16[128,256]{1,0:T(8,128)(2,1)S(1)} collective-permute-done((bf16[128,256]{1,0:T(8,128)(2,1)S(1)}, bf16[128,256]{1,0:T(8,128)(2,1)S(1)}, u32[]{:S(2)}, u32[]{:S(2)}) %collective-permute-start.10) | collective-permute-done | bytes 65568 | tf_op jit(solution)/shard_map/ppermute | solution.py:70
  46.6 0.4 collective-permute-done.12
  47.0 0.7 %add_convert_fusion = bf16[128,256]{1,0:T(8,128)(2,1)} fusion(bf16[128,256]{1,0:T(8,128)(2,1)S(1)} %collective-permute-done.13, bf16[128,256]{1,0:T(8,128)(2,1)S(1)} %get-tuple-element.35, bf16[128,256]{1,0:T(8,128)(2,1)S(1)} %collective-permute-done.12, bf16[128,256]{1,0:T(8,128)(2,1)S(1)} %collective-permute-done.10, ...), kind=kLoop, calls=%fused_computation.2 | loop fusion | flops 327680 | bytes 393216 | tf_op jit(solution)/shard_map/convert_element_type | solution.py:92
  (6 shorter events, 0.1 us)
Async XLA Ops:
  0.0 0.9 %copy-start = (bf16[256,256]{1,0:T(8,128)(2,1)S(1)}, bf16[256,256]{1,0:T(8,128)(2,1)}, u32[]{:S(2)}) copy-start(bf16[256,256]{1,0:T(8,128)(2,1)} %param.8) | copy-start | bytes 393220
  9.1 1.1 %copy-start.1 = (bf16[1,1,24,128,128]{4,3,2,1,0:T(8,128)(2,1)S(1)}, bf16[1,1,24,128,128]{4,3,2,1,0:T(8,128)(2,1)}, u32[]{:S(2)}) copy-start(bf16[1,1,24,128,128]{4,3,2,1,0:T(8,128)(2,1)} %param.10) | copy-start | bytes 2359300
  10.3 15.4 %copy-start.3 = (bf16[256,256]{1,0:T(8,128)(2,1)S(1)}, bf16[256,256]{1,0:T(8,128)(2,1)}, u32[]{:S(2)}) copy-start(bf16[256,256]{1,0:T(8,128)(2,1)} %param.9) | copy-start | bytes 393220
  11.8 19.9 %copy-start.2 = (bf16[1,1,24,128,128]{4,3,2,1,0:T(8,128)(2,1)S(1)}, bf16[1,1,24,128,128]{4,3,2,1,0:T(8,128)(2,1)}, u32[]{:S(2)}) copy-start(bf16[1,1,24,128,128]{4,3,2,1,0:T(8,128)(2,1)} %param.10) | copy-start | bytes 2359300
  11.8 4.6 %collective-permute-start = (bf16[128,256]{1,0:T(8,128)(2,1)S(1)}, bf16[128,256]{1,0:T(8,128)(2,1)S(1)}, u32[]{:S(2)}, u32[]{:S(2)}) collective-permute-start(bf16[128,256]{1,0:T(8,128)(2,1)S(1)} %get-tuple-element.22), channel_id=1, source_target_pairs={{0,1},{1,0},{2,3},{3,2},{4,5},{5,4},{6,7},{7,6},{8,9},{9,8},{10,11... | collective-permute-start | bytes 196616 | tf_op jit(solution)/shard_map/ppermute | solution.py:62
  13.4 4.9 %collective-permute-start.2 = (bf16[128,256]{1,0:T(8,128)(2,1)S(1)}, bf16[128,256]{1,0:T(8,128)(2,1)S(1)}, u32[]{:S(2)}, u32[]{:S(2)}) collective-permute-start(bf16[128,256]{1,0:T(8,128)(2,1)S(1)} %get-tuple-element.24), channel_id=1, source_target_pairs={{0,1},{1,0},{2,3},{3,2},{4,5},{5,4},{6,7},{7,6},{8,9},{9,8},{10,11... | collective-permute-start | bytes 196616 | tf_op jit(solution)/shard_map/ppermute | solution.py:62
  13.9 7.2 %collective-permute-start.4 = (bf16[128,256]{1,0:T(8,128)(2,1)S(1)}, bf16[128,256]{1,0:T(8,128)(2,1)S(1)}, u32[]{:S(2)}, u32[]{:S(2)}) collective-permute-start(bf16[128,256]{1,0:T(8,128)(2,1)S(1)} %get-tuple-element.26), channel_id=1, source_target_pairs={{0,1},{1,0},{2,3},{3,2},{4,5},{5,4},{6,7},{7,6},{8,9},{9,8},{10,11... | collective-permute-start | bytes 196616 | tf_op jit(solution)/shard_map/ppermute | solution.py:62
  15.5 8.0 %collective-permute-start.6 = (bf16[128,256]{1,0:T(8,128)(2,1)S(1)}, bf16[128,256]{1,0:T(8,128)(2,1)S(1)}, u32[]{:S(2)}, u32[]{:S(2)}) collective-permute-start(bf16[128,256]{1,0:T(8,128)(2,1)S(1)} %get-tuple-element.28), channel_id=1, source_target_pairs={{0,1},{1,0},{2,3},{3,2},{4,5},{5,4},{6,7},{7,6},{8,9},{9,8},{10,11... | collective-permute-start | bytes 196616 | tf_op jit(solution)/shard_map/ppermute | solution.py:62
  16.4 7.0 %collective-permute-start.1 = (bf16[128,256]{1,0:T(8,128)(2,1)S(1)}, bf16[128,256]{1,0:T(8,128)(2,1)S(1)}, u32[]{:S(2)}, u32[]{:S(2)}) collective-permute-start(bf16[128,256]{1,0:T(8,128)(2,1)S(1)} %add_convert_fusion.6), channel_id=1, source_target_pairs={{0,2},{1,3},{2,4},{3,5},{4,6},{5,7},{6,0},{7,1},{8,10},{9,11},{10,... | collective-permute-start | bytes 196616 | tf_op jit(solution)/shard_map/ppermute | solution.py:70
  18.4 6.9 %collective-permute-start.3 = (bf16[128,256]{1,0:T(8,128)(2,1)S(1)}, bf16[128,256]{1,0:T(8,128)(2,1)S(1)}, u32[]{:S(2)}, u32[]{:S(2)}) collective-permute-start(bf16[128,256]{1,0:T(8,128)(2,1)S(1)} %add_convert_fusion.5), channel_id=1, source_target_pairs={{0,4},{1,5},{2,6},{3,7},{4,0},{5,1},{6,2},{7,3},{8,12},{9,13},{10,... | collective-permute-start | bytes 196616 | tf_op jit(solution)/shard_map/ppermute | solution.py:70
  21.1 4.6 %collective-permute-start.5 = (bf16[128,256]{1,0:T(8,128)(2,1)S(1)}, bf16[128,256]{1,0:T(8,128)(2,1)S(1)}, u32[]{:S(2)}, u32[]{:S(2)}) collective-permute-start(bf16[128,256]{1,0:T(8,128)(2,1)S(1)} %add_convert_fusion.4), channel_id=1, source_target_pairs={{0,6},{1,7},{2,0},{3,1},{4,2},{5,3},{6,4},{7,5},{8,14},{9,15},{10,... | collective-permute-start | bytes 196616 | tf_op jit(solution)/shard_map/ppermute | solution.py:70
  33.1 4.6 %collective-permute-start.7 = (bf16[128,256]{1,0:T(8,128)(2,1)S(1)}, bf16[128,256]{1,0:T(8,128)(2,1)S(1)}, u32[]{:S(2)}, u32[]{:S(2)}) collective-permute-start(bf16[128,256]{1,0:T(8,128)(2,1)S(1)} %get-tuple-element.30), channel_id=1, source_target_pairs={{0,1},{1,0},{2,3},{3,2},{4,5},{5,4},{6,7},{7,6},{8,9},{9,8},{10,11... | collective-permute-start | bytes 196616 | tf_op jit(solution)/shard_map/ppermute | solution.py:62
  34.7 5.0 %collective-permute-start.9 = (bf16[128,256]{1,0:T(8,128)(2,1)S(1)}, bf16[128,256]{1,0:T(8,128)(2,1)S(1)}, u32[]{:S(2)}, u32[]{:S(2)}) collective-permute-start(bf16[128,256]{1,0:T(8,128)(2,1)S(1)} %get-tuple-element.32), channel_id=1, source_target_pairs={{0,1},{1,0},{2,3},{3,2},{4,5},{5,4},{6,7},{7,6},{8,9},{9,8},{10,11... | collective-permute-start | bytes 196616 | tf_op jit(solution)/shard_map/ppermute | solution.py:62
  35.2 7.3 %collective-permute-start.11 = (bf16[128,256]{1,0:T(8,128)(2,1)S(1)}, bf16[128,256]{1,0:T(8,128)(2,1)S(1)}, u32[]{:S(2)}, u32[]{:S(2)}) collective-permute-start(bf16[128,256]{1,0:T(8,128)(2,1)S(1)} %get-tuple-element.34), channel_id=1, source_target_pairs={{0,1},{1,0},{2,3},{3,2},{4,5},{5,4},{6,7},{7,6},{8,9},{9,8},{10,11... | collective-permute-start | bytes 196616 | tf_op jit(solution)/shard_map/ppermute | solution.py:62
  36.7 8.1 %collective-permute-start.13 = (bf16[128,256]{1,0:T(8,128)(2,1)S(1)}, bf16[128,256]{1,0:T(8,128)(2,1)S(1)}, u32[]{:S(2)}, u32[]{:S(2)}) collective-permute-start(bf16[128,256]{1,0:T(8,128)(2,1)S(1)} %get-tuple-element.36), channel_id=1, source_target_pairs={{0,1},{1,0},{2,3},{3,2},{4,5},{5,4},{6,7},{7,6},{8,9},{9,8},{10,11... | collective-permute-start | bytes 196616 | tf_op jit(solution)/shard_map/ppermute | solution.py:62
  37.7 7.1 %collective-permute-start.8 = (bf16[128,256]{1,0:T(8,128)(2,1)S(1)}, bf16[128,256]{1,0:T(8,128)(2,1)S(1)}, u32[]{:S(2)}, u32[]{:S(2)}) collective-permute-start(bf16[128,256]{1,0:T(8,128)(2,1)S(1)} %add_convert_fusion.3), channel_id=1, source_target_pairs={{0,2},{1,3},{2,4},{3,5},{4,6},{5,7},{6,0},{7,1},{8,10},{9,11},{10,... | collective-permute-start | bytes 196616 | tf_op jit(solution)/shard_map/ppermute | solution.py:70
  39.6 6.9 %collective-permute-start.10 = (bf16[128,256]{1,0:T(8,128)(2,1)S(1)}, bf16[128,256]{1,0:T(8,128)(2,1)S(1)}, u32[]{:S(2)}, u32[]{:S(2)}) collective-permute-start(bf16[128,256]{1,0:T(8,128)(2,1)S(1)} %add_convert_fusion.2), channel_id=1, source_target_pairs={{0,4},{1,5},{2,6},{3,7},{4,0},{5,1},{6,2},{7,3},{8,12},{9,13},{10,... | collective-permute-start | bytes 196616 | tf_op jit(solution)/shard_map/ppermute | solution.py:70
  42.4 4.6 %collective-permute-start.12 = (bf16[128,256]{1,0:T(8,128)(2,1)S(1)}, bf16[128,256]{1,0:T(8,128)(2,1)S(1)}, u32[]{:S(2)}, u32[]{:S(2)}) collective-permute-start(bf16[128,256]{1,0:T(8,128)(2,1)S(1)} %add_convert_fusion.1), channel_id=1, source_target_pairs={{0,6},{1,7},{2,0},{3,1},{4,2},{5,3},{6,4},{7,5},{8,14},{9,15},{10,... | collective-permute-start | bytes 196616 | tf_op jit(solution)/shard_map/ppermute | solution.py:70

commit v8 on v7

--- a/solution.py
+++ b/solution.py
@@ -1,3 +1,5 @@
+import functools
+
 import jax
 import jax.numpy as jnp
 from jax import lax
@@ -6,7 +8,7 @@
 from jax.sharding import PartitionSpec as P
 
 
-def _agg_kernel(rows_ref, cols_ref, cnt_ref, panel_ref, tiles_ref, *rest):
+def _agg_kernel(xor_order, rows_ref, cols_ref, cnt_ref, panel_ref, tiles_ref, *rest):
     out_refs, acc_ref = rest[:-1], rest[-1]
     n_rows = len(out_refs)
     outer = n_rows // 2
@@ -20,12 +22,14 @@
         pos = step * 2 + (row % 2 + me % 2) % 2
         dest = jnp.where(k < live, pos, n_rows)
         src = jnp.clip(cols_ref[k] // n_rows, 0, n_src - 1)
+        if xor_order:
+            src = src ^ lax.axis_index("blk")
         acc_ref[dest] += jnp.dot(tiles_ref[k], panel_ref[src], preferred_element_type=jnp.float32)
     for s, out_ref in enumerate(out_refs):
         out_ref[...] = acc_ref[s].astype(out_ref.dtype)
 
 
-def aggregate(panel_blocks, tile_vals, tile_row, tile_col, live_count, n_rows):
+def aggregate(panel_blocks, tile_vals, tile_row, tile_col, live_count, n_rows, xor_order):
     slots, blk, _ = tile_vals.shape
     feat = panel_blocks.shape[-1]
     smem = pl.BlockSpec(memory_space=pltpu.SMEM)
@@ -33,7 +37,7 @@
     flops = 2 * slots * blk * blk * feat
     nbytes = 2 * (panel_blocks.size + tile_vals.size + n_rows * blk * feat)
     return pl.pallas_call(
-        _agg_kernel,
+        functools.partial(_agg_kernel, xor_order),
         out_shape=[pltpu.VMEM((blk, feat), jnp.bfloat16) for _ in range(n_rows)],
         in_specs=[smem, smem, smem, vmem, vmem],
         out_specs=[vmem] * n_rows,
@@ -72,6 +76,20 @@
     return total
 
 
+def gather_blk(panel):
+    n = lax.axis_size("blk")
+    if n != 4:
+        return lax.all_gather(panel, "blk", axis=0, tiled=False), False
+
+    def swap(value, mask):
+        return lax.ppermute(value, "blk", [(i, i ^ mask) for i in range(n)])
+
+    across = swap(panel, 2)
+    beside = swap(panel, 1)
+    diagonal = swap(across, 1)
+    return jnp.stack([panel, beside, across, diagonal]), True
+
+
 def make_body():
     def body(features, weight_one, weight_two, tile_values, tile_rows, tile_cols, tile_count):
         tile_vals = tile_values[0, 0]
@@ -83,8 +101,8 @@
         for layer_id in range(2):
             weight = weight_one if layer_id == 0 else weight_two
             panel = jnp.dot(hidden, weight, preferred_element_type=jnp.float32).astype(jnp.bfloat16)
-            blocks = lax.all_gather(panel, "blk", axis=0, tiled=False)
-            partial = aggregate(blocks, tile_vals, tile_row, tile_col, live_count, replicas)
+            blocks, xor_order = gather_blk(panel)
+            partial = aggregate(blocks, tile_vals, tile_row, tile_col, live_count, replicas, xor_order)
             summed = exchange_rep(partial)
             if layer_id == 0:
                 hidden = jnp.maximum(summed, 0.0).astype(jnp.bfloat16)

time: 47.9 us -> 46.1 us (0.962)
  blocking collectives: 13 us -> 0 us
  waiting for transfers between devices: 6.04 us -> 12.5 us
  starting transfers between devices: 21.6 us -> 26.9 us
    all_gather x2 -> x0, blocking collectives: 13 us -> none  [body(): blocks = lax.all_gather(panel, 'blk', axis=0, tiled=False)]
    ppermute x0 -> x6, waiting for transfers between devices: none -> 6.87 us  [swap(): return lax.ppermute(value, 'blk', [(i, i ^ mask) for i in range(n)])]
    ppermute x0 -> x6, starting transfers between devices: none -> 4.56 us  [swap(): return lax.ppermute(value, 'blk', [(i, i ^ mask) for i in range(n)])]
    ppermute x6, starting transfers between devices: 13.4 us -> 14 us  [exchange_rep(): lax.ppermute(both.astype(jnp.bfloat16), 'rep', perm).astype(jnp.float32)]
    unnamed x8 -> x6, local copies, waits for them, and re-layouts: 1.37 us -> 0.91 us
  transfers between devices with their start and end apart: 14 -> 20, of which waited for: 8 -> 12; matrix products, arithmetic and copies ran while one was open for 0% -> 0% of each run, Pallas kernels for 0% -> 0%
where the time goes in v8:
time: 46.1 us; the launch traced here: 45.9 us
  starting transfers between devices  26.9 us (58%)
  waiting for transfers between devices  12.5 us (27%)
  Pallas kernels  2.84 us (6%)
  matrix products  1.17 us (3%)
  local copies, waits for them, and re-layouts  0.91 us (2%)
  other arithmetic  0.85 us (2%)
  between operations  0.76 us (2%)
    ppermute x6, starting transfers between devices, exchange_rep(): lax.ppermute(both.astype(jnp.bfloat16), 'rep', perm).astype(jnp.float32)  14 us
    ppermute x8, starting transfers between devices, exchange_rep(): got = {t: lax.ppermute(partial[t * 2 + 1], 'rep', pair) for t in order}  8.34 us
    ppermute x6, waiting for transfers between devices, swap(): return lax.ppermute(value, 'blk', [(i, i ^ mask) for i in range(n)])  6.87 us
    ppermute x6, starting transfers between devices, swap(): return lax.ppermute(value, 'blk', [(i, i ^ mask) for i in range(n)])  4.56 us
    ppermute x6, waiting for transfers between devices, exchange_rep(): lax.ppermute(both.astype(jnp.bfloat16), 'rep', perm).astype(jnp.float32)  4.29 us
    pallas_call x2, Pallas kernels, aggregate(): pl.pallas_call(functools.partial(_agg_kernel, xor_order), out_shape=[pltp...  2.84 us
    ppermute x8, waiting for transfers between devices, exchange_rep(): got = {t: lax.ppermute(partial[t * 2 + 1], 'rep', pair) for t in order}  1.38 us
    dot_general x2, matrix products, body(): jnp.dot(hidden, weight, preferred_element_type=jnp.float32)  1.17 us
  transfers between devices with their start and end apart: 20, of which 12 were waited for; matrix products, arithmetic and copies ran while one was open for 0% of the time, Pallas kernels for 0%

profile of v8, /device:TPU:0, one launch (start us, length us, event | category | flops | bytes accessed | tf_op | source)
XLA Modules:
  0.0 45.9 jit_solution(11036837307000051107)
XLA Ops:
  0.0 0.0 copy-start
  0.0 0.9 %copy-done = bf16[256,256]{1,0:T(8,128)(2,1)S(1)} copy-done((bf16[256,256]{1,0:T(8,128)(2,1)S(1)}, bf16[256,256]{1,0:T(8,128)(2,1)}, u32[]{:S(2)}) %copy-start) | copy-done | bytes 131096
  0.9 1.0 %convolution_convert_fusion.1 = bf16[128,256]{1,0:T(8,128)(2,1)S(1)} fusion(bf16[128,256]{1,0:T(8,128)(2,1)} %param.7, bf16[256,256]{1,0:T(8,128)(2,1)S(1)} %copy-done), kind=kOutput, calls=%fused_computation.1 | convolution fusion | flops 16809984 | bytes 262144 | tf_op jit(solution)/shard_map/dot_general | solution.py:103
  1.9 3.0 %collective-permute-start.1 = (bf16[128,256]{1,0:T(8,128)(2,1)S(1)}, bf16[128,256]{1,0:T(8,128)(2,1)S(1)}, u32[]{:S(2)}, u32[]{:S(2)}) collective-permute-start(bf16[128,256]{1,0:T(8,128)(2,1)S(1)} %convolution_convert_fusion.1), channel_id=1, source_target_pairs={{0,16},{8,24},{16,0},{24,8},{1,17},{9,25},{17,1},{25,9},{2,18},{10... | collective-permute-start | bytes 196616 | tf_op jit(solution)/shard_map/ppermute | solution.py:85
  4.9 0.0 collective-permute-start
  4.9 2.2 %collective-permute-done.1 = bf16[128,256]{1,0:T(8,128)(2,1)S(1)} collective-permute-done((bf16[128,256]{1,0:T(8,128)(2,1)S(1)}, bf16[128,256]{1,0:T(8,128)(2,1)S(1)}, u32[]{:S(2)}, u32[]{:S(2)}) %collective-permute-start.1) | collective-permute-done | bytes 65568 | tf_op jit(solution)/shard_map/ppermute | solution.py:85
  7.2 0.0 collective-permute-start.2
  7.8 0.0 collective-permute-done
  7.8 0.6 %collective-permute-done.2 = bf16[128,256]{1,0:T(8,128)(2,1)S(1)} collective-permute-done((bf16[128,256]{1,0:T(8,128)(2,1)S(1)}, bf16[128,256]{1,0:T(8,128)(2,1)S(1)}, u32[]{:S(2)}, u32[]{:S(2)}) %collective-permute-start.2) | collective-permute-done | bytes 65568 | tf_op jit(solution)/shard_map/ppermute | solution.py:85
  8.5 1.4 %shard_map.73 = (bf16[128,256]{1,0:T(8,128)(2,1)S(1)}, bf16[128,256]{1,0:T(8,128)(2,1)S(1)}, bf16[128,256]{1,0:T(8,128)(2,1)S(1)}, bf16[128,256]{1,0:T(8,128)(2,...) custom-call(s32[24]{0:T(128)} %bitcast.27, ...), custom_call_target="tpu_custom_call" | custom-call | flops 201326592 | bytes 1572864 | tf_op jit(solution)/shard_map/pallas_call | solution.py:39
  9.9 2.1 %collective-permute-start.3 = (bf16[128,256]{1,0:T(8,128)(2,1)S(1)}, bf16[128,256]{1,0:T(8,128)(2,1)S(1)}, u32[]{:S(2)}, u32[]{:S(2)}) collective-permute-start(bf16[128,256]{1,0:T(8,128)(2,1)S(1)} %get-tuple-element.22), channel_id=1, source_target_pairs={{0,1},{1,0},{2,3},{3,2},{4,5},{5,4},{6,7},{7,6},{8,9},{9,8},{10,11... | collective-permute-start | bytes 196616 | tf_op jit(solution)/shard_map/ppermute | solution.py:66
  12.0 0.1 collective-permute-start.5
  12.1 1.9 %collective-permute-start.7 = (bf16[128,256]{1,0:T(8,128)(2,1)S(1)}, bf16[128,256]{1,0:T(8,128)(2,1)S(1)}, u32[]{:S(2)}, u32[]{:S(2)}) collective-permute-start(bf16[128,256]{1,0:T(8,128)(2,1)S(1)} %get-tuple-element.26), channel_id=1, source_target_pairs={{0,1},{1,0},{2,3},{3,2},{4,5},{5,4},{6,7},{7,6},{8,9},{9,8},{10,11... | collective-permute-start | bytes 196616 | tf_op jit(solution)/shard_map/ppermute | solution.py:66
  14.0 0.1 collective-permute-start.9
  14.1 0.4 collective-permute-done.3
  14.5 2.3 %collective-permute-start.4 = (bf16[128,256]{1,0:T(8,128)(2,1)S(1)}, bf16[128,256]{1,0:T(8,128)(2,1)S(1)}, u32[]{:S(2)}, u32[]{:S(2)}) collective-permute-start(bf16[128,256]{1,0:T(8,128)(2,1)S(1)} %add_convert_fusion.6), channel_id=1, source_target_pairs={{0,2},{1,3},{2,4},{3,5},{4,6},{5,7},{6,0},{7,1},{8,10},{9,11},{10,... | collective-permute-start | bytes 196616 | tf_op jit(solution)/shard_map/ppermute | solution.py:74
  16.8 0.2 collective-permute-done.5
  17.0 0.0 copy-start.2
  17.0 2.7 %collective-permute-start.6 = (bf16[128,256]{1,0:T(8,128)(2,1)S(1)}, bf16[128,256]{1,0:T(8,128)(2,1)S(1)}, u32[]{:S(2)}, u32[]{:S(2)}) collective-permute-start(bf16[128,256]{1,0:T(8,128)(2,1)S(1)} %add_convert_fusion.5), channel_id=1, source_target_pairs={{0,4},{1,5},{2,6},{3,7},{4,0},{5,1},{6,2},{7,3},{8,12},{9,13},{10,... | collective-permute-start | bytes 196616 | tf_op jit(solution)/shard_map/ppermute | solution.py:74
  19.7 0.0 collective-permute-done.7
  19.7 2.2 %collective-permute-start.8 = (bf16[128,256]{1,0:T(8,128)(2,1)S(1)}, bf16[128,256]{1,0:T(8,128)(2,1)S(1)}, u32[]{:S(2)}, u32[]{:S(2)}) collective-permute-start(bf16[128,256]{1,0:T(8,128)(2,1)S(1)} %add_convert_fusion.4), channel_id=1, source_target_pairs={{0,6},{1,7},{2,0},{3,1},{4,2},{5,3},{6,4},{7,5},{8,14},{9,15},{10,... | collective-permute-start | bytes 196616 | tf_op jit(solution)/shard_map/ppermute | solution.py:74
  21.9 0.0 collective-permute-done.9
  21.9 0.0 collective-permute-done.4
  21.9 1.6 %collective-permute-done.6 = bf16[128,256]{1,0:T(8,128)(2,1)S(1)} collective-permute-done((bf16[128,256]{1,0:T(8,128)(2,1)S(1)}, bf16[128,256]{1,0:T(8,128)(2,1)S(1)}, u32[]{:S(2)}, u32[]{:S(2)}) %collective-permute-start.6) | collective-permute-done | bytes 65568 | tf_op jit(solution)/shard_map/ppermute | solution.py:74
  23.6 0.6 %collective-permute-done.8 = bf16[128,256]{1,0:T(8,128)(2,1)S(1)} collective-permute-done((bf16[128,256]{1,0:T(8,128)(2,1)S(1)}, bf16[128,256]{1,0:T(8,128)(2,1)S(1)}, u32[]{:S(2)}, u32[]{:S(2)}) %collective-permute-start.8) | collective-permute-done | bytes 65568 | tf_op jit(solution)/shard_map/ppermute | solution.py:74
  24.1 0.2 convolution_convert_fusion
  24.3 1.5 %collective-permute-start.11 = (bf16[128,256]{1,0:T(8,128)(2,1)S(1)}, bf16[128,256]{1,0:T(8,128)(2,1)S(1)}, u32[]{:S(2)}, u32[]{:S(2)}) collective-permute-start(bf16[128,256]{1,0:T(8,128)(2,1)S(1)} %convolution_convert_fusion), channel_id=1, source_target_pairs={{0,16},{8,24},{16,0},{24,8},{1,17},{9,25},{17,1},{25,9},{2,18},{10... | collective-permute-start | bytes 196616 | tf_op jit(solution)/shard_map/ppermute | solution.py:85
  25.9 0.0 collective-permute-start.10
  25.9 2.8 %collective-permute-done.11 = bf16[128,256]{1,0:T(8,128)(2,1)S(1)} collective-permute-done((bf16[128,256]{1,0:T(8,128)(2,1)S(1)}, bf16[128,256]{1,0:T(8,128)(2,1)S(1)}, u32[]{:S(2)}, u32[]{:S(2)}) %collective-permute-start.11) | collective-permute-done | bytes 65568 | tf_op jit(solution)/shard_map/ppermute | solution.py:85
  28.7 0.0 collective-permute-start.12
  28.7 0.0 collective-permute-done.10
  28.7 1.2 %collective-permute-done.12 = bf16[128,256]{1,0:T(8,128)(2,1)S(1)} collective-permute-done((bf16[128,256]{1,0:T(8,128)(2,1)S(1)}, bf16[128,256]{1,0:T(8,128)(2,1)S(1)}, u32[]{:S(2)}, u32[]{:S(2)}) %collective-permute-start.12) | collective-permute-done | bytes 65568 | tf_op jit(solution)/shard_map/ppermute | solution.py:85
  30.0 1.4 %shard_map.74 = (bf16[128,256]{1,0:T(8,128)(2,1)S(1)}, bf16[128,256]{1,0:T(8,128)(2,1)S(1)}, bf16[128,256]{1,0:T(8,128)(2,1)S(1)}, bf16[128,256]{1,0:T(8,128)(2,...) custom-call(s32[24]{0:T(128)} %bitcast.28, ...), custom_call_target="tpu_custom_call" | custom-call | flops 201326592 | bytes 1572864 | tf_op jit(solution)/shard_map/pallas_call | solution.py:39
  31.4 1.7 %collective-permute-start.13 = (bf16[128,256]{1,0:T(8,128)(2,1)S(1)}, bf16[128,256]{1,0:T(8,128)(2,1)S(1)}, u32[]{:S(2)}, u32[]{:S(2)}) collective-permute-start(bf16[128,256]{1,0:T(8,128)(2,1)S(1)} %get-tuple-element.30), channel_id=1, source_target_pairs={{0,1},{1,0},{2,3},{3,2},{4,5},{5,4},{6,7},{7,6},{8,9},{9,8},{10,11... | collective-permute-start | bytes 196616 | tf_op jit(solution)/shard_map/ppermute | solution.py:66
  33.1 0.3 collective-permute-start.15
  33.5 1.7 %collective-permute-start.17 = (bf16[128,256]{1,0:T(8,128)(2,1)S(1)}, bf16[128,256]{1,0:T(8,128)(2,1)S(1)}, u32[]{:S(2)}, u32[]{:S(2)}) collective-permute-start(bf16[128,256]{1,0:T(8,128)(2,1)S(1)} %get-tuple-element.34), channel_id=1, source_target_pairs={{0,1},{1,0},{2,3},{3,2},{4,5},{5,4},{6,7},{7,6},{8,9},{9,8},{10,11... | collective-permute-start | bytes 196616 | tf_op jit(solution)/shard_map/ppermute | solution.py:66
  35.2 0.3 collective-permute-start.19
  35.5 0.4 collective-permute-done.13
  35.9 1.8 %collective-permute-start.14 = (bf16[128,256]{1,0:T(8,128)(2,1)S(1)}, bf16[128,256]{1,0:T(8,128)(2,1)S(1)}, u32[]{:S(2)}, u32[]{:S(2)}) collective-permute-start(bf16[128,256]{1,0:T(8,128)(2,1)S(1)} %add_convert_fusion.3), channel_id=1, source_target_pairs={{0,2},{1,3},{2,4},{3,5},{4,6},{5,7},{6,0},{7,1},{8,10},{9,11},{10,... | collective-permute-start | bytes 196616 | tf_op jit(solution)/shard_map/ppermute | solution.py:74
  37.7 0.4 collective-permute-done.15
  38.1 2.6 %collective-permute-start.16 = (bf16[128,256]{1,0:T(8,128)(2,1)S(1)}, bf16[128,256]{1,0:T(8,128)(2,1)S(1)}, u32[]{:S(2)}, u32[]{:S(2)}) collective-permute-start(bf16[128,256]{1,0:T(8,128)(2,1)S(1)} %add_convert_fusion.2), channel_id=1, source_target_pairs={{0,4},{1,5},{2,6},{3,7},{4,0},{5,1},{6,2},{7,3},{8,12},{9,13},{10,... | collective-permute-start | bytes 196616 | tf_op jit(solution)/shard_map/ppermute | solution.py:74
  40.7 0.0 collective-permute-done.17
  40.7 2.4 %collective-permute-start.18 = (bf16[128,256]{1,0:T(8,128)(2,1)S(1)}, bf16[128,256]{1,0:T(8,128)(2,1)S(1)}, u32[]{:S(2)}, u32[]{:S(2)}) collective-permute-start(bf16[128,256]{1,0:T(8,128)(2,1)S(1)} %add_convert_fusion.1), channel_id=1, source_target_pairs={{0,6},{1,7},{2,0},{3,1},{4,2},{5,3},{6,4},{7,5},{8,14},{9,15},{10,... | collective-permute-start | bytes 196616 | tf_op jit(solution)/shard_map/ppermute | solution.py:74
  43.2 0.0 collective-permute-done.19
  43.2 0.0 collective-permute-done.14
  43.2 1.6 %collective-permute-done.16 = bf16[128,256]{1,0:T(8,128)(2,1)S(1)} collective-permute-done((bf16[128,256]{1,0:T(8,128)(2,1)S(1)}, bf16[128,256]{1,0:T(8,128)(2,1)S(1)}, u32[]{:S(2)}, u32[]{:S(2)}) %collective-permute-start.16) | collective-permute-done | bytes 65568 | tf_op jit(solution)/shard_map/ppermute | solution.py:74
  44.8 0.5 %collective-permute-done.18 = bf16[128,256]{1,0:T(8,128)(2,1)S(1)} collective-permute-done((bf16[128,256]{1,0:T(8,128)(2,1)S(1)}, bf16[128,256]{1,0:T(8,128)(2,1)S(1)}, u32[]{:S(2)}, u32[]{:S(2)}) %collective-permute-start.18) | collective-permute-done | bytes 65568 | tf_op jit(solution)/shard_map/ppermute | solution.py:74
  45.3 0.7 %add_convert_fusion = bf16[128,256]{1,0:T(8,128)(2,1)} fusion(bf16[128,256]{1,0:T(8,128)(2,1)S(1)} %collective-permute-done.19, bf16[128,256]{1,0:T(8,128)(2,1)S(1)} %get-tuple-element.35, bf16[128,256]{1,0:T(8,128)(2,1)S(1)} %collective-permute-done.18, bf16[128,256]{1,0:T(8,128)(2,1)S(1)} %collective-permute-done.16, ...), kind=kLoop, calls=%fused_computation.4 | loop fusion | flops 327680 | bytes 393216 | tf_op jit(solution)/shard_map/convert_element_type | solution.py:110
  (11 shorter events, 0.2 us)
Async XLA Ops:
  0.0 0.9 %copy-start = (bf16[256,256]{1,0:T(8,128)(2,1)S(1)}, bf16[256,256]{1,0:T(8,128)(2,1)}, u32[]{:S(2)}) copy-start(bf16[256,256]{1,0:T(8,128)(2,1)} %param.8) | copy-start | bytes 393220
  0.0 8.5 %copy-start.1 = (bf16[1,1,24,128,128]{4,3,2,1,0:T(8,128)(2,1)S(1)}, bf16[1,1,24,128,128]{4,3,2,1,0:T(8,128)(2,1)}, u32[]{:S(2)}) copy-start(bf16[1,1,24,128,128]{4,3,2,1,0:T(8,128)(2,1)} %param.10) | copy-start | bytes 2359300
  1.9 5.2 %collective-permute-start.1 = (bf16[128,256]{1,0:T(8,128)(2,1)S(1)}, bf16[128,256]{1,0:T(8,128)(2,1)S(1)}, u32[]{:S(2)}, u32[]{:S(2)}) collective-permute-start(bf16[128,256]{1,0:T(8,128)(2,1)S(1)} %convolution_convert_fusion.1), channel_id=1, source_target_pairs={{0,16},{8,24},{16,0},{24,8},{1,17},{9,25},{17,1},{25,9},{2,18},{10... | collective-permute-start | bytes 196616 | tf_op jit(solution)/shard_map/ppermute | solution.py:85
  4.9 2.9 %collective-permute-start = (bf16[128,256]{1,0:T(8,128)(2,1)S(1)}, bf16[128,256]{1,0:T(8,128)(2,1)S(1)}, u32[]{:S(2)}, u32[]{:S(2)}) collective-permute-start(bf16[128,256]{1,0:T(8,128)(2,1)S(1)} %convolution_convert_fusion.1), channel_id=1, source_target_pairs={{0,8},{8,0},{16,24},{24,16},{1,9},{9,1},{17,25},{25,17},{2,10},{10... | collective-permute-start | bytes 196616 | tf_op jit(solution)/shard_map/ppermute | solution.py:85
  7.2 1.3 %collective-permute-start.2 = (bf16[128,256]{1,0:T(8,128)(2,1)S(1)}, bf16[128,256]{1,0:T(8,128)(2,1)S(1)}, u32[]{:S(2)}, u32[]{:S(2)}) collective-permute-start(bf16[128,256]{1,0:T(8,128)(2,1)S(1)} %collective-permute-done.1), channel_id=1, source_target_pairs={{0,8},{8,0},{16,24},{24,16},{1,9},{9,1},{17,25},{25,17},{2,10},{10... | collective-permute-start | bytes 196616 | tf_op jit(solution)/shard_map/ppermute | solution.py:85
  9.9 4.6 %collective-permute-start.3 = (bf16[128,256]{1,0:T(8,128)(2,1)S(1)}, bf16[128,256]{1,0:T(8,128)(2,1)S(1)}, u32[]{:S(2)}, u32[]{:S(2)}) collective-permute-start(bf16[128,256]{1,0:T(8,128)(2,1)S(1)} %get-tuple-element.22), channel_id=1, source_target_pairs={{0,1},{1,0},{2,3},{3,2},{4,5},{5,4},{6,7},{7,6},{8,9},{9,8},{10,11... | collective-permute-start | bytes 196616 | tf_op jit(solution)/shard_map/ppermute | solution.py:66
  12.0 5.0 %collective-permute-start.5 = (bf16[128,256]{1,0:T(8,128)(2,1)S(1)}, bf16[128,256]{1,0:T(8,128)(2,1)S(1)}, u32[]{:S(2)}, u32[]{:S(2)}) collective-permute-start(bf16[128,256]{1,0:T(8,128)(2,1)S(1)} %get-tuple-element.24), channel_id=1, source_target_pairs={{0,1},{1,0},{2,3},{3,2},{4,5},{5,4},{6,7},{7,6},{8,9},{9,8},{10,11... | collective-permute-start | bytes 196616 | tf_op jit(solution)/shard_map/ppermute | solution.py:66
  12.1 7.6 %collective-permute-start.7 = (bf16[128,256]{1,0:T(8,128)(2,1)S(1)}, bf16[128,256]{1,0:T(8,128)(2,1)S(1)}, u32[]{:S(2)}, u32[]{:S(2)}) collective-permute-start(bf16[128,256]{1,0:T(8,128)(2,1)S(1)} %get-tuple-element.26), channel_id=1, source_target_pairs={{0,1},{1,0},{2,3},{3,2},{4,5},{5,4},{6,7},{7,6},{8,9},{9,8},{10,11... | collective-permute-start | bytes 196616 | tf_op jit(solution)/shard_map/ppermute | solution.py:66
  14.0 7.9 %collective-permute-start.9 = (bf16[128,256]{1,0:T(8,128)(2,1)S(1)}, bf16[128,256]{1,0:T(8,128)(2,1)S(1)}, u32[]{:S(2)}, u32[]{:S(2)}) collective-permute-start(bf16[128,256]{1,0:T(8,128)(2,1)S(1)} %get-tuple-element.28), channel_id=1, source_target_pairs={{0,1},{1,0},{2,3},{3,2},{4,5},{5,4},{6,7},{7,6},{8,9},{9,8},{10,11... | collective-permute-start | bytes 196616 | tf_op jit(solution)/shard_map/ppermute | solution.py:66
  14.5 7.5 %collective-permute-start.4 = (bf16[128,256]{1,0:T(8,128)(2,1)S(1)}, bf16[128,256]{1,0:T(8,128)(2,1)S(1)}, u32[]{:S(2)}, u32[]{:S(2)}) collective-permute-start(bf16[128,256]{1,0:T(8,128)(2,1)S(1)} %add_convert_fusion.6), channel_id=1, source_target_pairs={{0,2},{1,3},{2,4},{3,5},{4,6},{5,7},{6,0},{7,1},{8,10},{9,11},{10,... | collective-permute-start | bytes 196616 | tf_op jit(solution)/shard_map/ppermute | solution.py:74
  17.0 7.1 %copy-start.2 = (bf16[256,256]{1,0:T(8,128)(2,1)S(1)}, bf16[256,256]{1,0:T(8,128)(2,1)}, u32[]{:S(2)}) copy-start(bf16[256,256]{1,0:T(8,128)(2,1)} %param.9) | copy-start | bytes 393220
  17.0 6.6 %collective-permute-start.6 = (bf16[128,256]{1,0:T(8,128)(2,1)S(1)}, bf16[128,256]{1,0:T(8,128)(2,1)S(1)}, u32[]{:S(2)}, u32[]{:S(2)}) collective-permute-start(bf16[128,256]{1,0:T(8,128)(2,1)S(1)} %add_convert_fusion.5), channel_id=1, source_target_pairs={{0,4},{1,5},{2,6},{3,7},{4,0},{5,1},{6,2},{7,3},{8,12},{9,13},{10,... | collective-permute-start | bytes 196616 | tf_op jit(solution)/shard_map/ppermute | solution.py:74
  19.7 4.4 %collective-permute-start.8 = (bf16[128,256]{1,0:T(8,128)(2,1)S(1)}, bf16[128,256]{1,0:T(8,128)(2,1)S(1)}, u32[]{:S(2)}, u32[]{:S(2)}) collective-permute-start(bf16[128,256]{1,0:T(8,128)(2,1)S(1)} %add_convert_fusion.4), channel_id=1, source_target_pairs={{0,6},{1,7},{2,0},{3,1},{4,2},{5,3},{6,4},{7,5},{8,14},{9,15},{10,... | collective-permute-start | bytes 196616 | tf_op jit(solution)/shard_map/ppermute | solution.py:74
  24.3 4.3 %collective-permute-start.11 = (bf16[128,256]{1,0:T(8,128)(2,1)S(1)}, bf16[128,256]{1,0:T(8,128)(2,1)S(1)}, u32[]{:S(2)}, u32[]{:S(2)}) collective-permute-start(bf16[128,256]{1,0:T(8,128)(2,1)S(1)} %convolution_convert_fusion), channel_id=1, source_target_pairs={{0,16},{8,24},{16,0},{24,8},{1,17},{9,25},{17,1},{25,9},{2,18},{10... | collective-permute-start | bytes 196616 | tf_op jit(solution)/shard_map/ppermute | solution.py:85
  25.9 2.8 %collective-permute-start.10 = (bf16[128,256]{1,0:T(8,128)(2,1)S(1)}, bf16[128,256]{1,0:T(8,128)(2,1)S(1)}, u32[]{:S(2)}, u32[]{:S(2)}) collective-permute-start(bf16[128,256]{1,0:T(8,128)(2,1)S(1)} %convolution_convert_fusion), channel_id=1, source_target_pairs={{0,8},{8,0},{16,24},{24,16},{1,9},{9,1},{17,25},{25,17},{2,10},{10... | collective-permute-start | bytes 196616 | tf_op jit(solution)/shard_map/ppermute | solution.py:85
  28.7 1.3 %collective-permute-start.12 = (bf16[128,256]{1,0:T(8,128)(2,1)S(1)}, bf16[128,256]{1,0:T(8,128)(2,1)S(1)}, u32[]{:S(2)}, u32[]{:S(2)}) collective-permute-start(bf16[128,256]{1,0:T(8,128)(2,1)S(1)} %collective-permute-done.11), channel_id=1, source_target_pairs={{0,8},{8,0},{16,24},{24,16},{1,9},{9,1},{17,25},{25,17},{2,10},{10... | collective-permute-start | bytes 196616 | tf_op jit(solution)/shard_map/ppermute | solution.py:85
  31.4 4.5 %collective-permute-start.13 = (bf16[128,256]{1,0:T(8,128)(2,1)S(1)}, bf16[128,256]{1,0:T(8,128)(2,1)S(1)}, u32[]{:S(2)}, u32[]{:S(2)}) collective-permute-start(bf16[128,256]{1,0:T(8,128)(2,1)S(1)} %get-tuple-element.30), channel_id=1, source_target_pairs={{0,1},{1,0},{2,3},{3,2},{4,5},{5,4},{6,7},{7,6},{8,9},{9,8},{10,11... | collective-permute-start | bytes 196616 | tf_op jit(solution)/shard_map/ppermute | solution.py:66
  33.1 5.0 %collective-permute-start.15 = (bf16[128,256]{1,0:T(8,128)(2,1)S(1)}, bf16[128,256]{1,0:T(8,128)(2,1)S(1)}, u32[]{:S(2)}, u32[]{:S(2)}) collective-permute-start(bf16[128,256]{1,0:T(8,128)(2,1)S(1)} %get-tuple-element.32), channel_id=1, source_target_pairs={{0,1},{1,0},{2,3},{3,2},{4,5},{5,4},{6,7},{7,6},{8,9},{9,8},{10,11... | collective-permute-start | bytes 196616 | tf_op jit(solution)/shard_map/ppermute | solution.py:66
  33.5 7.2 %collective-permute-start.17 = (bf16[128,256]{1,0:T(8,128)(2,1)S(1)}, bf16[128,256]{1,0:T(8,128)(2,1)S(1)}, u32[]{:S(2)}, u32[]{:S(2)}) collective-permute-start(bf16[128,256]{1,0:T(8,128)(2,1)S(1)} %get-tuple-element.34), channel_id=1, source_target_pairs={{0,1},{1,0},{2,3},{3,2},{4,5},{5,4},{6,7},{7,6},{8,9},{9,8},{10,11... | collective-permute-start | bytes 196616 | tf_op jit(solution)/shard_map/ppermute | solution.py:66
  35.2 8.0 %collective-permute-start.19 = (bf16[128,256]{1,0:T(8,128)(2,1)S(1)}, bf16[128,256]{1,0:T(8,128)(2,1)S(1)}, u32[]{:S(2)}, u32[]{:S(2)}) collective-permute-start(bf16[128,256]{1,0:T(8,128)(2,1)S(1)} %get-tuple-element.36), channel_id=1, source_target_pairs={{0,1},{1,0},{2,3},{3,2},{4,5},{5,4},{6,7},{7,6},{8,9},{9,8},{10,11... | collective-permute-start | bytes 196616 | tf_op jit(solution)/shard_map/ppermute | solution.py:66
  35.9 7.3 %collective-permute-start.14 = (bf16[128,256]{1,0:T(8,128)(2,1)S(1)}, bf16[128,256]{1,0:T(8,128)(2,1)S(1)}, u32[]{:S(2)}, u32[]{:S(2)}) collective-permute-start(bf16[128,256]{1,0:T(8,128)(2,1)S(1)} %add_convert_fusion.3), channel_id=1, source_target_pairs={{0,2},{1,3},{2,4},{3,5},{4,6},{5,7},{6,0},{7,1},{8,10},{9,11},{10,... | collective-permute-start | bytes 196616 | tf_op jit(solution)/shard_map/ppermute | solution.py:74
  38.1 6.7 %collective-permute-start.16 = (bf16[128,256]{1,0:T(8,128)(2,1)S(1)}, bf16[128,256]{1,0:T(8,128)(2,1)S(1)}, u32[]{:S(2)}, u32[]{:S(2)}) collective-permute-start(bf16[128,256]{1,0:T(8,128)(2,1)S(1)} %add_convert_fusion.2), channel_id=1, source_target_pairs={{0,4},{1,5},{2,6},{3,7},{4,0},{5,1},{6,2},{7,3},{8,12},{9,13},{10,... | collective-permute-start | bytes 196616 | tf_op jit(solution)/shard_map/ppermute | solution.py:74
  40.7 4.5 %collective-permute-start.18 = (bf16[128,256]{1,0:T(8,128)(2,1)S(1)}, bf16[128,256]{1,0:T(8,128)(2,1)S(1)}, u32[]{:S(2)}, u32[]{:S(2)}) collective-permute-start(bf16[128,256]{1,0:T(8,128)(2,1)S(1)} %add_convert_fusion.1), channel_id=1, source_target_pairs={{0,6},{1,7},{2,0},{3,1},{4,2},{5,3},{6,4},{7,5},{8,14},{9,15},{10,... | collective-permute-start | bytes 196616 | tf_op jit(solution)/shard_map/ppermute | solution.py:74
